TPU v7x, 512 devices: a whole 4x4x16 slice. The times are simulated.
512 devices in a mesh: ch: 128 (over z, x, y_lo), af: 4 (over y_hi, core).
Axes of the slice: x: 4, y: 4 (y_hi: 2, y_lo: 2; y = y_hi * 2 + y_lo), z: 16, core: 2. Of those that a mesh axis runs over, the one named last changes fastest.
Arguments:
- records: bfloat16 [128, 8192, 1024], P('ch', 'af'), may hold values from -80 to 80
- quality: int32 [1024], replicated, may hold values 0 or 1
- band_low: int32 [1024], P('ch'), may hold values from 0 to 31
- band_high: int32 [1024], P('ch'), may hold values from 96 to 128
Outputs:
- cross_spectra: float32 [1024, 129, 2, 512], P('ch', None, None, 'af')
All inputs are finite; a program needn't handle non-finite values.
Results may differ from a plain program's by a relative error of at most 0.0054.
Values may be sent and summed in bfloat16 or wider, within the bound.
No kernel may reach another device: no remote copies, remote signals or barrier semaphores. Data moves between devices by JAX's collectives and lax.ppermute only.
A program may use at most 64 MiB of HBM per device.

v0:
```python
import math

import jax
import jax.numpy as jnp
from jax import lax
from jax.sharding import PartitionSpec as P

SEGLEN = 8192
BINS = 512
LOWBIN = 64
SMOOTH = 32
REACH = 128


def extended(cells, sides, width):
    for axis, dim in sides:
        count = lax.axis_size(axis)
        ends = count - 1
        head = lax.slice_in_dim(cells, 0, width, axis=dim)
        tail = lax.slice_in_dim(cells, cells.shape[dim] - width, cells.shape[dim], axis=dim)
        cells = jnp.concatenate(
            [
                lax.ppermute(tail, axis, [(i, (i + 1) % count) for i in range(ends)]),
                cells,
                lax.ppermute(head, axis, [((i + 1) % count, i) for i in range(ends)]),
            ],
            axis=dim,
        )
    return cells


def passed_along(value, axis, steps):
    count = lax.axis_size(axis)
    initial, last = (max(0, -steps), min(count, count - steps))
    return lax.ppermute(value, axis, [(source, source + steps) for source in range(initial, last)])


def taper_table(bin_index, sample_index, length):
    phase_index = bin_index[:, None] * sample_index[None, :] % length
    angles = phase_index.astype(jnp.float32) * (2.0 * math.pi / length)
    tapers = 0.5 - 0.5 * jnp.cos(sample_index.astype(jnp.float32) * (2.0 * math.pi / length))
    real_row = (tapers[None, :] * jnp.cos(angles)).astype(jnp.bfloat16)
    imag_row = (-(tapers[None, :] * jnp.sin(angles))).astype(jnp.bfloat16)
    return jnp.stack([real_row, imag_row], axis=1)


def band_sum(padded, half_width):
    row_count = padded.shape[0] - 2 * half_width
    row_ids = jnp.arange(row_count, dtype=jnp.int32)[:, None]
    col_ids = jnp.arange(padded.shape[0], dtype=jnp.int32)[None, :]
    band_matrix = ((col_ids >= row_ids) & (col_ids <= row_ids + 2 * half_width)).astype(jnp.float32)
    return jnp.dot(
        band_matrix, padded, precision=lax.Precision.HIGHEST, preferred_element_type=jnp.float32
    )


def per_device(records, quality, band_low, band_high):
    local_record = records[0]
    quarter = local_record.shape[0]
    channels = local_record.shape[1]
    band_rows = BINS // lax.axis_size("af")
    sample_index = lax.axis_index("af") * quarter + jnp.arange(quarter, dtype=jnp.int32)
    bin_index = LOWBIN + jnp.int32(0) + jnp.arange(lax.axis_size("af") * band_rows, dtype=jnp.int32)
    basis_table = taper_table(bin_index, sample_index, SEGLEN).reshape(
        2 * (lax.axis_size("af") * band_rows), quarter
    )
    spectra = lax.psum_scatter(
        jnp.dot(basis_table, local_record, preferred_element_type=jnp.float32).reshape(
            lax.axis_size("af") * band_rows, 2, channels
        ),
        "af",
        scatter_dimension=0,
        tiled=True,
    )
    power_bins = spectra[:, 0] * spectra[:, 0] + spectra[:, 1] * spectra[:, 1]
    padded = extended(power_bins, (("af", 0),), SMOOTH)
    smoothed = band_sum(padded, SMOOTH)
    factor = quality.astype(jnp.float32)[None, :] / jnp.sqrt(
        smoothed * (1.0 / (2 * SMOOTH + 1)) + 1e-06
    )
    whitened = (spectra * factor[:, None, :]).astype(jnp.bfloat16)
    slab_count = lax.axis_size("ch")
    slab_width = channels // slab_count
    above_count = REACH // slab_width
    centre = lax.all_to_all(
        whitened.reshape(band_rows, 2, slab_count, slab_width),
        "ch",
        split_axis=2,
        concat_axis=2,
        tiled=True,
    )
    pieces = [centre]
    for block_index in range(1, above_count + 1):
        pieces.append(passed_along(centre, "ch", -block_index))
    joined = jnp.concatenate(pieces, axis=3)
    segments = centre.shape[2]
    real_a = centre[:, 0]
    imag_a = centre[:, 1]
    left_side = jnp.stack(
        [jnp.concatenate([real_a, imag_a], axis=1), jnp.concatenate([imag_a, -real_a], axis=1)],
        axis=1,
    )
    right_side = jnp.concatenate([joined[:, 0], joined[:, 1]], axis=1)
    cross_all = jnp.einsum(
        "fpsc,fse->fpce", left_side, right_side, preferred_element_type=jnp.float32
    )
    offsets = jnp.arange(REACH + 1, dtype=jnp.int32)
    row_ids = jnp.arange(slab_width, dtype=jnp.int32)[:, None]
    target = row_ids + offsets[None, :]
    picked = cross_all[:, :, row_ids, target]
    inside_band = (
        (offsets[None, :] >= band_low[:, None]) & (offsets[None, :] <= band_high[:, None])
    ).astype(jnp.float32)
    result = (
        jnp.transpose(picked, (2, 3, 1, 0))
        * inside_band[:, :, None, None]
        * (1.0 / math.sqrt(segments))
    )
    return result


def solution(mesh):
    return jax.shard_map(
        per_device,
        mesh=mesh,
        in_specs=(P("ch", "af", None), P(), P("ch"), P("ch")),
        out_specs=P("ch", None, None, "af"),
        check_vma=False,
    )
```

profile of v0, /device:TPU:33, one launch (start us, length us, event | category | flops | bytes accessed | tf_op | source)
XLA Modules:
  0.0 525.0 jit_solution(7221408600105725252)
XLA Ops:
  6.6 17.5 %multiply_convert_fusion = (bf16[512,1,2048]{2,0,1:T(8,128)(2,1)S(1)}, bf16[512,1,2048]{2,0,1:T(8,128)(2,1)S(1)}) fusion(s32[2048]{0:T(1024)S(1)} %iota_add_fusion, s32[512]{0:T(512)S(1)} %iota_add_fusion.1, f32[2048]{0:T(1024)S(1)} %multiply_subtract_fusion), kind=kLoop, calls=%fused_computation.21 | loop fusion | flops 19922944 | bytes 4212736 | tf_op jit(solution)/shard_map/convert_element_type | solution.py:42
  24.2 8.2 %fusion.6 = f32[512,2,1024]{2,0,1:T(8,128)} fusion(bf16[512,1,2048]{2,0,1:T(8,128)(2,1)S(1)} %get-tuple-element.14, bf16[512,1,2048]{2,0,1:T(8,128)(2,1)S(1)} %get-tuple-element.13, bf16[1,2048,1024]{2,1,0:T(8,128)(2,1)} %param.4), kind=kOutput, calls=%fused_computation.15 | convolution fusion | flops 4297064448 | bytes 12582912 | tf_op jit(solution)/shard_map/dot_general | solution.py:68
  32.4 71.0 %reduce-scatter.2.cloned.1.call-done = f32[128,2,1024]{2,0,1:T(8,128)} async-done(((f32[512,2,1024]{2,0,1:T(8,128)}), f32[128,2,1024]{2,0,1:T(8,128)}) %reduce-scatter.2.cloned.1.call-update) | async-done | bytes 1048592 | tf_op jit(solution)/shard_map/reduce_scatter | solution.py:67
  103.4 1.4 fusion.22
  104.9 2.9 collective-permute-start
  107.7 1.9 collective-permute-start.1
  109.7 1.3 fusion.35
  110.9 4.6 collective-permute-done.1
  115.5 0.5 fusion.13
  116.2 0.3 copy.34
  116.4 0.9 copy.35
  117.3 16.8 %all-to-all-start = ((bf16[128,2,128,8]{0,3,1,2:T(8,128)(2,1)}), bf16[128,2,128,8]{0,3,1,2:T(8,128)(2,1)S(1)}, u32[]{:S(2)}, u32[]{:S(2)}) async-start(bf16[128,2,128,8]{0,3,1,2:T(8,128)(2,1)} %copy.35), calls=%async_computation.1 | async-start | bytes 1048576 | tf_op jit(solution)/shard_map/all_to_all | solution.py:85
  134.3 30.7 %all-to-all-done = bf16[128,2,128,8]{0,3,1,2:T(8,128)(2,1)S(1)} async-done(((bf16[128,2,128,8]{0,3,1,2:T(8,128)(2,1)}), bf16[128,2,128,8]{0,3,1,2:T(8,128)(2,1)S(1)}, u32[]{:S(2)}, u32[]{:S(2)}) %all-to-all-start) | async-done | bytes 524320 | tf_op jit(solution)/shard_map/all_to_all | solution.py:85
  165.0 0.6 copy.36
  165.6 3.4 collective-permute-start.2
  169.0 2.5 collective-permute-start.3
  171.5 2.5 collective-permute-start.4
  174.0 1.9 collective-permute-start.5
  175.9 1.9 collective-permute-start.6
  178.0 0.9 constant_dynamic-update-slice_fusion.16
  178.9 13.4 %collective-permute-done.2 = bf16[128,2,128,8]{2,3,0,1:T(8,128)(2,1)S(1)} collective-permute-done((bf16[128,2,128,8]{2,3,0,1:T(8,128)(2,1)S(1)}, bf16[128,2,128,8]{2,3,0,1:T(8,128)(2,1)S(1)}, u32[]{:S(2)}, u32[]{:S(2)}) %collective-permute-start.2) | collective-permute-done | bytes 524320 | tf_op jit(solution)/shard_map/ppermute | solution.py:35
  192.3 1.9 collective-permute-start.7
  194.2 0.9 constant_dynamic-update-slice_fusion.15
  195.1 14.3 %collective-permute-done.3 = bf16[128,2,128,8]{2,3,0,1:T(8,128)(2,1)S(1)} collective-permute-done((bf16[128,2,128,8]{2,3,0,1:T(8,128)(2,1)S(1)}, bf16[128,2,128,8]{2,3,0,1:T(8,128)(2,1)S(1)}, u32[]{:S(2)}, u32[]{:S(2)}) %collective-permute-start.3) | collective-permute-done | bytes 524320 | tf_op jit(solution)/shard_map/ppermute | solution.py:35
  209.4 1.9 collective-permute-start.8
  211.4 0.9 constant_dynamic-update-slice_fusion.14
  212.2 13.8 %collective-permute-done.4 = bf16[128,2,128,8]{2,3,0,1:T(8,128)(2,1)S(1)} collective-permute-done((bf16[128,2,128,8]{2,3,0,1:T(8,128)(2,1)S(1)}, bf16[128,2,128,8]{2,3,0,1:T(8,128)(2,1)S(1)}, u32[]{:S(2)}, u32[]{:S(2)}) %collective-permute-start.4) | collective-permute-done | bytes 524320 | tf_op jit(solution)/shard_map/ppermute | solution.py:35
  226.1 1.9 collective-permute-start.9
  228.0 0.9 constant_dynamic-update-slice_fusion.13
  228.9 11.1 %collective-permute-done.5 = bf16[128,2,128,8]{2,3,0,1:T(8,128)(2,1)S(1)} collective-permute-done((bf16[128,2,128,8]{2,3,0,1:T(8,128)(2,1)S(1)}, bf16[128,2,128,8]{2,3,0,1:T(8,128)(2,1)S(1)}, u32[]{:S(2)}, u32[]{:S(2)}) %collective-permute-start.5) | collective-permute-done | bytes 524320 | tf_op jit(solution)/shard_map/ppermute | solution.py:35
  240.0 1.3 collective-permute-start.10
  241.3 0.9 constant_dynamic-update-slice_fusion.12
  242.2 9.1 %collective-permute-done.6 = bf16[128,2,128,8]{2,3,0,1:T(8,128)(2,1)S(1)} collective-permute-done((bf16[128,2,128,8]{2,3,0,1:T(8,128)(2,1)S(1)}, bf16[128,2,128,8]{2,3,0,1:T(8,128)(2,1)S(1)}, u32[]{:S(2)}, u32[]{:S(2)}) %collective-permute-start.6) | collective-permute-done | bytes 524320 | tf_op jit(solution)/shard_map/ppermute | solution.py:35
  251.3 1.3 collective-permute-start.11
  252.5 0.9 constant_dynamic-update-slice_fusion.11
  253.4 9.1 %collective-permute-done.7 = bf16[128,2,128,8]{2,3,0,1:T(8,128)(2,1)S(1)} collective-permute-done((bf16[128,2,128,8]{2,3,0,1:T(8,128)(2,1)S(1)}, bf16[128,2,128,8]{2,3,0,1:T(8,128)(2,1)S(1)}, u32[]{:S(2)}, u32[]{:S(2)}) %collective-permute-start.7) | collective-permute-done | bytes 524320 | tf_op jit(solution)/shard_map/ppermute | solution.py:35
  262.5 1.3 collective-permute-start.12
  263.8 0.9 constant_dynamic-update-slice_fusion.10
  264.7 9.1 %collective-permute-done.8 = bf16[128,2,128,8]{2,3,0,1:T(8,128)(2,1)S(1)} collective-permute-done((bf16[128,2,128,8]{2,3,0,1:T(8,128)(2,1)S(1)}, bf16[128,2,128,8]{2,3,0,1:T(8,128)(2,1)S(1)}, u32[]{:S(2)}, u32[]{:S(2)}) %collective-permute-start.8) | collective-permute-done | bytes 524320 | tf_op jit(solution)/shard_map/ppermute | solution.py:35
  273.7 1.3 collective-permute-start.13
  275.0 0.9 constant_dynamic-update-slice_fusion.9
  275.9 26.8 %collective-permute-done.9 = bf16[128,2,128,8]{2,3,0,1:T(8,128)(2,1)S(1)} collective-permute-done((bf16[128,2,128,8]{2,3,0,1:T(8,128)(2,1)S(1)}, bf16[128,2,128,8]{2,3,0,1:T(8,128)(2,1)S(1)}, u32[]{:S(2)}, u32[]{:S(2)}) %collective-permute-start.9) | collective-permute-done | bytes 524320 | tf_op jit(solution)/shard_map/ppermute | solution.py:35
  302.7 1.3 collective-permute-start.14
  304.0 0.9 constant_dynamic-update-slice_fusion.8
  304.9 1.3 collective-permute-start.15
  306.2 0.9 constant_dynamic-update-slice_fusion.7
  307.1 24.0 %collective-permute-done.11 = bf16[128,2,128,8]{2,3,0,1:T(8,128)(2,1)S(1)} collective-permute-done((bf16[128,2,128,8]{2,3,0,1:T(8,128)(2,1)S(1)}, bf16[128,2,128,8]{2,3,0,1:T(8,128)(2,1)S(1)}, u32[]{:S(2)}, u32[]{:S(2)}) %collective-permute-start.11) | collective-permute-done | bytes 524320 | tf_op jit(solution)/shard_map/ppermute | solution.py:35
  331.1 1.3 collective-permute-start.16
  332.4 0.9 constant_dynamic-update-slice_fusion.6
  333.3 4.1 collective-permute-done.12
  337.4 1.5 collective-permute-start.17
  338.8 0.9 constant_dynamic-update-slice_fusion.5
  339.7 30.4 %collective-permute-done.13 = bf16[128,2,128,8]{2,3,0,1:T(8,128)(2,1)S(1)} collective-permute-done((bf16[128,2,128,8]{2,3,0,1:T(8,128)(2,1)S(1)}, bf16[128,2,128,8]{2,3,0,1:T(8,128)(2,1)S(1)}, u32[]{:S(2)}, u32[]{:S(2)}) %collective-permute-start.13) | collective-permute-done | bytes 524320 | tf_op jit(solution)/shard_map/ppermute | solution.py:35
  370.1 0.9 constant_dynamic-update-slice_fusion.4
  371.0 0.9 constant_dynamic-update-slice_fusion.3
  371.9 0.9 constant_dynamic-update-slice_fusion.2
  372.8 0.9 constant_dynamic-update-slice_fusion.1
  373.8 122.2 %collective-permute-done.17 = bf16[128,2,128,8]{2,3,0,1:T(8,128)(2,1)S(1)} collective-permute-done((bf16[128,2,128,8]{2,3,0,1:T(8,128)(2,1)S(1)}, bf16[128,2,128,8]{2,3,0,1:T(8,128)(2,1)S(1)}, u32[]{:S(2)}, u32[]{:S(2)}) %collective-permute-start.17) | collective-permute-done | bytes 524320 | tf_op jit(solution)/shard_map/ppermute | solution.py:35
  495.9 0.9 constant_dynamic-update-slice_fusion
  496.8 5.1 slice_bitcast_fusion.1
  502.0 3.5 fusion
  505.5 2.5 copy.56
  508.0 7.8 %gather_fusion = f32[1032,128,2]{1,2,0:T(2,128)S(1)} fusion(f32[128,2,8,136]{0,1,3,2:T(2,128)S(1)} %copy.56, s32[1032]{0:T(1024)S(1)} %reshape.277), kind=kCustom, calls=%fused_computation | custom fusion | bytes 2121792 | tf_op jit(solution)/shard_map/gather | solution.py:110
  515.8 2.3 multiply_bitcast_fusion
  (28 shorter events, 0.6 us)
Async XLA Ops:
  6.5 96.9 %reduce-scatter.2.cloned.1.call-start = ((), (), s32[]{:S(2)}) async-start(), calls=%async_computation.2 | async-start | bytes 5242880 | tf_op jit(solution)/shard_map/reduce_scatter | solution.py:67
  24.2 8.2 %copy-start.1 = (s32[1024]{0:T(1024)S(1)}, s32[1024]{0:T(1024)}, u32[]{:S(2)}) copy-start(s32[1024]{0:T(1024)} %param.5) | copy-start | bytes 12292
  103.4 12.6 %copy-start = (f32[128,2,1024]{2,0,1:T(8,128)S(1)}, f32[128,2,1024]{2,0,1:T(8,128)}, u32[]{:S(2)}) copy-start(f32[128,2,1024]{2,0,1:T(8,128)} %reduce-scatter.2.cloned.1.call-done) | copy-start | bytes 3145732
  104.8 29.4 %copy-start.2 = (s32[8]{0:T(128)S(1)}, s32[8]{0:T(128)}, u32[]{:S(2)}) copy-start(s32[8]{0:T(128)} %param.7) | copy-start | bytes 100
  104.8 29.4 %copy-start.3 = (s32[8]{0:T(128)S(1)}, s32[8]{0:T(128)}, u32[]{:S(2)}) copy-start(s32[8]{0:T(128)} %param.6) | copy-start | bytes 100
  104.9 6.1 %collective-permute-start = (f32[32,1024]{1,0:T(8,128)S(1)}, f32[32,1024]{1,0:T(8,128)S(1)}, u32[]{:S(2)}, u32[]{:S(2)}) collective-permute-start(f32[32,1024]{1,0:T(8,128)S(1)} %get-tuple-element.9), channel_id=1, source_target_pairs={{0,1},{1,2},{2,3},{4,5},{5,6},{6,7},{8,9},{9,10},{10,11},{12,13},{... | collective-permute-start | bytes 393224 | tf_op jit(solution)/shard_map/ppermute | solution.py:23
  107.7 7.8 %collective-permute-start.1 = (f32[32,1024]{1,0:T(8,128)S(1)}, f32[32,1024]{1,0:T(8,128)S(1)}, u32[]{:S(2)}, u32[]{:S(2)}) collective-permute-start(f32[32,1024]{1,0:T(8,128)S(1)} %get-tuple-element.10), channel_id=1, source_target_pairs={{1,0},{2,1},{3,2},{5,4},{6,5},{7,6},{9,8},{10,9},{11,10},{13,12},{... | collective-permute-start | bytes 393224 | tf_op jit(solution)/shard_map/ppermute | solution.py:25
  117.3 47.7 %all-to-all-start = ((bf16[128,2,128,8]{0,3,1,2:T(8,128)(2,1)}), bf16[128,2,128,8]{0,3,1,2:T(8,128)(2,1)S(1)}, u32[]{:S(2)}, u32[]{:S(2)}) async-start(bf16[128,2,128,8]{0,3,1,2:T(8,128)(2,1)} %copy.35), calls=%async_computation.1 | async-start | bytes 1048576 | tf_op jit(solution)/shard_map/all_to_all | solution.py:85
  165.6 26.7 %collective-permute-start.2 = (bf16[128,2,128,8]{2,3,0,1:T(8,128)(2,1)S(1)}, bf16[128,2,128,8]{2,3,0,1:T(8,128)(2,1)S(1)}, u32[]{:S(2)}, u32[]{:S(2)}) collective-permute-start(bf16[128,2,128,8]{2,3,0,1:T(8,128)(2,1)S(1)} %copy.36), channel_id=1, source_target_pairs={{4,0},{8,4},{12,8},{16,12},{20,16},{24,20},{28,24},{32,28},{36,32}... | collective-permute-start | bytes 1572872 | tf_op jit(solution)/shard_map/ppermute | solution.py:35
  169.0 40.5 %collective-permute-start.3 = (bf16[128,2,128,8]{2,3,0,1:T(8,128)(2,1)S(1)}, bf16[128,2,128,8]{2,3,0,1:T(8,128)(2,1)S(1)}, u32[]{:S(2)}, u32[]{:S(2)}) collective-permute-start(bf16[128,2,128,8]{2,3,0,1:T(8,128)(2,1)S(1)} %copy.36), channel_id=1, source_target_pairs={{8,0},{12,4},{16,8},{20,12},{24,16},{28,20},{32,24},{36,28},{40,32... | collective-permute-start | bytes 1572872 | tf_op jit(solution)/shard_map/ppermute | solution.py:35
  171.5 54.6 %collective-permute-start.4 = (bf16[128,2,128,8]{2,3,0,1:T(8,128)(2,1)S(1)}, bf16[128,2,128,8]{2,3,0,1:T(8,128)(2,1)S(1)}, u32[]{:S(2)}, u32[]{:S(2)}) collective-permute-start(bf16[128,2,128,8]{2,3,0,1:T(8,128)(2,1)S(1)} %copy.36), channel_id=1, source_target_pairs={{12,0},{16,4},{20,8},{24,12},{28,16},{32,20},{36,24},{40,28},{44,3... | collective-permute-start | bytes 1572872 | tf_op jit(solution)/shard_map/ppermute | solution.py:35
  174.0 66.1 %collective-permute-start.5 = (bf16[128,2,128,8]{2,3,0,1:T(8,128)(2,1)S(1)}, bf16[128,2,128,8]{2,3,0,1:T(8,128)(2,1)S(1)}, u32[]{:S(2)}, u32[]{:S(2)}) collective-permute-start(bf16[128,2,128,8]{2,3,0,1:T(8,128)(2,1)S(1)} %copy.36), channel_id=1, source_target_pairs={{16,0},{20,4},{24,8},{28,12},{32,16},{36,20},{40,24},{44,28},{48,3... | collective-permute-start | bytes 1572872 | tf_op jit(solution)/shard_map/ppermute | solution.py:35
  175.9 75.4 %collective-permute-start.6 = (bf16[128,2,128,8]{2,3,0,1:T(8,128)(2,1)S(1)}, bf16[128,2,128,8]{2,3,0,1:T(8,128)(2,1)S(1)}, u32[]{:S(2)}, u32[]{:S(2)}) collective-permute-start(bf16[128,2,128,8]{2,3,0,1:T(8,128)(2,1)S(1)} %copy.36), channel_id=1, source_target_pairs={{20,0},{24,4},{28,8},{32,12},{36,16},{40,20},{44,24},{48,28},{52,3... | collective-permute-start | bytes 1572872 | tf_op jit(solution)/shard_map/ppermute | solution.py:35
  192.3 70.2 %collective-permute-start.7 = (bf16[128,2,128,8]{2,3,0,1:T(8,128)(2,1)S(1)}, bf16[128,2,128,8]{2,3,0,1:T(8,128)(2,1)S(1)}, u32[]{:S(2)}, u32[]{:S(2)}) collective-permute-start(bf16[128,2,128,8]{2,3,0,1:T(8,128)(2,1)S(1)} %copy.36), channel_id=1, source_target_pairs={{24,0},{28,4},{32,8},{36,12},{40,16},{44,20},{48,24},{52,28},{56,3... | collective-permute-start | bytes 1572872 | tf_op jit(solution)/shard_map/ppermute | solution.py:35
  209.4 64.3 %collective-permute-start.8 = (bf16[128,2,128,8]{2,3,0,1:T(8,128)(2,1)S(1)}, bf16[128,2,128,8]{2,3,0,1:T(8,128)(2,1)S(1)}, u32[]{:S(2)}, u32[]{:S(2)}) collective-permute-start(bf16[128,2,128,8]{2,3,0,1:T(8,128)(2,1)S(1)} %copy.36), channel_id=1, source_target_pairs={{28,0},{32,4},{36,8},{40,12},{44,16},{48,20},{52,24},{56,28},{60,3... | collective-permute-start | bytes 1572872 | tf_op jit(solution)/shard_map/ppermute | solution.py:35
  226.1 76.6 %collective-permute-start.9 = (bf16[128,2,128,8]{2,3,0,1:T(8,128)(2,1)S(1)}, bf16[128,2,128,8]{2,3,0,1:T(8,128)(2,1)S(1)}, u32[]{:S(2)}, u32[]{:S(2)}) collective-permute-start(bf16[128,2,128,8]{2,3,0,1:T(8,128)(2,1)S(1)} %copy.36), channel_id=1, source_target_pairs={{32,0},{36,4},{40,8},{44,12},{48,16},{52,20},{56,24},{60,28},{64,3... | collective-permute-start | bytes 1572872 | tf_op jit(solution)/shard_map/ppermute | solution.py:35
  240.0 64.9 %collective-permute-start.10 = (bf16[128,2,128,8]{2,3,0,1:T(8,128)(2,1)S(1)}, bf16[128,2,128,8]{2,3,0,1:T(8,128)(2,1)S(1)}, u32[]{:S(2)}, u32[]{:S(2)}) collective-permute-start(bf16[128,2,128,8]{2,3,0,1:T(8,128)(2,1)S(1)} %copy.36), channel_id=1, source_target_pairs={{36,0},{40,4},{44,8},{48,12},{52,16},{56,20},{60,24},{64,28},{68,3... | collective-permute-start | bytes 1572872 | tf_op jit(solution)/shard_map/ppermute | solution.py:35
  251.3 79.8 %collective-permute-start.11 = (bf16[128,2,128,8]{2,3,0,1:T(8,128)(2,1)S(1)}, bf16[128,2,128,8]{2,3,0,1:T(8,128)(2,1)S(1)}, u32[]{:S(2)}, u32[]{:S(2)}) collective-permute-start(bf16[128,2,128,8]{2,3,0,1:T(8,128)(2,1)S(1)} %copy.36), channel_id=1, source_target_pairs={{40,0},{44,4},{48,8},{52,12},{56,16},{60,20},{64,24},{68,28},{72,3... | collective-permute-start | bytes 1572872 | tf_op jit(solution)/shard_map/ppermute | solution.py:35
  262.5 74.9 %collective-permute-start.12 = (bf16[128,2,128,8]{2,3,0,1:T(8,128)(2,1)S(1)}, bf16[128,2,128,8]{2,3,0,1:T(8,128)(2,1)S(1)}, u32[]{:S(2)}, u32[]{:S(2)}) collective-permute-start(bf16[128,2,128,8]{2,3,0,1:T(8,128)(2,1)S(1)} %copy.36), channel_id=1, source_target_pairs={{44,0},{48,4},{52,8},{56,12},{60,16},{64,20},{68,24},{72,28},{76,3... | collective-permute-start | bytes 1572872 | tf_op jit(solution)/shard_map/ppermute | solution.py:35
  273.7 96.3 %collective-permute-start.13 = (bf16[128,2,128,8]{2,3,0,1:T(8,128)(2,1)S(1)}, bf16[128,2,128,8]{2,3,0,1:T(8,128)(2,1)S(1)}, u32[]{:S(2)}, u32[]{:S(2)}) collective-permute-start(bf16[128,2,128,8]{2,3,0,1:T(8,128)(2,1)S(1)} %copy.36), channel_id=1, source_target_pairs={{48,0},{52,4},{56,8},{60,12},{64,16},{68,20},{72,24},{76,28},{80,3... | collective-permute-start | bytes 1572872 | tf_op jit(solution)/shard_map/ppermute | solution.py:35
  302.7 68.3 %collective-permute-start.14 = (bf16[128,2,128,8]{2,3,0,1:T(8,128)(2,1)S(1)}, bf16[128,2,128,8]{2,3,0,1:T(8,128)(2,1)S(1)}, u32[]{:S(2)}, u32[]{:S(2)}) collective-permute-start(bf16[128,2,128,8]{2,3,0,1:T(8,128)(2,1)S(1)} %copy.36), channel_id=1, source_target_pairs={{52,0},{56,4},{60,8},{64,12},{68,16},{72,20},{76,24},{80,28},{84,3... | collective-permute-start | bytes 1572872 | tf_op jit(solution)/shard_map/ppermute | solution.py:35
  304.9 67.0 %collective-permute-start.15 = (bf16[128,2,128,8]{2,3,0,1:T(8,128)(2,1)S(1)}, bf16[128,2,128,8]{2,3,0,1:T(8,128)(2,1)S(1)}, u32[]{:S(2)}, u32[]{:S(2)}) collective-permute-start(bf16[128,2,128,8]{2,3,0,1:T(8,128)(2,1)S(1)} %copy.36), channel_id=1, source_target_pairs={{56,0},{60,4},{64,8},{68,12},{72,16},{76,20},{80,24},{84,28},{88,3... | collective-permute-start | bytes 1572872 | tf_op jit(solution)/shard_map/ppermute | solution.py:35
  331.1 41.7 %collective-permute-start.16 = (bf16[128,2,128,8]{2,3,0,1:T(8,128)(2,1)S(1)}, bf16[128,2,128,8]{2,3,0,1:T(8,128)(2,1)S(1)}, u32[]{:S(2)}, u32[]{:S(2)}) collective-permute-start(bf16[128,2,128,8]{2,3,0,1:T(8,128)(2,1)S(1)} %copy.36), channel_id=1, source_target_pairs={{60,0},{64,4},{68,8},{72,12},{76,16},{80,20},{84,24},{88,28},{92,3... | collective-permute-start | bytes 1572872 | tf_op jit(solution)/shard_map/ppermute | solution.py:35
  337.4 158.6 %collective-permute-start.17 = (bf16[128,2,128,8]{2,3,0,1:T(8,128)(2,1)S(1)}, bf16[128,2,128,8]{2,3,0,1:T(8,128)(2,1)S(1)}, u32[]{:S(2)}, u32[]{:S(2)}) collective-permute-start(bf16[128,2,128,8]{2,3,0,1:T(8,128)(2,1)S(1)} %copy.36), channel_id=1, source_target_pairs={{64,0},{68,4},{72,8},{76,12},{80,16},{84,20},{88,24},{92,28},{96,3... | collective-permute-start | bytes 1572872 | tf_op jit(solution)/shard_map/ppermute | solution.py:35
Sparse Core Ops, SparseCore 0:
  32.5 70.8 reduce-scatter.1
where the time goes:
time: 526 us; the launch traced here: 525 us
  waiting for transfers between devices  394 us (75%)
  starting transfers between devices  49.9 us (9%)
  local copies, waits for them, and re-layouts  32.7 us (6%)
  other arithmetic  22.9 us (4%)
  between operations  13.8 us (3%)
  matrix products  12.2 us (2%)
    ppermute x16, waiting for transfers between devices, passed_along(): lax.ppermute(value, axis, [(source, source + steps) for source in range(i...  287 us
    reduce_scatter x1, waiting for transfers between devices, per_device(): lax.psum_scatter(jnp.dot(basis_table, local_record, preferred_element_typ...  71 us
    all_to_all x1, waiting for transfers between devices, per_device(): lax.all_to_all(whitened.reshape(band_rows, 2, slab_count, slab_width), 'c...  30.7 us
    ppermute x16, starting transfers between devices, passed_along(): lax.ppermute(value, axis, [(source, source + steps) for source in range(i...  28.3 us
    convert_element_type x1, other arithmetic, taper_table(): real_row = (tapers[None, :] * jnp.cos(angles)).astype(jnp.bfloat16)  17.5 us
    all_to_all x1, starting transfers between devices, per_device(): lax.all_to_all(whitened.reshape(band_rows, 2, slab_count, slab_width), 'c...  16.8 us
    unnamed x24, local copies, waits for them, and re-layouts  14.4 us
  transfers between devices with their start and end apart: 20, of which 15 were waited for; matrix products, arithmetic and copies ran while one was open for 3% of the time, Pallas kernels for 0%

commit v1 on v0

--- a/solution.py
+++ b/solution.py
@@ -29,12 +29,6 @@
     return cells
 
 
-def passed_along(value, axis, steps):
-    count = lax.axis_size(axis)
-    initial, last = (max(0, -steps), min(count, count - steps))
-    return lax.ppermute(value, axis, [(source, source + steps) for source in range(initial, last)])
-
-
 def taper_table(bin_index, sample_index, length):
     phase_index = bin_index[:, None] * sample_index[None, :] % length
     angles = phase_index.astype(jnp.float32) * (2.0 * math.pi / length)
@@ -54,19 +48,18 @@
     )
 
 
-def per_device(records, quality, band_low, band_high):
+def whiten_local(records, quality):
     local_record = records[0]
     quarter = local_record.shape[0]
     channels = local_record.shape[1]
-    band_rows = BINS // lax.axis_size("af")
+    parts = lax.axis_size("af")
+    band_rows = BINS // parts
     sample_index = lax.axis_index("af") * quarter + jnp.arange(quarter, dtype=jnp.int32)
-    bin_index = LOWBIN + jnp.int32(0) + jnp.arange(lax.axis_size("af") * band_rows, dtype=jnp.int32)
-    basis_table = taper_table(bin_index, sample_index, SEGLEN).reshape(
-        2 * (lax.axis_size("af") * band_rows), quarter
-    )
+    bin_index = LOWBIN + jnp.arange(BINS, dtype=jnp.int32)
+    basis_table = taper_table(bin_index, sample_index, SEGLEN).reshape(2 * BINS, quarter)
     spectra = lax.psum_scatter(
         jnp.dot(basis_table, local_record, preferred_element_type=jnp.float32).reshape(
-            lax.axis_size("af") * band_rows, 2, channels
+            BINS, 2, channels
         ),
         "af",
         scatter_dimension=0,
@@ -78,41 +71,57 @@
     factor = quality.astype(jnp.float32)[None, :] / jnp.sqrt(
         smoothed * (1.0 / (2 * SMOOTH + 1)) + 1e-06
     )
-    whitened = (spectra * factor[:, None, :]).astype(jnp.bfloat16)
+    return (spectra * factor[:, None, :]).astype(jnp.bfloat16)
+
+
+def bin_cross(whitened, block):
+    segs, _, channels = whitened.shape
+    blocks = channels // block
+    real_w = whitened[:, 0]
+    imag_w = whitened[:, 1]
+    right = jnp.concatenate([real_w, imag_w], axis=0)
+    left = jnp.stack([right, jnp.concatenate([imag_w, -real_w], axis=0)], axis=0)
+    depth = right.shape[0]
+    right_pad = jnp.pad(right, ((0, 0), (0, block))).reshape(depth, blocks + 1, block)
+    windows = jnp.concatenate([right_pad[:, :blocks], right_pad[:, 1:]], axis=2)
+    left_blocks = left.reshape(2, depth, blocks, block)
+    gram = jnp.einsum(
+        "pkbc,kbe->bcpe", left_blocks, windows, preferred_element_type=jnp.float32
+    )
+    width = 2 * block
+    flat = gram.transpose(0, 2, 1, 3).reshape(blocks, 2, block * width)
+    flat = jnp.pad(flat, ((0, 0), (0, 0), (0, block)))
+    skew = flat.reshape(blocks, 2, block, width + 1)[:, :, :, : REACH + 1]
+    return skew.transpose(0, 2, 3, 1).reshape(channels, REACH + 1, 2)
+
+
+def per_device(records, quality, band_low, band_high):
+    whitened = whiten_local(records, quality)
+    band_rows, _, channels = whitened.shape
     slab_count = lax.axis_size("ch")
     slab_width = channels // slab_count
-    above_count = REACH // slab_width
-    centre = lax.all_to_all(
-        whitened.reshape(band_rows, 2, slab_count, slab_width),
+    by_bin = lax.all_to_all(
+        whitened.reshape(band_rows, 1, 2, channels),
         "ch",
-        split_axis=2,
-        concat_axis=2,
+        split_axis=0,
+        concat_axis=1,
+        tiled=True,
+    )[0]
+    segments = by_bin.shape[0]
+    cross = bin_cross(by_bin, REACH)
+    back = lax.all_to_all(
+        cross.reshape(slab_count, slab_width, REACH + 1, 2),
+        "ch",
+        split_axis=0,
+        concat_axis=0,
         tiled=True,
     )
-    pieces = [centre]
-    for block_index in range(1, above_count + 1):
-        pieces.append(passed_along(centre, "ch", -block_index))
-    joined = jnp.concatenate(pieces, axis=3)
-    segments = centre.shape[2]
-    real_a = centre[:, 0]
-    imag_a = centre[:, 1]
-    left_side = jnp.stack(
-        [jnp.concatenate([real_a, imag_a], axis=1), jnp.concatenate([imag_a, -real_a], axis=1)],
-        axis=1,
-    )
-    right_side = jnp.concatenate([joined[:, 0], joined[:, 1]], axis=1)
-    cross_all = jnp.einsum(
-        "fpsc,fse->fpce", left_side, right_side, preferred_element_type=jnp.float32
-    )
     offsets = jnp.arange(REACH + 1, dtype=jnp.int32)
-    row_ids = jnp.arange(slab_width, dtype=jnp.int32)[:, None]
-    target = row_ids + offsets[None, :]
-    picked = cross_all[:, :, row_ids, target]
     inside_band = (
         (offsets[None, :] >= band_low[:, None]) & (offsets[None, :] <= band_high[:, None])
     ).astype(jnp.float32)
     result = (
-        jnp.transpose(picked, (2, 3, 1, 0))
+        jnp.transpose(back, (1, 2, 3, 0))
         * inside_band[:, :, None, None]
         * (1.0 / math.sqrt(segments))
     )

time: 526 us -> 293 us (0.56)
  the two profiles are of different devices: /device:TPU:33 before, /device:TPU:6 now
where the time goes in v1:
time: 293 us; the launch traced here: 289 us
  waiting for transfers between devices  171 us (58%)
  blocking collectives  47.2 us (16%)
  other arithmetic  20.9 us (7%)
  local copies, waits for them, and re-layouts  15.9 us (5%)
  between operations  13.6 us (5%)
  starting transfers between devices  11.9 us (4%)
  matrix products  8.3 us (3%)
    all_to_all x1, waiting for transfers between devices, per_device(): lax.all_to_all(cross.reshape(slab_count, slab_width, REACH + 1, 2), 'ch',...  97.7 us
    reduce_scatter x1, waiting for transfers between devices, whiten_local(): lax.psum_scatter(jnp.dot(basis_table, local_record, preferred_element_typ...  70.8 us
    all_to_all x1, blocking collectives, per_device(): lax.all_to_all(whitened.reshape(band_rows, 1, 2, channels), 'ch', split_a...  47.2 us
    convert_element_type x1, other arithmetic, taper_table(): real_row = (tapers[None, :] * jnp.cos(angles)).astype(jnp.bfloat16)  17.5 us
    all_to_all x1, starting transfers between devices, per_device(): lax.all_to_all(cross.reshape(slab_count, slab_width, REACH + 1, 2), 'ch',...  9.07 us
    dot_general x1, matrix products, whiten_local(): jnp.dot(basis_table, local_record, preferred_element_type=jnp.float32)  6.02 us
  transfers between devices with their start and end apart: 4, of which 3 were waited for; matrix products, arithmetic and copies ran while one was open for 0% of the time, Pallas kernels for 0%

profile of v1, /device:TPU:6, one launch (start us, length us, event | category | flops | bytes accessed | tf_op | source)
XLA Modules:
  0.0 288.8 jit_solution(11344321749798023196)
XLA Ops:
  6.5 0.0 reduce-scatter.2.cloned.1.call-start
  6.5 0.1 multiply_subtract_fusion
  6.6 0.0 copy-start.4
  6.6 17.5 %multiply_convert_fusion = (bf16[512,1,2048]{2,0,1:T(8,128)(2,1)S(1)}, bf16[512,1,2048]{2,0,1:T(8,128)(2,1)S(1)}) fusion(s32[2048]{0:T(1024)S(1)} %iota_add_fusion, s32[512]{0:T(512)S(1)} %iota_add_fusion.1, f32[2048]{0:T(1024)S(1)} %multiply_subtract_fusion), kind=kLoop, calls=%fused_computation.14 | loop fusion | flops 19922944 | bytes 4212736 | tf_op jit(solution)/shard_map/convert_element_type | solution.py:36
  24.2 0.0 copy-done.4
  24.2 6.0 %fusion.3 = f32[512,2,1024]{2,0,1:T(8,128)} fusion(bf16[512,1,2048]{2,0,1:T(8,128)(2,1)S(1)} %get-tuple-element.14, bf16[512,1,2048]{2,0,1:T(8,128)(2,1)S(1)} %get-tuple-element.13, bf16[1,2048,1024]{2,1,0:T(8,128)(2,1)S(1)} %copy-done.4), kind=kOutput, calls=%fused_computation.8 | convolution fusion | flops 4297064448 | bytes 12582912 | tf_op jit(solution)/shard_map/dot_general | solution.py:61
  30.2 0.0 copy-start.1
  30.2 0.0 reduce-scatter.2.cloned.1.call-update
  30.2 0.7 copy-done.1
  30.9 70.8 %reduce-scatter.2.cloned.1.call-done = f32[128,2,1024]{2,0,1:T(8,128)} async-done(((f32[512,2,1024]{2,0,1:T(8,128)}), f32[128,2,1024]{2,0,1:T(8,128)}) %reduce-scatter.2.cloned.1.call-update) | async-done | bytes 1048592 | tf_op jit(solution)/shard_map/reduce_scatter | solution.py:60
  101.7 0.0 copy-start
  101.7 1.4 fusion.30
  103.1 1.6 collective-permute-start
  104.7 1.3 collective-permute-start.1
  106.0 0.0 copy-done
  106.0 0.1 fusion.40
  106.1 0.0 collective-permute-done
  106.1 2.3 collective-permute-done.1
  108.4 0.5 fusion.10
  108.9 0.1 fusion.29
  109.1 0.5 copy.20
  109.6 47.2 %all_to_all.14 = bf16[128,1,2,1024]{3,2,1,0:T(2,128)(2,1)S(1)} all-to-all(bf16[128,1,2,1024]{3,2,1,0:T(2,128)(2,1)S(1)} %copy.20), channel_id=1, replica_groups=mesh['ch'=128,'af'=4] {'ch'}, dimensions={0} | all-to-all | bytes 1048576 | tf_op jit(solution)/shard_map/all_to_all | solution.py:103
  156.8 0.5 copy.21
  157.4 0.1 slice_bitcast_fusion.3
  157.5 0.1 fusion.28
  157.6 0.1 fusion.39
  157.7 0.3 copy.28
  158.0 0.3 copy.29
  158.2 0.1 neg.19
  158.3 1.8 fusion.13
  160.1 2.7 reshape.283
  162.7 1.2 copy.24
  164.0 1.5 pad.9
  165.4 3.7 %reshape.284 = f32[8,2,128,257]{3,2,0,1:T(8,128)S(1)} reshape(f32[8,2,32896]{2,0,1:T(8,128)} %pad.9) | data formatting | bytes 4210688 | tf_op jit(solution)/shard_map/reshape | solution.py:94
  169.1 0.2 slice.54
  169.3 1.6 copy.25
  170.9 0.0 copy-start.2
  170.9 0.0 copy-start.3
  170.9 9.1 %all-to-all-start.1 = ((f32[128,8,129,2]{2,1,3,0:T(8,128)}), f32[128,8,129,2]{2,1,3,0:T(8,128)S(1)}, u32[]{:S(2)}, u32[]{:S(2)}) async-start(f32[128,8,129,2]{2,1,3,0:T(8,128)} %copy.25), calls=%async_computation.2 | async-start | bytes 4194304 | tf_op jit(solution)/shard_map/all_to_all | solution.py:112
  180.0 0.0 copy-done.2
  180.0 0.0 copy-done.3
  180.0 0.1 fusion.35
  180.1 97.7 %all-to-all-done.1 = f32[128,8,129,2]{2,1,3,0:T(8,128)S(1)} async-done(((f32[128,8,129,2]{2,1,3,0:T(8,128)}), f32[128,8,129,2]{2,1,3,0:T(8,128)S(1)}, u32[]{:S(2)}, u32[]{:S(2)}) %all-to-all-start.1) | async-done | bytes 1056800 | tf_op jit(solution)/shard_map/all_to_all | solution.py:112
  277.7 1.6 multiply_bitcast_fusion
  279.3 2.6 copy.26
  (5 shorter events, 0.0 us)
Async XLA Ops:
  6.5 95.2 %reduce-scatter.2.cloned.1.call-start = ((), (), s32[]{:S(2)}) async-start(), calls=%async_computation.3 | async-start | bytes 5242880 | tf_op jit(solution)/shard_map/reduce_scatter | solution.py:60
  6.6 17.6 %copy-start.4 = (bf16[1,2048,1024]{2,1,0:T(8,128)(2,1)S(1)}, bf16[1,2048,1024]{2,1,0:T(8,128)(2,1)}, u32[]{:S(2)}) copy-start(bf16[1,2048,1024]{2,1,0:T(8,128)(2,1)} %param.4) | copy-start | bytes 12582916
  30.2 0.7 copy-start.1
  101.7 4.3 %copy-start = (f32[128,2,1024]{2,0,1:T(8,128)S(1)}, f32[128,2,1024]{2,0,1:T(8,128)}, u32[]{:S(2)}) copy-start(f32[128,2,1024]{2,0,1:T(8,128)} %reduce-scatter.2.cloned.1.call-done) | copy-start | bytes 3145732
  103.1 3.0 %collective-permute-start = (f32[32,1024]{1,0:T(8,128)S(1)}, f32[32,1024]{1,0:T(8,128)S(1)}, u32[]{:S(2)}, u32[]{:S(2)}) collective-permute-start(f32[32,1024]{1,0:T(8,128)S(1)} %get-tuple-element.11), channel_id=1, source_target_pairs={{0,1},{1,2},{2,3},{4,5},{5,6},{6,7},{8,9},{9,10},{10,11},{12,13},{... | collective-permute-start | bytes 393224 | tf_op jit(solution)/shard_map/ppermute | solution.py:23
  104.7 3.7 %collective-permute-start.1 = (f32[32,1024]{1,0:T(8,128)S(1)}, f32[32,1024]{1,0:T(8,128)S(1)}, u32[]{:S(2)}, u32[]{:S(2)}) collective-permute-start(f32[32,1024]{1,0:T(8,128)S(1)} %get-tuple-element.12), channel_id=1, source_target_pairs={{1,0},{2,1},{3,2},{5,4},{6,5},{7,6},{9,8},{10,9},{11,10},{13,12},{... | collective-permute-start | bytes 393224 | tf_op jit(solution)/shard_map/ppermute | solution.py:25
  170.9 9.1 %copy-start.2 = (s32[8]{0:T(128)S(1)}, s32[8]{0:T(128)}, u32[]{:S(2)}) copy-start(s32[8]{0:T(128)} %param.7) | copy-start | bytes 100
  170.9 9.1 %copy-start.3 = (s32[8]{0:T(128)S(1)}, s32[8]{0:T(128)}, u32[]{:S(2)}) copy-start(s32[8]{0:T(128)} %param.6) | copy-start | bytes 100
  170.9 106.8 %all-to-all-start.1 = ((f32[128,8,129,2]{2,1,3,0:T(8,128)}), f32[128,8,129,2]{2,1,3,0:T(8,128)S(1)}, u32[]{:S(2)}, u32[]{:S(2)}) async-start(f32[128,8,129,2]{2,1,3,0:T(8,128)} %copy.25), calls=%async_computation.2 | async-start | bytes 4194304 | tf_op jit(solution)/shard_map/all_to_all | solution.py:112
Sparse Core Ops, SparseCore 0:
  30.3 71.3 reduce-scatter.1

commit v2 on v1

--- a/solution.py
+++ b/solution.py
@@ -29,12 +29,25 @@
     return cells
 
 
-def taper_table(bin_index, sample_index, length):
-    phase_index = bin_index[:, None] * sample_index[None, :] % length
-    angles = phase_index.astype(jnp.float32) * (2.0 * math.pi / length)
-    tapers = 0.5 - 0.5 * jnp.cos(sample_index.astype(jnp.float32) * (2.0 * math.pi / length))
-    real_row = (tapers[None, :] * jnp.cos(angles)).astype(jnp.bfloat16)
-    imag_row = (-(tapers[None, :] * jnp.sin(angles))).astype(jnp.bfloat16)
+def taper_table(bin_index, sample_start, quarter, length):
+    fine = 64
+    coarse = quarter // fine
+    step = 2.0 * math.pi / length
+    coarse_t = sample_start + fine * jnp.arange(coarse, dtype=jnp.int32)
+    fine_t = jnp.arange(fine, dtype=jnp.int32)
+    coarse_angle = (bin_index[:, None] * coarse_t[None, :] % length).astype(jnp.float32) * step
+    fine_angle = (bin_index[:, None] * fine_t[None, :] % length).astype(jnp.float32) * step
+    cos_c = jnp.cos(coarse_angle)[:, :, None]
+    sin_c = jnp.sin(coarse_angle)[:, :, None]
+    cos_f = jnp.cos(fine_angle)[:, None, :]
+    sin_f = jnp.sin(fine_angle)[:, None, :]
+    rows = bin_index.shape[0]
+    cos_a = (cos_c * cos_f - sin_c * sin_f).reshape(rows, quarter)
+    sin_a = (sin_c * cos_f + cos_c * sin_f).reshape(rows, quarter)
+    sample_index = sample_start + jnp.arange(quarter, dtype=jnp.int32)
+    tapers = 0.5 - 0.5 * jnp.cos(sample_index.astype(jnp.float32) * step)
+    real_row = (tapers[None, :] * cos_a).astype(jnp.bfloat16)
+    imag_row = (-(tapers[None, :] * sin_a)).astype(jnp.bfloat16)
     return jnp.stack([real_row, imag_row], axis=1)
 
 
@@ -54,9 +67,9 @@
     channels = local_record.shape[1]
     parts = lax.axis_size("af")
     band_rows = BINS // parts
-    sample_index = lax.axis_index("af") * quarter + jnp.arange(quarter, dtype=jnp.int32)
+    sample_start = lax.axis_index("af") * quarter
     bin_index = LOWBIN + jnp.arange(BINS, dtype=jnp.int32)
-    basis_table = taper_table(bin_index, sample_index, SEGLEN).reshape(2 * BINS, quarter)
+    basis_table = taper_table(bin_index, sample_start, quarter, SEGLEN).reshape(2 * BINS, quarter)
     spectra = lax.psum_scatter(
         jnp.dot(basis_table, local_record, preferred_element_type=jnp.float32).reshape(
             BINS, 2, channels
@@ -110,12 +123,12 @@
     segments = by_bin.shape[0]
     cross = bin_cross(by_bin, REACH)
     back = lax.all_to_all(
-        cross.reshape(slab_count, slab_width, REACH + 1, 2),
+        cross.astype(jnp.bfloat16).reshape(slab_count, slab_width, REACH + 1, 2),
         "ch",
         split_axis=0,
         concat_axis=0,
         tiled=True,
-    )
+    ).astype(jnp.float32)
     offsets = jnp.arange(REACH + 1, dtype=jnp.int32)
     inside_band = (
         (offsets[None, :] >= band_low[:, None]) & (offsets[None, :] <= band_high[:, None])

time: 293 us -> 243 us (0.83)
  waiting for transfers between devices: 171 us -> 129 us
  other arithmetic: 20.9 us -> 12.3 us
  local copies, waits for them, and re-layouts: 15.9 us -> 20 us
    all_to_all x1, waiting for transfers between devices: 97.7 us -> 55.7 us  [per_device(): lax.all_to_all(cross.astype(jnp.bfloat16).reshape(slab_count, slab_width,...]
    convert_element_type x1, other arithmetic: 17.5 us -> 4.79 us  [taper_table(): real_row = (tapers[None, :] * cos_a).astype(jnp.bfloat16)]
    sub x0 -> x1, local copies, waits for them, and re-layouts: none -> 5.47 us  [taper_table(): cos_a = (cos_c * cos_f - sin_c * sin_f).reshape(rows, quarter)]
    add x0 -> x1, local copies, waits for them, and re-layouts: none -> 5.44 us  [taper_table(): sin_a = (sin_c * cos_f + cos_c * sin_f).reshape(rows, quarter)]
    sub x1 -> x2, other arithmetic: 0.05 us -> 4.54 us  [the longest x1 4.49 us: taper_table(): cos_a = (cos_c * cos_f - sin_c * sin_f).reshape(rows, quarter)]
    reshape x2, local copies, waits for them, and re-layouts: 3.87 us -> 0.86 us  [bin_cross(): flat = gram.transpose(0, 2, 1, 3).reshape(blocks, 2, block * width)]
where the time goes in v2:
time: 243 us; the launch traced here: 241 us
  waiting for transfers between devices  129 us (53%)
  blocking collectives  47.2 us (19%)
  local copies, waits for them, and re-layouts  20 us (8%)
  between operations  13.6 us (6%)
  other arithmetic  12.3 us (5%)
  starting transfers between devices  11.8 us (5%)
  matrix products  7 us (3%)
    reduce_scatter x1, waiting for transfers between devices, whiten_local(): lax.psum_scatter(jnp.dot(basis_table, local_record, preferred_element_typ...  70.8 us
    all_to_all x1, waiting for transfers between devices, per_device(): lax.all_to_all(cross.astype(jnp.bfloat16).reshape(slab_count, slab_width,...  55.7 us
    all_to_all x1, blocking collectives, per_device(): lax.all_to_all(whitened.reshape(band_rows, 1, 2, channels), 'ch', split_a...  47.2 us
    all_to_all x1, starting transfers between devices, per_device(): lax.all_to_all(cross.astype(jnp.bfloat16).reshape(slab_count, slab_width,...  8.92 us
    dot_general x1, matrix products, whiten_local(): jnp.dot(basis_table, local_record, preferred_element_type=jnp.float32)  6.04 us
    sub x1, local copies, waits for them, and re-layouts, taper_table(): cos_a = (cos_c * cos_f - sin_c * sin_f).reshape(rows, quarter)  5.47 us
    add x1, local copies, waits for them, and re-layouts, taper_table(): sin_a = (sin_c * cos_f + cos_c * sin_f).reshape(rows, quarter)  5.44 us
  transfers between devices with their start and end apart: 4, of which 3 were waited for; matrix products, arithmetic and copies ran while one was open for 0% of the time, Pallas kernels for 0%

profile of v2, /device:TPU:6, one launch (start us, length us, event | category | flops | bytes accessed | tf_op | source)
XLA Modules:
  0.0 240.7 jit_solution(4766008947748566075)
XLA Ops:
  6.5 0.0 reduce-scatter.2.cloned.1.call-start
  6.5 0.1 multiply_subtract_fusion.1
  6.6 0.5 fusion.40
  7.1 0.3 fusion.42
  7.5 4.5 %multiply_subtract_fusion = (f32[512,32,64]{0,2,1:T(8,128)}, f32[512,32,64]{0,2,1:T(8,128)}) fusion(f32[512,64]{0,1:T(8,128)S(1)} %get-tuple-element.20, f32[512,32]{0,1:T(8,128)S(1)} %get-tuple-element.18, f32[512,64]{0,1:T(8,128)S(1)} %get-tuple-element.19, f32[512,32]{0,1:T(8,128)S(1)} %get-tuple-element.17), kind=kLoop, calls=%fused_computation.8 | loop fusion | flops 6291456 | bytes 8781824 | tf_op jit(solution)/shard_map/sub | solution.py:45
  12.0 5.5 %copy.22 = f32[512,1,2048]{2,0,1:T(8,128)} copy(f32[512,1,2048]{0,2,1:T(8,128)} %bitcast.37) | data formatting | bytes 8388608 | tf_op jit(solution)/shard_map/sub | solution.py:45
  17.4 5.4 %copy.23 = f32[512,1,2048]{2,0,1:T(8,128)} copy(f32[512,1,2048]{0,2,1:T(8,128)} %bitcast.36) | data formatting | bytes 8388608 | tf_op jit(solution)/shard_map/add | solution.py:46
  22.9 0.0 copy-start.4
  22.9 4.8 %multiply_convert_fusion = (bf16[512,1,2048]{2,0,1:T(8,128)(2,1)S(1)}, bf16[512,1,2048]{2,0,1:T(8,128)(2,1)S(1)}) fusion(f32[512,1,2048]{2,0,1:T(8,128)} %copy.22, f32[2048]{0:T(1024)S(1)} %multiply_subtract_fusion.1, f32[512,1,2048]{2,0,1:T(8,128)} %copy.23), kind=kLoop, calls=%fused_computation.7 | loop fusion | flops 5242880 | bytes 12591104 | tf_op jit(solution)/shard_map/convert_element_type | solution.py:49
  27.7 0.0 copy-done.4
  27.7 6.0 %fusion = f32[512,2,1024]{2,0,1:T(8,128)} fusion(bf16[512,1,2048]{2,0,1:T(8,128)(2,1)S(1)} %get-tuple-element.16, bf16[512,1,2048]{2,0,1:T(8,128)(2,1)S(1)} %get-tuple-element.15, bf16[1,2048,1024]{2,1,0:T(8,128)(2,1)S(1)} %copy-done.4), kind=kOutput, calls=%fused_computation | convolution fusion | flops 4297064448 | bytes 12582912 | tf_op jit(solution)/shard_map/dot_general | solution.py:74
  33.7 0.0 copy-start.1
  33.7 0.0 reduce-scatter.2.cloned.1.call-update
  33.7 0.7 copy-done.1
  34.4 70.8 %reduce-scatter.2.cloned.1.call-done = f32[128,2,1024]{2,0,1:T(8,128)} async-done(((f32[512,2,1024]{2,0,1:T(8,128)}), f32[128,2,1024]{2,0,1:T(8,128)}) %reduce-scatter.2.cloned.1.call-update) | async-done | bytes 1048592 | tf_op jit(solution)/shard_map/reduce_scatter | solution.py:73
  105.2 0.0 copy-start
  105.2 1.4 fusion.26
  106.6 1.6 collective-permute-start
  108.2 1.3 collective-permute-start.1
  109.5 0.0 copy-done
  109.5 0.1 fusion.49
  109.6 0.0 collective-permute-done
  109.6 2.3 collective-permute-done.1
  111.9 0.5 fusion.7
  112.5 0.1 fusion.25
  112.6 0.5 copy.24
  113.1 47.2 %all_to_all.14 = bf16[128,1,2,1024]{3,2,1,0:T(2,128)(2,1)S(1)} all-to-all(bf16[128,1,2,1024]{3,2,1,0:T(2,128)(2,1)S(1)} %copy.24), channel_id=1, replica_groups=mesh['ch'=128,'af'=4] {'ch'}, dimensions={0} | all-to-all | bytes 1048576 | tf_op jit(solution)/shard_map/all_to_all | solution.py:116
  160.4 0.5 copy.25
  160.9 0.1 slice_bitcast_fusion.3
  161.0 0.1 fusion.24
  161.1 0.1 fusion.48
  161.2 0.3 copy.32
  161.5 0.3 copy.33
  161.8 0.1 neg.19
  161.8 0.4 convolution_convert_fusion
  162.3 0.3 reshape.377
  162.6 0.6 copy.28
  163.2 0.1 pad.10
  163.2 2.9 %reshape.378 = bf16[8,2,128,257]{3,2,0,1:T(8,128)(2,1)S(1)} reshape(bf16[8,2,32896]{2,0,1:T(8,128)(2,1)S(1)} %pad.10) | data formatting | bytes 2105344 | tf_op jit(solution)/shard_map/reshape | solution.py:107
  166.2 0.1 slice.55
  166.2 0.0 copy-start.2
  166.3 0.0 copy-start.3
  166.3 1.1 copy.29
  167.3 8.9 %all-to-all-start.1 = ((bf16[128,8,129,2]{2,1,3,0:T(8,128)(2,1)}), bf16[128,8,129,2]{2,1,3,0:T(8,128)(2,1)S(1)}, u32[]{:S(2)}, u32[]{:S(2)}) async-start(bf16[128,8,129,2]{2,1,3,0:T(8,128)(2,1)} %copy.29), calls=%async_computation.2 | async-start | bytes 2097152 | tf_op jit(solution)/shard_map/all_to_all | solution.py:125
  176.2 0.0 copy-done.2
  176.3 0.0 copy-done.3
  176.3 0.1 fusion.44
  176.3 55.7 %all-to-all-done.1 = bf16[128,8,129,2]{2,1,3,0:T(8,128)(2,1)S(1)} async-done(((bf16[128,8,129,2]{2,1,3,0:T(8,128)(2,1)}), bf16[128,8,129,2]{2,1,3,0:T(8,128)(2,1)S(1)}, u32[]{:S(2)}, u32[]{:S(2)}) %all-to-all-start.1) | async-done | bytes 528416 | tf_op jit(solution)/shard_map/all_to_all | solution.py:125
  232.1 0.3 multiply_bitcast_fusion
  232.4 1.5 copy.30
  (5 shorter events, 0.0 us)
Async XLA Ops:
  6.5 98.7 %reduce-scatter.2.cloned.1.call-start = ((), (), s32[]{:S(2)}) async-start(), calls=%async_computation.3 | async-start | bytes 5242880 | tf_op jit(solution)/shard_map/reduce_scatter | solution.py:73
  22.9 4.8 %copy-start.4 = (bf16[1,2048,1024]{2,1,0:T(8,128)(2,1)S(1)}, bf16[1,2048,1024]{2,1,0:T(8,128)(2,1)}, u32[]{:S(2)}) copy-start(bf16[1,2048,1024]{2,1,0:T(8,128)(2,1)} %param.4) | copy-start | bytes 12582916
  33.7 0.7 copy-start.1
  105.2 4.3 %copy-start = (f32[128,2,1024]{2,0,1:T(8,128)S(1)}, f32[128,2,1024]{2,0,1:T(8,128)}, u32[]{:S(2)}) copy-start(f32[128,2,1024]{2,0,1:T(8,128)} %reduce-scatter.2.cloned.1.call-done) | copy-start | bytes 3145732
  106.6 3.0 %collective-permute-start = (f32[32,1024]{1,0:T(8,128)S(1)}, f32[32,1024]{1,0:T(8,128)S(1)}, u32[]{:S(2)}, u32[]{:S(2)}) collective-permute-start(f32[32,1024]{1,0:T(8,128)S(1)} %get-tuple-element.11), channel_id=1, source_target_pairs={{0,1},{1,2},{2,3},{4,5},{5,6},{6,7},{8,9},{9,10},{10,11},{12,13},{... | collective-permute-start | bytes 393224 | tf_op jit(solution)/shard_map/ppermute | solution.py:23
  108.2 3.7 %collective-permute-start.1 = (f32[32,1024]{1,0:T(8,128)S(1)}, f32[32,1024]{1,0:T(8,128)S(1)}, u32[]{:S(2)}, u32[]{:S(2)}) collective-permute-start(f32[32,1024]{1,0:T(8,128)S(1)} %get-tuple-element.12), channel_id=1, source_target_pairs={{1,0},{2,1},{3,2},{5,4},{6,5},{7,6},{9,8},{10,9},{11,10},{13,12},{... | collective-permute-start | bytes 393224 | tf_op jit(solution)/shard_map/ppermute | solution.py:25
  166.2 10.0 %copy-start.2 = (s32[8]{0:T(128)S(1)}, s32[8]{0:T(128)}, u32[]{:S(2)}) copy-start(s32[8]{0:T(128)} %param.7) | copy-start | bytes 100
  166.3 10.0 %copy-start.3 = (s32[8]{0:T(128)S(1)}, s32[8]{0:T(128)}, u32[]{:S(2)}) copy-start(s32[8]{0:T(128)} %param.6) | copy-start | bytes 100
  167.3 64.7 %all-to-all-start.1 = ((bf16[128,8,129,2]{2,1,3,0:T(8,128)(2,1)}), bf16[128,8,129,2]{2,1,3,0:T(8,128)(2,1)S(1)}, u32[]{:S(2)}, u32[]{:S(2)}) async-start(bf16[128,8,129,2]{2,1,3,0:T(8,128)(2,1)} %copy.29), calls=%async_computation.2 | async-start | bytes 2097152 | tf_op jit(solution)/shard_map/all_to_all | solution.py:125
Sparse Core Ops, SparseCore 0:
  33.9 71.3 reduce-scatter.1

commit v3 on v1

--- a/solution.py
+++ b/solution.py
@@ -29,13 +29,38 @@
     return cells
 
 
-def taper_table(bin_index, sample_index, length):
-    phase_index = bin_index[:, None] * sample_index[None, :] % length
-    angles = phase_index.astype(jnp.float32) * (2.0 * math.pi / length)
-    tapers = 0.5 - 0.5 * jnp.cos(sample_index.astype(jnp.float32) * (2.0 * math.pi / length))
-    real_row = (tapers[None, :] * jnp.cos(angles)).astype(jnp.bfloat16)
-    imag_row = (-(tapers[None, :] * jnp.sin(angles))).astype(jnp.bfloat16)
+def taper_table(bin_start, sample_index, length):
+    fine = 64
+    groups = 8
+    step = 2.0 * math.pi / length
+    coarse_bins = bin_start + fine * jnp.arange(groups, dtype=jnp.int32)
+    fine_bins = jnp.arange(fine, dtype=jnp.int32)
+    coarse_angle = (coarse_bins[:, None] * sample_index[None, :] % length).astype(jnp.float32) * step
+    fine_angle = (fine_bins[:, None] * sample_index[None, :] % length).astype(jnp.float32) * step
+    cos_c = jnp.cos(coarse_angle)[:, None, :]
+    sin_c = jnp.sin(coarse_angle)[:, None, :]
+    cos_f = jnp.cos(fine_angle)[None, :, :]
+    sin_f = jnp.sin(fine_angle)[None, :, :]
+    rows = groups * fine
+    cos_a = (cos_c * cos_f - sin_c * sin_f).reshape(rows, -1)
+    sin_a = (sin_c * cos_f + cos_c * sin_f).reshape(rows, -1)
+    tapers = 0.5 - 0.5 * jnp.cos(sample_index.astype(jnp.float32) * step)
+    real_row = (tapers[None, :] * cos_a).astype(jnp.bfloat16)
+    imag_row = (-(tapers[None, :] * sin_a)).astype(jnp.bfloat16)
     return jnp.stack([real_row, imag_row], axis=1)
+
+
+def reduce_scatter_af(partial):
+    index = lax.axis_index("af")
+    core = index % 2
+    chip = index // 2
+    quarters = partial.reshape(2, 2, partial.shape[0] // 4, *partial.shape[1:])
+    keep = lax.dynamic_index_in_dim(quarters, core, axis=1, keepdims=False)
+    send = lax.dynamic_index_in_dim(quarters, 1 - core, axis=1, keepdims=False)
+    half = keep + lax.ppermute(send, "af", [(0, 1), (1, 0), (2, 3), (3, 2)])
+    keep = lax.dynamic_index_in_dim(half, chip, axis=0, keepdims=False)
+    send = lax.dynamic_index_in_dim(half, 1 - chip, axis=0, keepdims=False)
+    return keep + lax.ppermute(send, "af", [(0, 2), (2, 0), (1, 3), (3, 1)])
 
 
 def band_sum(padded, half_width):
@@ -55,15 +80,11 @@
     parts = lax.axis_size("af")
     band_rows = BINS // parts
     sample_index = lax.axis_index("af") * quarter + jnp.arange(quarter, dtype=jnp.int32)
-    bin_index = LOWBIN + jnp.arange(BINS, dtype=jnp.int32)
-    basis_table = taper_table(bin_index, sample_index, SEGLEN).reshape(2 * BINS, quarter)
-    spectra = lax.psum_scatter(
+    basis_table = taper_table(LOWBIN, sample_index, SEGLEN).reshape(2 * BINS, quarter)
+    spectra = reduce_scatter_af(
         jnp.dot(basis_table, local_record, preferred_element_type=jnp.float32).reshape(
             BINS, 2, channels
-        ),
-        "af",
-        scatter_dimension=0,
-        tiled=True,
+        )
     )
     power_bins = spectra[:, 0] * spectra[:, 0] + spectra[:, 1] * spectra[:, 1]
     padded = extended(power_bins, (("af", 0),), SMOOTH)
@@ -110,12 +131,12 @@
     segments = by_bin.shape[0]
     cross = bin_cross(by_bin, REACH)
     back = lax.all_to_all(
-        cross.reshape(slab_count, slab_width, REACH + 1, 2),
+        cross.astype(jnp.bfloat16).reshape(slab_count, slab_width, REACH + 1, 2),
         "ch",
         split_axis=0,
         concat_axis=0,
         tiled=True,
-    )
+    ).astype(jnp.float32)
     offsets = jnp.arange(REACH + 1, dtype=jnp.int32)
     inside_band = (
         (offsets[None, :] >= band_low[:, None]) & (offsets[None, :] <= band_high[:, None])

time: 293 us -> 185 us (0.63)
  waiting for transfers between devices: 171 us -> 88.8 us
  between operations: 13.6 us -> 0.39 us
  other arithmetic: 20.9 us -> 9.58 us
  starting transfers between devices: 11.9 us -> 18.5 us
  local copies, waits for them, and re-layouts: 15.9 us -> 11.4 us
    reduce_scatter x1 -> x0, waiting for transfers between devices: 70.8 us -> none  [whiten_local(): lax.psum_scatter(jnp.dot(basis_table, local_record, preferred_element_typ...]
    all_to_all x1, waiting for transfers between devices: 97.7 us -> 55.7 us  [per_device(): lax.all_to_all(cross.astype(jnp.bfloat16).reshape(slab_count, slab_width,...]
    ppermute x0 -> x2, waiting for transfers between devices: none -> 27.8 us  [the longest x1 23.6 us: reduce_scatter_af(): return keep + lax.ppermute(send, 'af', [(0, 2), (2, 0), (1, 3), (3, 1)])]
    convert_element_type x1, other arithmetic: 17.5 us -> 1.2 us  [taper_table(): real_row = (tapers[None, :] * cos_a).astype(jnp.bfloat16)]
    ppermute x0 -> x2, starting transfers between devices: none -> 7.01 us  [the longest x1 5.1 us: reduce_scatter_af(): return keep + lax.ppermute(send, 'af', [(0, 2), (2, 0), (1, 3), (3, 1)])]
    add x1 -> x3, other arithmetic: 0.01 us -> 3.98 us  [the longest x1 2.61 us: reduce_scatter_af(): half = keep + lax.ppermute(send, 'af', [(0, 1), (1, 0), (2, 3), (3, 2)])]
    reshape x2, local copies, waits for them, and re-layouts: 3.87 us -> 0.86 us  [bin_cross(): flat = gram.transpose(0, 2, 1, 3).reshape(blocks, 2, block * width)]
    ppermute x1, waiting for transfers between devices: 2.31 us -> 5.26 us  [extended(): lax.ppermute(head, axis, [((i + 1) % count, i) for i in range(ends)])]
  transfers between devices with their start and end apart: 4 -> 5, of which waited for: 3 -> 4; matrix products, arithmetic and copies ran while one was open for 0% -> 0% of each run, Pallas kernels for 0% -> 0%
where the time goes in v3:
time: 185 us; the launch traced here: 183 us
  waiting for transfers between devices  88.8 us (48%)
  blocking collectives  49.3 us (27%)
  starting transfers between devices  18.5 us (10%)
  local copies, waits for them, and re-layouts  11.4 us (6%)
  other arithmetic  9.58 us (5%)
  matrix products  5.44 us (3%)
    all_to_all x1, waiting for transfers between devices, per_device(): lax.all_to_all(cross.astype(jnp.bfloat16).reshape(slab_count, slab_width,...  55.7 us
    all_to_all x1, blocking collectives, per_device(): lax.all_to_all(whitened.reshape(band_rows, 1, 2, channels), 'ch', split_a...  49.3 us
    ppermute x1, waiting for transfers between devices, reduce_scatter_af(): return keep + lax.ppermute(send, 'af', [(0, 2), (2, 0), (1, 3), (3, 1)])  23.6 us
    all_to_all x1, starting transfers between devices, per_device(): lax.all_to_all(cross.astype(jnp.bfloat16).reshape(slab_count, slab_width,...  8.92 us
    ppermute x1, waiting for transfers between devices, extended(): lax.ppermute(head, axis, [((i + 1) % count, i) for i in range(ends)])  5.26 us
    ppermute x1, starting transfers between devices, reduce_scatter_af(): return keep + lax.ppermute(send, 'af', [(0, 2), (2, 0), (1, 3), (3, 1)])  5.1 us
    dot_general x1, matrix products, whiten_local(): jnp.dot(basis_table, local_record, preferred_element_type=jnp.float32)  4.48 us
    ppermute x1, waiting for transfers between devices, reduce_scatter_af(): half = keep + lax.ppermute(send, 'af', [(0, 1), (1, 0), (2, 3), (3, 2)])  4.23 us
  transfers between devices with their start and end apart: 5, of which 4 were waited for; matrix products, arithmetic and copies ran while one was open for 0% of the time, Pallas kernels for 0%

profile of v3, /device:TPU:6, one launch (start us, length us, event | category | flops | bytes accessed | tf_op | source)
XLA Modules:
  0.0 183.4 jit_solution(15796282115065816590)
XLA Ops:
  0.0 0.1 multiply_subtract_fusion.1
  0.1 2.0 %fusion.34 = (f32[64,2048]{1,0:T(8,128)S(1)}, f32[64,2048]{1,0:T(8,128)S(1)}) fusion(s32[2048]{0:T(1024)S(1)} %iota_add_fusion), kind=kLoop, calls=%fused_computation.53 | loop fusion | flops 1835008 | bytes 1056768 | tf_op jit(solution)/shard_map/cos | solution.py:42
  2.1 0.3 fusion.42
  2.5 1.2 multiply_subtract_fusion
  3.7 0.0 copy-start.4
  3.7 1.2 multiply_convert_fusion
  4.9 1.0 copy-done.4
  5.9 4.5 %fusion = f32[2,2,128,2,1024]{4,2,3,1,0:T(8,128)S(1)} fusion(bf16[2,2,128,1,2048]{4,2,3,1,0:T(8,128)(2,1)S(1)} %get-tuple-element.18, bf16[2,2,128,1,2048]{4,2,3,1,0:T(8,128)(2,1)S(1)} %get-tuple-element.17, bf16[1,2048,1024]{2,1,0:T(8,128)(2,1)S(1)} %copy-done.4), kind=kOutput, calls=%fused_computation | convolution fusion | flops 4297064448 | bytes 12582912 | tf_op jit(solution)/shard_map/dot_general | solution.py:85
  10.3 0.0 copy-start
  10.4 0.1 dynamic-slice_bitcast_fusion
  10.5 1.8 copy-done
  12.3 1.9 %collective-permute-start = (f32[2,128,2,1024]{3,1,2,0:T(8,128)S(1)}, f32[2,128,2,1024]{3,1,2,0:T(8,128)}, u32[]{:S(2)}, u32[]{:S(2)}) collective-permute-start(f32[2,128,2,1024]{3,1,2,0:T(8,128)S(1)} %dynamic-slice_bitcast_fusion), channel_id=1, source_target_pairs={{0,1},{1,0},{2,3},{3,2},{4,5},{5,4},{6,7},{7,6},{8,9},{9,8},{10,11... | collective-permute-start | bytes 6291464 | tf_op jit(solution)/shard_map/ppermute | solution.py:60
  14.3 4.2 %collective-permute-done = f32[2,128,2,1024]{3,1,2,0:T(8,128)} collective-permute-done((f32[2,128,2,1024]{3,1,2,0:T(8,128)S(1)}, f32[2,128,2,1024]{3,1,2,0:T(8,128)}, u32[]{:S(2)}, u32[]{:S(2)}) %collective-permute-start) | collective-permute-done | bytes 2097184 | tf_op jit(solution)/shard_map/ppermute | solution.py:60
  18.5 2.6 %bitcast_add_fusion = f32[2,128,2,1024]{3,1,2,0:T(8,128)S(1)} fusion(f32[2,128,2,1024]{3,1,2,0:T(8,128)} %collective-permute-done, f32[2,2,128,2,1024]{4,2,3,1,0:T(8,128)} %copy-done, s32[]{:T(128)S(6)} %select_n.54), kind=kLoop, calls=%fused_computation.9 | loop fusion | flops 524288 | bytes 6291460 | tf_op jit(solution)/shard_map/add | solution.py:60
  21.1 0.0 copy-start.1
  21.1 0.1 dynamic-slice_bitcast_fusion.1
  21.2 5.1 %collective-permute-start.1 = (f32[128,2,1024]{2,0,1:T(8,128)S(1)}, f32[128,2,1024]{2,0,1:T(8,128)}, u32[]{:S(2)}, u32[]{:S(2)}) collective-permute-start(f32[128,2,1024]{2,0,1:T(8,128)S(1)} %dynamic-slice_bitcast_fusion.1), channel_id=1, source_target_pairs={{0,2},{2,0},{1,3},{3,1},{4,6},{6,4},{5,7},{7,5},{8,10},{10,8},{9,1... | collective-permute-start | bytes 3145736 | tf_op jit(solution)/shard_map/ppermute | solution.py:63
  26.3 0.0 copy-done.1
  26.4 23.6 %collective-permute-done.1 = f32[128,2,1024]{2,0,1:T(8,128)} collective-permute-done((f32[128,2,1024]{2,0,1:T(8,128)S(1)}, f32[128,2,1024]{2,0,1:T(8,128)}, u32[]{:S(2)}, u32[]{:S(2)}) %collective-permute-start.1) | collective-permute-done | bytes 1048608 | tf_op jit(solution)/shard_map/ppermute | solution.py:63
  49.9 1.4 bitcast_add_fusion.1
  51.3 0.1 fusion.29
  51.4 1.3 collective-permute-start.2
  52.7 1.3 collective-permute-start.3
  54.0 0.1 fusion.49
  54.1 0.0 collective-permute-done.2
  54.1 5.3 %collective-permute-done.3 = f32[32,1024]{1,0:T(8,128)S(1)} collective-permute-done((f32[32,1024]{1,0:T(8,128)S(1)}, f32[32,1024]{1,0:T(8,128)S(1)}, u32[]{:S(2)}, u32[]{:S(2)}) %collective-permute-start.3) | collective-permute-done | bytes 131104 | tf_op jit(solution)/shard_map/ppermute | solution.py:25
  59.4 0.5 fusion.7
  59.9 0.1 fusion.28
  60.0 0.5 copy.13
  60.6 49.3 %all_to_all.14 = bf16[128,1,2,1024]{3,2,1,0:T(2,128)(2,1)S(1)} all-to-all(bf16[128,1,2,1024]{3,2,1,0:T(2,128)(2,1)S(1)} %copy.13), channel_id=1, replica_groups=mesh['ch'=128,'af'=4] {'ch'}, dimensions={0} | all-to-all | bytes 1048576 | tf_op jit(solution)/shard_map/all_to_all | solution.py:124
  109.9 0.5 copy.14
  110.4 0.1 slice_bitcast_fusion.3
  110.6 0.1 fusion.24
  110.6 0.1 fusion.48
  110.7 0.3 copy.22
  111.0 0.3 copy.23
  111.3 0.1 neg.20
  111.4 0.4 convolution_convert_fusion
  111.8 0.3 reshape.368
  112.1 0.6 copy.17
  112.7 0.1 pad.10
  112.8 2.9 %reshape.369 = bf16[8,2,128,257]{3,2,0,1:T(8,128)(2,1)S(1)} reshape(bf16[8,2,32896]{2,0,1:T(8,128)(2,1)S(1)} %pad.10) | data formatting | bytes 2105344 | tf_op jit(solution)/shard_map/reshape | solution.py:115
  115.7 0.1 slice.55
  115.8 0.0 copy-start.2
  115.8 0.0 copy-start.3
  115.8 1.1 copy.18
  116.8 8.9 %all-to-all-start.1 = ((bf16[128,8,129,2]{2,1,3,0:T(8,128)(2,1)}), bf16[128,8,129,2]{2,1,3,0:T(8,128)(2,1)S(1)}, u32[]{:S(2)}, u32[]{:S(2)}) async-start(bf16[128,8,129,2]{2,1,3,0:T(8,128)(2,1)} %copy.18), calls=%async_computation.1 | async-start | bytes 2097152 | tf_op jit(solution)/shard_map/all_to_all | solution.py:133
  125.8 0.0 copy-done.2
  125.8 0.0 copy-done.3
  125.8 0.1 fusion.44
  125.9 55.7 %all-to-all-done.1 = bf16[128,8,129,2]{2,1,3,0:T(8,128)(2,1)S(1)} async-done(((bf16[128,8,129,2]{2,1,3,0:T(8,128)(2,1)}), bf16[128,8,129,2]{2,1,3,0:T(8,128)(2,1)S(1)}, u32[]{:S(2)}, u32[]{:S(2)}) %all-to-all-start.1) | async-done | bytes 528416 | tf_op jit(solution)/shard_map/all_to_all | solution.py:133
  181.6 0.3 multiply_bitcast_fusion
  181.9 1.5 copy.19
  (5 shorter events, 0.0 us)
Async XLA Ops:
  3.7 2.2 %copy-start.4 = (bf16[1,2048,1024]{2,1,0:T(8,128)(2,1)S(1)}, bf16[1,2048,1024]{2,1,0:T(8,128)(2,1)}, u32[]{:S(2)}) copy-start(bf16[1,2048,1024]{2,1,0:T(8,128)(2,1)} %param.4) | copy-start | bytes 12582916
  10.3 2.0 %copy-start = (f32[2,2,128,2,1024]{4,2,3,1,0:T(8,128)}, f32[2,2,128,2,1024]{4,2,3,1,0:T(8,128)S(1)}, u32[]{:S(2)}) copy-start(f32[2,2,128,2,1024]{4,2,3,1,0:T(8,128)S(1)} %fusion) | copy-start | bytes 12582916
  12.3 6.2 %collective-permute-start = (f32[2,128,2,1024]{3,1,2,0:T(8,128)S(1)}, f32[2,128,2,1024]{3,1,2,0:T(8,128)}, u32[]{:S(2)}, u32[]{:S(2)}) collective-permute-start(f32[2,128,2,1024]{3,1,2,0:T(8,128)S(1)} %dynamic-slice_bitcast_fusion), channel_id=1, source_target_pairs={{0,1},{1,0},{2,3},{3,2},{4,5},{5,4},{6,7},{7,6},{8,9},{9,8},{10,11... | collective-permute-start | bytes 6291464 | tf_op jit(solution)/shard_map/ppermute | solution.py:60
  21.1 5.2 %copy-start.1 = (s32[1024]{0:T(1024)S(1)}, s32[1024]{0:T(1024)}, u32[]{:S(2)}) copy-start(s32[1024]{0:T(1024)} %param.5) | copy-start | bytes 12292
  21.2 28.7 %collective-permute-start.1 = (f32[128,2,1024]{2,0,1:T(8,128)S(1)}, f32[128,2,1024]{2,0,1:T(8,128)}, u32[]{:S(2)}, u32[]{:S(2)}) collective-permute-start(f32[128,2,1024]{2,0,1:T(8,128)S(1)} %dynamic-slice_bitcast_fusion.1), channel_id=1, source_target_pairs={{0,2},{2,0},{1,3},{3,1},{4,6},{6,4},{5,7},{7,5},{8,10},{10,8},{9,1... | collective-permute-start | bytes 3145736 | tf_op jit(solution)/shard_map/ppermute | solution.py:63
  51.4 2.7 %collective-permute-start.2 = (f32[32,1024]{1,0:T(8,128)S(1)}, f32[32,1024]{1,0:T(8,128)S(1)}, u32[]{:S(2)}, u32[]{:S(2)}) collective-permute-start(f32[32,1024]{1,0:T(8,128)S(1)} %get-tuple-element.13), channel_id=1, source_target_pairs={{0,1},{1,2},{2,3},{4,5},{5,6},{6,7},{8,9},{9,10},{10,11},{12,13},{... | collective-permute-start | bytes 393224 | tf_op jit(solution)/shard_map/ppermute | solution.py:23
  52.7 6.7 %collective-permute-start.3 = (f32[32,1024]{1,0:T(8,128)S(1)}, f32[32,1024]{1,0:T(8,128)S(1)}, u32[]{:S(2)}, u32[]{:S(2)}) collective-permute-start(f32[32,1024]{1,0:T(8,128)S(1)} %get-tuple-element.14), channel_id=1, source_target_pairs={{1,0},{2,1},{3,2},{5,4},{6,5},{7,6},{9,8},{10,9},{11,10},{13,12},{... | collective-permute-start | bytes 393224 | tf_op jit(solution)/shard_map/ppermute | solution.py:25
  115.8 10.0 %copy-start.2 = (s32[8]{0:T(128)S(1)}, s32[8]{0:T(128)}, u32[]{:S(2)}) copy-start(s32[8]{0:T(128)} %param.7) | copy-start | bytes 100
  115.8 10.0 %copy-start.3 = (s32[8]{0:T(128)S(1)}, s32[8]{0:T(128)}, u32[]{:S(2)}) copy-start(s32[8]{0:T(128)} %param.6) | copy-start | bytes 100
  116.8 64.7 %all-to-all-start.1 = ((bf16[128,8,129,2]{2,1,3,0:T(8,128)(2,1)}), bf16[128,8,129,2]{2,1,3,0:T(8,128)(2,1)S(1)}, u32[]{:S(2)}, u32[]{:S(2)}) async-start(bf16[128,8,129,2]{2,1,3,0:T(8,128)(2,1)} %copy.18), calls=%async_computation.1 | async-start | bytes 2097152 | tf_op jit(solution)/shard_map/all_to_all | solution.py:133

commit v4 on v3

--- a/solution.py
+++ b/solution.py
@@ -95,7 +95,7 @@
     return (spectra * factor[:, None, :]).astype(jnp.bfloat16)
 
 
-def bin_cross(whitened, block):
+def bin_cross(whitened, block, slab_width):
     segs, _, channels = whitened.shape
     blocks = channels // block
     real_w = whitened[:, 0]
@@ -107,13 +107,15 @@
     windows = jnp.concatenate([right_pad[:, :blocks], right_pad[:, 1:]], axis=2)
     left_blocks = left.reshape(2, depth, blocks, block)
     gram = jnp.einsum(
-        "pkbc,kbe->bcpe", left_blocks, windows, preferred_element_type=jnp.float32
-    )
+        "pkbc,kbe->bpce", left_blocks, windows, preferred_element_type=jnp.float32
+    ).astype(jnp.bfloat16)
     width = 2 * block
-    flat = gram.transpose(0, 2, 1, 3).reshape(blocks, 2, block * width)
+    flat = gram.reshape(blocks, 2, block * width)
     flat = jnp.pad(flat, ((0, 0), (0, 0), (0, block)))
     skew = flat.reshape(blocks, 2, block, width + 1)[:, :, :, : REACH + 1]
-    return skew.transpose(0, 2, 3, 1).reshape(channels, REACH + 1, 2)
+    slabs = block // slab_width
+    rows = skew.reshape(blocks, 2, slabs, slab_width * (REACH + 1)).transpose(0, 2, 1, 3)
+    return rows.reshape(blocks * slabs, 2 * slab_width * (REACH + 1))
 
 
 def per_device(records, quality, band_low, band_high):
@@ -129,20 +131,15 @@
         tiled=True,
     )[0]
     segments = by_bin.shape[0]
-    cross = bin_cross(by_bin, REACH)
-    back = lax.all_to_all(
-        cross.astype(jnp.bfloat16).reshape(slab_count, slab_width, REACH + 1, 2),
-        "ch",
-        split_axis=0,
-        concat_axis=0,
-        tiled=True,
-    ).astype(jnp.float32)
+    rows = bin_cross(by_bin, REACH, slab_width)
+    back = lax.all_to_all(rows, "ch", split_axis=0, concat_axis=0, tiled=True)
+    back = back.reshape(slab_count, 2, slab_width, REACH + 1).astype(jnp.float32)
     offsets = jnp.arange(REACH + 1, dtype=jnp.int32)
     inside_band = (
         (offsets[None, :] >= band_low[:, None]) & (offsets[None, :] <= band_high[:, None])
     ).astype(jnp.float32)
     result = (
-        jnp.transpose(back, (1, 2, 3, 0))
+        jnp.transpose(back, (2, 3, 1, 0))
         * inside_band[:, :, None, None]
         * (1.0 / math.sqrt(segments))
     )

time: 185 us -> 175 us (0.946)
  waiting for transfers between devices: 88.8 us -> 66.2 us
  local copies, waits for them, and re-layouts: 11.4 us -> 17.1 us
  other arithmetic: 9.58 us -> 13.6 us
  blocking collectives: 49.3 us -> 52.3 us
    all_to_all x1, waiting for transfers between devices: 55.7 us -> 37.5 us  [per_device(): back = lax.all_to_all(rows, 'ch', split_axis=0, concat_axis=0, tiled=True)]
    ppermute x1, waiting for transfers between devices: 5.26 us -> 0.01 us  [extended(): lax.ppermute(head, axis, [((i + 1) % count, i) for i in range(ends)])]
    all_to_all x0 -> x1, other arithmetic: none -> 4.13 us  [per_device(): back = lax.all_to_all(rows, 'ch', split_axis=0, concat_axis=0, tiled=True)]
    all_to_all x1, blocking collectives: 49.3 us -> 52.3 us  [per_device(): lax.all_to_all(whitened.reshape(band_rows, 1, 2, channels), 'ch', split_a...]
    all_to_all x0 -> x3, local copies, waits for them, and re-layouts: none -> 2.65 us  [per_device(): back = lax.all_to_all(rows, 'ch', split_axis=0, concat_axis=0, tiled=True)]
    unnamed x12 -> x14, local copies, waits for them, and re-layouts: 3.35 us -> 5.37 us
where the time goes in v4:
time: 175 us
  waiting for transfers between devices  66.2 us (38%)
  blocking collectives  52.3 us (30%)
  starting transfers between devices  19.8 us (11%)
  local copies, waits for them, and re-layouts  17.1 us (10%)
  other arithmetic  13.6 us (8%)
  matrix products  5.44 us (3%)
    all_to_all x1, blocking collectives, per_device(): lax.all_to_all(whitened.reshape(band_rows, 1, 2, channels), 'ch', split_a...  52.3 us
    all_to_all x1, waiting for transfers between devices, per_device(): back = lax.all_to_all(rows, 'ch', split_axis=0, concat_axis=0, tiled=True)  37.5 us
    ppermute x1, waiting for transfers between devices, reduce_scatter_af(): return keep + lax.ppermute(send, 'af', [(0, 2), (2, 0), (1, 3), (3, 1)])  23.6 us
    all_to_all x1, starting transfers between devices, per_device(): back = lax.all_to_all(rows, 'ch', split_axis=0, concat_axis=0, tiled=True)  8.44 us
    unnamed x14, local copies, waits for them, and re-layouts  5.37 us
    ppermute x1, starting transfers between devices, reduce_scatter_af(): return keep + lax.ppermute(send, 'af', [(0, 2), (2, 0), (1, 3), (3, 1)])  5.1 us
    dot_general x1, matrix products, whiten_local(): jnp.dot(basis_table, local_record, preferred_element_type=jnp.float32)  4.48 us
    ppermute x1, waiting for transfers between devices, reduce_scatter_af(): half = keep + lax.ppermute(send, 'af', [(0, 1), (1, 0), (2, 3), (3, 2)])  4.23 us
  transfers between devices with their start and end apart: 5, of which 4 were waited for; matrix products, arithmetic and copies ran while one was open for 0% of the time, Pallas kernels for 0%

profile of v4, /device:TPU:6, one launch (start us, length us, event | category | flops | bytes accessed | tf_op | source)
XLA Modules:
  0.0 174.8 jit_solution(12443002005334332731)
XLA Ops:
  0.0 0.1 multiply_subtract_fusion.1
  0.1 2.0 %fusion.34 = (f32[64,2048]{1,0:T(8,128)S(1)}, f32[64,2048]{1,0:T(8,128)S(1)}) fusion(s32[2048]{0:T(1024)S(1)} %iota_add_fusion), kind=kLoop, calls=%fused_computation.53 | loop fusion | flops 1835008 | bytes 1056768 | tf_op jit(solution)/shard_map/cos | solution.py:42
  2.1 0.3 fusion.42
  2.5 1.2 multiply_subtract_fusion
  3.7 0.0 copy-start.4
  3.7 1.2 multiply_convert_fusion
  4.9 1.0 copy-done.4
  5.9 4.5 %fusion = f32[2,2,128,2,1024]{4,2,3,1,0:T(8,128)S(1)} fusion(bf16[2,2,128,1,2048]{4,2,3,1,0:T(8,128)(2,1)S(1)} %get-tuple-element.18, bf16[2,2,128,1,2048]{4,2,3,1,0:T(8,128)(2,1)S(1)} %get-tuple-element.17, bf16[1,2048,1024]{2,1,0:T(8,128)(2,1)S(1)} %copy-done.4), kind=kOutput, calls=%fused_computation | convolution fusion | flops 4297064448 | bytes 12582912 | tf_op jit(solution)/shard_map/dot_general | solution.py:85
  10.3 0.0 copy-start
  10.4 0.1 dynamic-slice_bitcast_fusion
  10.5 1.8 %copy-done = f32[2,2,128,2,1024]{4,2,3,1,0:T(8,128)} copy-done((f32[2,2,128,2,1024]{4,2,3,1,0:T(8,128)}, f32[2,2,128,2,1024]{4,2,3,1,0:T(8,128)S(1)}, u32[]{:S(2)}) %copy-start) | copy-done | bytes 4194328
  12.3 1.9 %collective-permute-start = (f32[2,128,2,1024]{3,1,2,0:T(8,128)S(1)}, f32[2,128,2,1024]{3,1,2,0:T(8,128)}, u32[]{:S(2)}, u32[]{:S(2)}) collective-permute-start(f32[2,128,2,1024]{3,1,2,0:T(8,128)S(1)} %dynamic-slice_bitcast_fusion), channel_id=1, source_target_pairs={{0,1},{1,0},{2,3},{3,2},{4,5},{5,4},{6,7},{7,6},{8,9},{9,8},{10,11... | collective-permute-start | bytes 6291464 | tf_op jit(solution)/shard_map/ppermute | solution.py:60
  14.3 4.2 %collective-permute-done = f32[2,128,2,1024]{3,1,2,0:T(8,128)} collective-permute-done((f32[2,128,2,1024]{3,1,2,0:T(8,128)S(1)}, f32[2,128,2,1024]{3,1,2,0:T(8,128)}, u32[]{:S(2)}, u32[]{:S(2)}) %collective-permute-start) | collective-permute-done | bytes 2097184 | tf_op jit(solution)/shard_map/ppermute | solution.py:60
  18.5 2.6 %bitcast_add_fusion = f32[2,128,2,1024]{3,1,2,0:T(8,128)S(1)} fusion(f32[2,128,2,1024]{3,1,2,0:T(8,128)} %collective-permute-done, f32[2,2,128,2,1024]{4,2,3,1,0:T(8,128)} %copy-done, s32[]{:T(128)S(6)} %select_n.54), kind=kLoop, calls=%fused_computation.9 | loop fusion | flops 524288 | bytes 6291460 | tf_op jit(solution)/shard_map/add | solution.py:60
  21.1 0.0 copy-start.1
  21.1 0.1 dynamic-slice_bitcast_fusion.1
  21.2 5.1 %collective-permute-start.1 = (f32[128,2,1024]{2,0,1:T(8,128)S(1)}, f32[128,2,1024]{2,0,1:T(8,128)}, u32[]{:S(2)}, u32[]{:S(2)}) collective-permute-start(f32[128,2,1024]{2,0,1:T(8,128)S(1)} %dynamic-slice_bitcast_fusion.1), channel_id=1, source_target_pairs={{0,2},{2,0},{1,3},{3,1},{4,6},{6,4},{5,7},{7,5},{8,10},{10,8},{9,1... | collective-permute-start | bytes 3145736 | tf_op jit(solution)/shard_map/ppermute | solution.py:63
  26.3 0.0 copy-done.1
  26.4 23.6 %collective-permute-done.1 = f32[128,2,1024]{2,0,1:T(8,128)} collective-permute-done((f32[128,2,1024]{2,0,1:T(8,128)S(1)}, f32[128,2,1024]{2,0,1:T(8,128)}, u32[]{:S(2)}, u32[]{:S(2)}) %collective-permute-start.1) | collective-permute-done | bytes 1048608 | tf_op jit(solution)/shard_map/ppermute | solution.py:63
  49.9 1.4 bitcast_add_fusion.1
  51.3 0.1 fusion.29
  51.4 1.3 collective-permute-start.3
  52.7 3.0 %collective-permute-start.2 = (f32[32,1024]{1,0:T(8,128)S(1)}, f32[32,1024]{1,0:T(8,128)S(1)}, u32[]{:S(2)}, u32[]{:S(2)}) collective-permute-start(f32[32,1024]{1,0:T(8,128)S(1)} %get-tuple-element.13), channel_id=1, source_target_pairs={{0,1},{1,2},{2,3},{4,5},{5,6},{6,7},{8,9},{9,10},{10,11},{12,13},{... | collective-permute-start | bytes 393224 | tf_op jit(solution)/shard_map/ppermute | solution.py:23
  55.8 0.1 fusion.49
  55.8 0.0 collective-permute-done.3
  55.9 0.9 collective-permute-done.2
  56.7 0.5 fusion.7
  57.2 0.1 fusion.28
  57.4 0.5 copy.26
  57.9 52.3 %all_to_all.19 = bf16[128,1,2,1024]{3,2,1,0:T(2,128)(2,1)S(1)} all-to-all(bf16[128,1,2,1024]{3,2,1,0:T(2,128)(2,1)S(1)} %copy.26), channel_id=1, replica_groups=mesh['ch'=128,'af'=4] {'ch'}, dimensions={0} | all-to-all | bytes 1048576 | tf_op jit(solution)/shard_map/all_to_all | solution.py:126
  110.2 0.5 copy.27
  110.7 0.1 slice_bitcast_fusion.3
  110.9 0.1 neg.20
  110.9 0.1 fusion.24
  111.0 0.1 fusion.48
  111.1 0.3 copy.41
  111.4 0.3 copy.40
  111.7 0.4 convolution_convert_fusion
  112.1 0.3 reshape.373
  112.4 0.6 copy.30
  113.0 0.1 pad.9
  113.1 2.9 %reshape.374 = bf16[8,2,128,257]{3,2,0,1:T(8,128)(2,1)S(1)} reshape(bf16[8,2,32896]{2,0,1:T(8,128)(2,1)S(1)} %pad.9) | data formatting | bytes 2105344 | tf_op jit(solution)/shard_map/reshape | solution.py:115
  116.0 0.1 slice.54
  116.1 1.1 reshape.379
  117.1 0.6 copy.32
  117.7 0.7 all_to_all.16
  118.4 0.0 copy-start.2
  118.4 0.0 copy-start.3
  118.4 0.5 broadcast.278
  118.9 4.1 %reduce = bf16[128,2064]{1,0:T(8,128)(2,1)S(1)} reduce(bf16[128,1,2064]{2,1,0:T(2,128)(2,1)S(1)} %all_to_all.16, bf16[]{:T(256)} %broadcast.278), dimensions={1}, to_apply=%all_to_all.16.reduce_sub_computation | reduce | bytes 1056770 | tf_op jit(solution)/shard_map/all_to_all | solution.py:135
  123.1 1.4 reshape.380
  124.5 8.4 %all-to-all-start.1 = ((bf16[128,2,1032]{2,1,0:T(2,128)(2,1)}), bf16[128,2,1032]{2,1,0:T(2,128)(2,1)S(1)}, u32[]{:S(2)}, u32[]{:S(2)}) async-start(bf16[128,2,1032]{2,1,0:T(2,128)(2,1)} %reshape.380), calls=%async_computation.1 | async-start | bytes 1179648 | tf_op jit(solution)/shard_map/all_to_all | solution.py:135
  132.9 0.0 copy-done.2
  132.9 0.0 copy-done.3
  132.9 0.1 fusion.44
  133.0 37.5 %all-to-all-done.1 = bf16[128,2,1032]{2,1,0:T(2,128)(2,1)S(1)} async-done(((bf16[128,2,1032]{2,1,0:T(2,128)(2,1)}), bf16[128,2,1032]{2,1,0:T(2,128)(2,1)S(1)}, u32[]{:S(2)}, u32[]{:S(2)}) %all-to-all-start.1) | async-done | bytes 528416 | tf_op jit(solution)/shard_map/all_to_all | solution.py:135
  170.5 0.6 reshape.381
  171.2 1.5 copy.34
  172.7 0.1 reshape.376
  172.8 0.2 multiply_bitcast_fusion
  173.0 1.8 %copy.35 = f32[8,129,2,128]{3,2,1,0:T(2,128)} copy(f32[8,129,2,128]{3,1,0,2:T(8,128)S(1)} %multiply_bitcast_fusion) | data formatting | bytes 2113536 | tf_op jit(solution)/shard_map/mul | solution.py:142
  (5 shorter events, 0.0 us)
Async XLA Ops:
  3.7 2.2 %copy-start.4 = (bf16[1,2048,1024]{2,1,0:T(8,128)(2,1)S(1)}, bf16[1,2048,1024]{2,1,0:T(8,128)(2,1)}, u32[]{:S(2)}) copy-start(bf16[1,2048,1024]{2,1,0:T(8,128)(2,1)} %param.4) | copy-start | bytes 12582916
  10.3 2.0 %copy-start = (f32[2,2,128,2,1024]{4,2,3,1,0:T(8,128)}, f32[2,2,128,2,1024]{4,2,3,1,0:T(8,128)S(1)}, u32[]{:S(2)}) copy-start(f32[2,2,128,2,1024]{4,2,3,1,0:T(8,128)S(1)} %fusion) | copy-start | bytes 12582916
  12.3 6.2 %collective-permute-start = (f32[2,128,2,1024]{3,1,2,0:T(8,128)S(1)}, f32[2,128,2,1024]{3,1,2,0:T(8,128)}, u32[]{:S(2)}, u32[]{:S(2)}) collective-permute-start(f32[2,128,2,1024]{3,1,2,0:T(8,128)S(1)} %dynamic-slice_bitcast_fusion), channel_id=1, source_target_pairs={{0,1},{1,0},{2,3},{3,2},{4,5},{5,4},{6,7},{7,6},{8,9},{9,8},{10,11... | collective-permute-start | bytes 6291464 | tf_op jit(solution)/shard_map/ppermute | solution.py:60
  21.1 5.2 %copy-start.1 = (s32[1024]{0:T(1024)S(1)}, s32[1024]{0:T(1024)}, u32[]{:S(2)}) copy-start(s32[1024]{0:T(1024)} %param.5) | copy-start | bytes 12292
  21.2 28.7 %collective-permute-start.1 = (f32[128,2,1024]{2,0,1:T(8,128)S(1)}, f32[128,2,1024]{2,0,1:T(8,128)}, u32[]{:S(2)}, u32[]{:S(2)}) collective-permute-start(f32[128,2,1024]{2,0,1:T(8,128)S(1)} %dynamic-slice_bitcast_fusion.1), channel_id=1, source_target_pairs={{0,2},{2,0},{1,3},{3,1},{4,6},{6,4},{5,7},{7,5},{8,10},{10,8},{9,1... | collective-permute-start | bytes 3145736 | tf_op jit(solution)/shard_map/ppermute | solution.py:63
  51.4 4.4 %collective-permute-start.3 = (f32[32,1024]{1,0:T(8,128)S(1)}, f32[32,1024]{1,0:T(8,128)S(1)}, u32[]{:S(2)}, u32[]{:S(2)}) collective-permute-start(f32[32,1024]{1,0:T(8,128)S(1)} %get-tuple-element.14), channel_id=1, source_target_pairs={{1,0},{2,1},{3,2},{5,4},{6,5},{7,6},{9,8},{10,9},{11,10},{13,12},{... | collective-permute-start | bytes 393224 | tf_op jit(solution)/shard_map/ppermute | solution.py:25
  52.7 4.0 %collective-permute-start.2 = (f32[32,1024]{1,0:T(8,128)S(1)}, f32[32,1024]{1,0:T(8,128)S(1)}, u32[]{:S(2)}, u32[]{:S(2)}) collective-permute-start(f32[32,1024]{1,0:T(8,128)S(1)} %get-tuple-element.13), channel_id=1, source_target_pairs={{0,1},{1,2},{2,3},{4,5},{5,6},{6,7},{8,9},{9,10},{10,11},{12,13},{... | collective-permute-start | bytes 393224 | tf_op jit(solution)/shard_map/ppermute | solution.py:23
  118.4 14.5 %copy-start.2 = (s32[8]{0:T(128)S(1)}, s32[8]{0:T(128)}, u32[]{:S(2)}) copy-start(s32[8]{0:T(128)} %param.7) | copy-start | bytes 100
  118.4 14.5 %copy-start.3 = (s32[8]{0:T(128)S(1)}, s32[8]{0:T(128)}, u32[]{:S(2)}) copy-start(s32[8]{0:T(128)} %param.6) | copy-start | bytes 100
  124.5 46.1 %all-to-all-start.1 = ((bf16[128,2,1032]{2,1,0:T(2,128)(2,1)}), bf16[128,2,1032]{2,1,0:T(2,128)(2,1)S(1)}, u32[]{:S(2)}, u32[]{:S(2)}) async-start(bf16[128,2,1032]{2,1,0:T(2,128)(2,1)} %reshape.380), calls=%async_computation.1 | async-start | bytes 1179648 | tf_op jit(solution)/shard_map/all_to_all | solution.py:135

commit v5 on v4

--- a/solution.py
+++ b/solution.py
@@ -73,14 +73,8 @@
     )
 
 
-def whiten_local(records, quality):
-    local_record = records[0]
-    quarter = local_record.shape[0]
+def whiten_local(local_record, basis_table, quality):
     channels = local_record.shape[1]
-    parts = lax.axis_size("af")
-    band_rows = BINS // parts
-    sample_index = lax.axis_index("af") * quarter + jnp.arange(quarter, dtype=jnp.int32)
-    basis_table = taper_table(LOWBIN, sample_index, SEGLEN).reshape(2 * BINS, quarter)
     spectra = reduce_scatter_af(
         jnp.dot(basis_table, local_record, preferred_element_type=jnp.float32).reshape(
             BINS, 2, channels
@@ -93,6 +87,17 @@
         smoothed * (1.0 / (2 * SMOOTH + 1)) + 1e-06
     )
     return (spectra * factor[:, None, :]).astype(jnp.bfloat16)
+
+
+def to_bins(whitened):
+    band_rows, _, channels = whitened.shape
+    return lax.all_to_all(
+        whitened.reshape(band_rows, 1, 2, channels),
+        "ch",
+        split_axis=0,
+        concat_axis=1,
+        tiled=True,
+    )[0]
 
 
 def bin_cross(whitened, block, slab_width):
@@ -119,17 +124,25 @@
 
 
 def per_device(records, quality, band_low, band_high):
-    whitened = whiten_local(records, quality)
-    band_rows, _, channels = whitened.shape
+    local_record = records[0]
+    quarter, channels = local_record.shape
+    sample_index = lax.axis_index("af") * quarter + jnp.arange(quarter, dtype=jnp.int32)
+    basis_table = taper_table(LOWBIN, sample_index, SEGLEN).reshape(2 * BINS, quarter)
+    chunks = 2
+    width = channels // chunks
+    pieces = []
+    whitened = None
+    for chunk in range(chunks):
+        part = slice(chunk * width, (chunk + 1) * width)
+        chunk_record = local_record[:, part]
+        if whitened is not None:
+            whitened, chunk_record = lax.optimization_barrier((whitened, chunk_record))
+            pieces.append(to_bins(whitened))
+        whitened = whiten_local(chunk_record, basis_table, quality[part])
+    pieces.append(to_bins(whitened))
+    by_bin = jnp.concatenate(pieces, axis=2)
     slab_count = lax.axis_size("ch")
     slab_width = channels // slab_count
-    by_bin = lax.all_to_all(
-        whitened.reshape(band_rows, 1, 2, channels),
-        "ch",
-        split_axis=0,
-        concat_axis=1,
-        tiled=True,
-    )[0]
     segments = by_bin.shape[0]
     rows = bin_cross(by_bin, REACH, slab_width)
     back = lax.all_to_all(rows, "ch", split_axis=0, concat_axis=0, tiled=True)

time: 175 us -> 188 us (1.074)
  blocking collectives: 52.3 us -> 0 us
  starting transfers between devices: 19.8 us -> 59 us
  waiting for transfers between devices: 66.2 us -> 90.4 us
  local copies, waits for them, and re-layouts: 17.1 us -> 19.1 us
    all_to_all x1 -> x0, blocking collectives: 52.3 us -> none  [per_device(): lax.all_to_all(whitened.reshape(band_rows, 1, 2, channels), 'ch', split_a...]
    all_to_all x0 -> x2, waiting for transfers between devices: none -> 37.5 us  [to_bins(): lax.all_to_all(whitened.reshape(band_rows, 1, 2, channels), 'ch', split_a...]
    all_to_all x0 -> x2, starting transfers between devices: none -> 25.8 us  [to_bins(): lax.all_to_all(whitened.reshape(band_rows, 1, 2, channels), 'ch', split_a...]
    ppermute x1 -> x2, waiting for transfers between devices: 23.6 us -> 10.8 us  [reduce_scatter_af(): return keep + lax.ppermute(send, 'af', [(0, 2), (2, 0), (1, 3), (3, 1)])]
    ppermute x1 -> x2, starting transfers between devices: 5.1 us -> 11.1 us  [reduce_scatter_af(): return keep + lax.ppermute(send, 'af', [(0, 2), (2, 0), (1, 3), (3, 1)])]
    ppermute x1 -> x2, starting transfers between devices: 1.91 us -> 7.07 us  [reduce_scatter_af(): half = keep + lax.ppermute(send, 'af', [(0, 1), (1, 0), (2, 3), (3, 2)])]
    ppermute x1 -> x2, starting transfers between devices: 3.04 us -> 6.07 us  [extended(): lax.ppermute(tail, axis, [(i, (i + 1) % count) for i in range(ends)])]
    all_to_all x1, starting transfers between devices: 8.44 us -> 6.21 us  [per_device(): back = lax.all_to_all(rows, 'ch', split_axis=0, concat_axis=0, tiled=True)]
  transfers between devices with their start and end apart: 5 -> 11, of which waited for: 4 -> 8; matrix products, arithmetic and copies ran while one was open for 0% -> 2% of each run, Pallas kernels for 0% -> 0%
where the time goes in v5:
time: 188 us
  waiting for transfers between devices  90.4 us (48%)
  starting transfers between devices  59 us (31%)
  local copies, waits for them, and re-layouts  19.1 us (10%)
  other arithmetic  12.7 us (7%)
  matrix products  5.77 us (3%)
    all_to_all x2, waiting for transfers between devices, to_bins(): lax.all_to_all(whitened.reshape(band_rows, 1, 2, channels), 'ch', split_a...  37.5 us
    all_to_all x1, waiting for transfers between devices, per_device(): back = lax.all_to_all(rows, 'ch', split_axis=0, concat_axis=0, tiled=True)  35.5 us
    all_to_all x2, starting transfers between devices, to_bins(): lax.all_to_all(whitened.reshape(band_rows, 1, 2, channels), 'ch', split_a...  25.8 us
    ppermute x2, starting transfers between devices, reduce_scatter_af(): return keep + lax.ppermute(send, 'af', [(0, 2), (2, 0), (1, 3), (3, 1)])  11.1 us
    ppermute x2, waiting for transfers between devices, reduce_scatter_af(): return keep + lax.ppermute(send, 'af', [(0, 2), (2, 0), (1, 3), (3, 1)])  10.8 us
    ppermute x2, starting transfers between devices, reduce_scatter_af(): half = keep + lax.ppermute(send, 'af', [(0, 1), (1, 0), (2, 3), (3, 2)])  7.07 us
    all_to_all x1, starting transfers between devices, per_device(): back = lax.all_to_all(rows, 'ch', split_axis=0, concat_axis=0, tiled=True)  6.21 us
    ppermute x2, starting transfers between devices, extended(): lax.ppermute(tail, axis, [(i, (i + 1) % count) for i in range(ends)])  6.07 us
  transfers between devices with their start and end apart: 11, of which 8 were waited for; matrix products, arithmetic and copies ran while one was open for 2% of the time, Pallas kernels for 0%

profile of v5, /device:TPU:6, one launch (start us, length us, event | category | flops | bytes accessed | tf_op | source)
XLA Modules:
  0.0 187.5 jit_solution(5066839314433552216)
XLA Ops:
  0.1 2.0 %fusion.42 = (f32[64,2048]{1,0:T(8,128)S(1)}, f32[64,2048]{1,0:T(8,128)S(1)}) fusion(s32[2048]{0:T(1024)S(1)} %iota_add_fusion), kind=kLoop, calls=%fused_computation.74 | loop fusion | flops 1835008 | bytes 1056768 | tf_op jit(solution)/shard_map/cos | solution.py:42
  2.1 0.3 fusion.52
  2.5 1.2 multiply_subtract_fusion
  3.7 1.2 multiply_convert_fusion
  4.9 1.0 copy-done.4
  5.9 2.3 %fusion.1 = f32[2,2,128,2,512]{4,2,3,1,0:T(8,128)S(1)} fusion(bf16[2,2,128,1,2048]{4,2,3,1,0:T(8,128)(2,1)S(1)} %get-tuple-element.22, bf16[2,2,128,1,2048]{4,2,3,1,0:T(8,128)(2,1)S(1)} %get-tuple-element.21, bf16[2048,1024]{1,0:T(8,128)(2,1)S(1)} %bitcast.78), kind=kOutput, calls=%fused_computation.6 | convolution fusion | flops 2149580800 | bytes 8388608 | tf_op jit(solution)/shard_map/dot_general | solution.py:79
  8.3 0.1 dynamic-slice_bitcast_fusion.1
  8.3 1.9 %collective-permute-start = (f32[2,128,2,512]{3,1,2,0:T(8,128)S(1)}, f32[2,128,2,512]{3,1,2,0:T(8,128)}, u32[]{:S(2)}, u32[]{:S(2)}) collective-permute-start(f32[2,128,2,512]{3,1,2,0:T(8,128)S(1)} %dynamic-slice_bitcast_fusion.1), channel_id=1, source_target_pairs={{0,1},{1,0},{2,3},{3,2},{4,5},{5,4},{6,7},{7,6},{8,9},{9,8},{10,11... | collective-permute-start | bytes 3145736 | tf_op jit(solution)/shard_map/ppermute | solution.py:60
  10.3 2.7 %collective-permute-done = f32[2,128,2,512]{3,1,2,0:T(8,128)} collective-permute-done((f32[2,128,2,512]{3,1,2,0:T(8,128)S(1)}, f32[2,128,2,512]{3,1,2,0:T(8,128)}, u32[]{:S(2)}, u32[]{:S(2)}) %collective-permute-start) | collective-permute-done | bytes 1048608 | tf_op jit(solution)/shard_map/ppermute | solution.py:60
  13.0 1.4 bitcast_add_fusion.1
  14.5 0.8 dynamic-slice_bitcast_fusion.3
  15.3 5.1 %collective-permute-start.1 = (f32[128,2,512]{2,0,1:T(8,128)}, f32[128,2,512]{2,0,1:T(8,128)}, u32[]{:S(2)}, u32[]{:S(2)}) collective-permute-start(f32[128,2,512]{2,0,1:T(8,128)} %dynamic-slice_bitcast_fusion.3), channel_id=1, source_target_pairs={{0,2},{2,0},{1,3},{3,1},{4,6},{6,4},{5,7},{7,5},{8,10},{10,8},{9,1... | collective-permute-start | bytes 1572872 | tf_op jit(solution)/shard_map/ppermute | solution.py:63
  20.4 1.7 slice.93
  22.2 10.8 %collective-permute-done.1 = f32[128,2,512]{2,0,1:T(8,128)} collective-permute-done((f32[128,2,512]{2,0,1:T(8,128)}, f32[128,2,512]{2,0,1:T(8,128)}, u32[]{:S(2)}, u32[]{:S(2)}) %collective-permute-start.1) | collective-permute-done | bytes 524320 | tf_op jit(solution)/shard_map/ppermute | solution.py:63
  33.0 1.3 bitcast_add_fusion.3
  34.3 1.4 collective-permute-start.3
  35.8 3.0 %collective-permute-start.2 = (f32[32,512]{1,0:T(8,128)S(1)}, f32[32,512]{1,0:T(8,128)S(1)}, u32[]{:S(2)}, u32[]{:S(2)}) collective-permute-start(f32[32,512]{1,0:T(8,128)S(1)} %get-tuple-element.17), channel_id=1, source_target_pairs={{0,1},{1,2},{2,3},{4,5},{5,6},{6,7},{8,9},{9,10},{10,11},{12,13},{... | collective-permute-start | bytes 196616 | tf_op jit(solution)/shard_map/ppermute | solution.py:23
  38.9 0.8 collective-permute-done.2
  39.7 0.3 fusion.9
  40.0 0.1 multiply_convert_fusion.2
  40.1 2.3 %fusion = f32[2,2,128,2,512]{4,2,3,1,0:T(8,128)S(1)} fusion(bf16[2,2,128,1,2048]{4,2,3,1,0:T(8,128)(2,1)S(1)} %copy-done.3, bf16[2,2,128,1,2048]{4,2,3,1,0:T(8,128)(2,1)S(1)} %copy-done.1, bf16[2048,512]{1,0:T(8,128)(2,1)S(1)} %slice.93), kind=kOutput, calls=%fused_computation.5 | convolution fusion | flops 2149580800 | bytes 8388608 | tf_op jit(solution)/shard_map/dot_general | solution.py:79
  42.4 0.1 dynamic-slice_bitcast_fusion
  42.5 5.1 %collective-permute-start.4 = (f32[2,128,2,512]{3,1,2,0:T(8,128)S(1)}, f32[2,128,2,512]{3,1,2,0:T(8,128)S(1)}, u32[]{:S(2)}, u32[]{:S(2)}) collective-permute-start(f32[2,128,2,512]{3,1,2,0:T(8,128)S(1)} %dynamic-slice_bitcast_fusion), channel_id=1, source_target_pairs={{0,1},{1,0},{2,3},{3,2},{4,5},{5,4},{6,7},{7,6},{8,9},{9,8},{10,11... | collective-permute-start | bytes 3145736 | tf_op jit(solution)/shard_map/ppermute | solution.py:60
  47.7 2.3 %collective-permute-done.4 = f32[2,128,2,512]{3,1,2,0:T(8,128)S(1)} collective-permute-done((f32[2,128,2,512]{3,1,2,0:T(8,128)S(1)}, f32[2,128,2,512]{3,1,2,0:T(8,128)S(1)}, u32[]{:S(2)}, u32[]{:S(2)}) %collective-permute-start.4) | collective-permute-done | bytes 1048608 | tf_op jit(solution)/shard_map/ppermute | solution.py:60
  50.0 0.2 bitcast_add_fusion
  50.2 6.0 %collective-permute-start.5 = (f32[128,2,512]{2,0,1:T(8,128)S(1)}, f32[128,2,512]{2,0,1:T(8,128)S(1)}, u32[]{:S(2)}, u32[]{:S(2)}) collective-permute-start(f32[128,2,512]{2,0,1:T(8,128)S(1)} %dynamic-slice_bitcast_fusion.2), channel_id=1, source_target_pairs={{0,2},{2,0},{1,3},{3,1},{4,6},{6,4},{5,7},{7,5},{8,10},{10,8},{9,1... | collective-permute-start | bytes 1572872 | tf_op jit(solution)/shard_map/ppermute | solution.py:63
  56.3 1.0 copy.29
  57.3 19.6 %all-to-all-start = ((bf16[128,1,2,512]{3,2,1,0:T(2,128)(2,1)}), bf16[128,1,2,512]{3,2,1,0:T(2,128)(2,1)S(1)}, u32[]{:S(2)}, u32[]{:S(2)}) async-start(bf16[128,1,2,512]{3,2,1,0:T(2,128)(2,1)} %copy.29), calls=%async_computation | async-start | bytes 524288 | tf_op jit(solution)/shard_map/all_to_all | solution.py:94
  76.9 0.1 bitcast_add_fusion.2
  77.0 1.3 collective-permute-start.7
  78.3 3.0 %collective-permute-start.6 = (f32[32,512]{1,0:T(8,128)S(1)}, f32[32,512]{1,0:T(8,128)S(1)}, u32[]{:S(2)}, u32[]{:S(2)}) collective-permute-start(f32[32,512]{1,0:T(8,128)S(1)} %get-tuple-element.15), channel_id=1, source_target_pairs={{0,1},{1,2},{2,3},{4,5},{5,6},{6,7},{8,9},{9,10},{10,11},{12,13},{... | collective-permute-start | bytes 196616 | tf_op jit(solution)/shard_map/ppermute | solution.py:23
  81.4 0.8 collective-permute-done.6
  82.3 0.3 fusion.10
  82.6 0.1 fusion.37
  82.7 1.0 copy.31
  83.6 15.9 %all-to-all-done = bf16[128,1,2,512]{3,2,1,0:T(2,128)(2,1)S(1)} async-done(((bf16[128,1,2,512]{3,2,1,0:T(2,128)(2,1)}), bf16[128,1,2,512]{3,2,1,0:T(2,128)(2,1)S(1)}, u32[]{:S(2)}, u32[]{:S(2)}) %all-to-all-start) | async-done | bytes 262176 | tf_op jit(solution)/shard_map/all_to_all | solution.py:94
  99.6 6.2 %all-to-all-start.1 = ((bf16[128,1,2,512]{3,2,1,0:T(2,128)(2,1)}), bf16[128,1,2,512]{3,2,1,0:T(2,128)(2,1)S(1)}, u32[]{:S(2)}, u32[]{:S(2)}) async-start(bf16[128,1,2,512]{3,2,1,0:T(2,128)(2,1)} %copy.31), calls=%async_computation.1 | async-start | bytes 524288 | tf_op jit(solution)/shard_map/all_to_all | solution.py:94
  105.8 0.2 copy.30
  106.0 21.6 %all-to-all-done.1 = bf16[128,1,2,512]{3,2,1,0:T(2,128)(2,1)S(1)} async-done(((bf16[128,1,2,512]{3,2,1,0:T(2,128)(2,1)}), bf16[128,1,2,512]{3,2,1,0:T(2,128)(2,1)S(1)}, u32[]{:S(2)}, u32[]{:S(2)}) %all-to-all-start.1) | async-done | bytes 262176 | tf_op jit(solution)/shard_map/all_to_all | solution.py:94
  127.6 0.2 copy.32
  127.9 0.1 fusion.20
  128.0 0.1 fusion.60
  128.1 0.3 copy.47
  128.4 0.3 copy.46
  128.7 0.4 convolution_convert_fusion
  129.1 0.3 reshape.390
  129.4 0.6 copy.35
  130.0 0.1 pad.9
  130.1 2.9 %reshape.391 = bf16[8,2,128,257]{3,2,0,1:T(8,128)(2,1)S(1)} reshape(bf16[8,2,32896]{2,0,1:T(8,128)(2,1)S(1)} %pad.9) | data formatting | bytes 2105344 | tf_op jit(solution)/shard_map/reshape | solution.py:120
  133.0 0.1 slice.102
  133.1 1.1 reshape.397
  134.1 0.6 copy.37
  134.8 0.7 all_to_all.24
  135.5 0.5 broadcast.297
  136.0 4.1 %reduce = bf16[128,2064]{1,0:T(8,128)(2,1)S(1)} reduce(bf16[128,1,2064]{2,1,0:T(2,128)(2,1)S(1)} %all_to_all.24, bf16[]{:T(256)} %broadcast.297), dimensions={1}, to_apply=%all_to_all.24.reduce_sub_computation | reduce | bytes 1056770 | tf_op jit(solution)/shard_map/all_to_all | solution.py:148
  140.1 1.4 reshape.398
  141.5 6.2 %all-to-all-start.2 = ((bf16[128,2,1032]{2,1,0:T(2,128)(2,1)}), bf16[128,2,1032]{2,1,0:T(2,128)(2,1)S(1)}, u32[]{:S(2)}, u32[]{:S(2)}) async-start(bf16[128,2,1032]{2,1,0:T(2,128)(2,1)} %reshape.398), calls=%async_computation.2 | async-start | bytes 1179648 | tf_op jit(solution)/shard_map/all_to_all | solution.py:148
  147.7 0.1 fusion.54
  147.8 35.5 %all-to-all-done.2 = bf16[128,2,1032]{2,1,0:T(2,128)(2,1)S(1)} async-done(((bf16[128,2,1032]{2,1,0:T(2,128)(2,1)}), bf16[128,2,1032]{2,1,0:T(2,128)(2,1)S(1)}, u32[]{:S(2)}, u32[]{:S(2)}) %all-to-all-start.2) | async-done | bytes 528416 | tf_op jit(solution)/shard_map/all_to_all | solution.py:148
  183.3 0.6 reshape.399
  183.9 1.5 copy.39
  185.4 0.1 reshape.393
  185.5 0.2 multiply_bitcast_fusion
  185.8 1.8 copy.40
  (32 shorter events, 0.4 us)
Async XLA Ops:
  3.7 2.2 %copy-start.4 = (bf16[1,2048,1024]{2,1,0:T(8,128)(2,1)S(1)}, bf16[1,2048,1024]{2,1,0:T(8,128)(2,1)}, u32[]{:S(2)}) copy-start(bf16[1,2048,1024]{2,1,0:T(8,128)(2,1)} %param.4) | copy-start | bytes 12582916
  4.9 3.4 %copy-start = (bf16[2,2,128,1,2048]{4,2,3,1,0:T(8,128)(2,1)}, bf16[2,2,128,1,2048]{4,2,3,1,0:T(8,128)(2,1)S(1)}, u32[]{:S(2)}) copy-start(bf16[2,2,128,1,2048]{4,2,3,1,0:T(8,128)(2,1)S(1)} %get-tuple-element.21) | copy-start | bytes 6291460
  4.9 3.4 %copy-start.2 = (bf16[2,2,128,1,2048]{4,2,3,1,0:T(8,128)(2,1)}, bf16[2,2,128,1,2048]{4,2,3,1,0:T(8,128)(2,1)S(1)}, u32[]{:S(2)}) copy-start(bf16[2,2,128,1,2048]{4,2,3,1,0:T(8,128)(2,1)S(1)} %get-tuple-element.22) | copy-start | bytes 6291460
  8.3 4.7 %collective-permute-start = (f32[2,128,2,512]{3,1,2,0:T(8,128)S(1)}, f32[2,128,2,512]{3,1,2,0:T(8,128)}, u32[]{:S(2)}, u32[]{:S(2)}) collective-permute-start(f32[2,128,2,512]{3,1,2,0:T(8,128)S(1)} %dynamic-slice_bitcast_fusion.1), channel_id=1, source_target_pairs={{0,1},{1,0},{2,3},{3,2},{4,5},{5,4},{6,7},{7,6},{8,9},{9,8},{10,11... | collective-permute-start | bytes 3145736 | tf_op jit(solution)/shard_map/ppermute | solution.py:60
  15.3 17.7 %collective-permute-start.1 = (f32[128,2,512]{2,0,1:T(8,128)}, f32[128,2,512]{2,0,1:T(8,128)}, u32[]{:S(2)}, u32[]{:S(2)}) collective-permute-start(f32[128,2,512]{2,0,1:T(8,128)} %dynamic-slice_bitcast_fusion.3), channel_id=1, source_target_pairs={{0,2},{2,0},{1,3},{3,1},{4,6},{6,4},{5,7},{7,5},{8,10},{10,8},{9,1... | collective-permute-start | bytes 1572872 | tf_op jit(solution)/shard_map/ppermute | solution.py:63
  20.4 1.8 copy-start.5
  33.0 7.1 %copy-start.3 = (bf16[2,2,128,1,2048]{4,2,3,1,0:T(8,128)(2,1)S(1)}, bf16[2,2,128,1,2048]{4,2,3,1,0:T(8,128)(2,1)}, u32[]{:S(2)}) copy-start(bf16[2,2,128,1,2048]{4,2,3,1,0:T(8,128)(2,1)} %copy-done.2) | copy-start | bytes 6291460
  34.2 5.9 %copy-start.1 = (bf16[2,2,128,1,2048]{4,2,3,1,0:T(8,128)(2,1)S(1)}, bf16[2,2,128,1,2048]{4,2,3,1,0:T(8,128)(2,1)}, u32[]{:S(2)}) copy-start(bf16[2,2,128,1,2048]{4,2,3,1,0:T(8,128)(2,1)} %copy-done) | copy-start | bytes 6291460
  34.3 4.5 %collective-permute-start.3 = (f32[32,512]{1,0:T(8,128)S(1)}, f32[32,512]{1,0:T(8,128)S(1)}, u32[]{:S(2)}, u32[]{:S(2)}) collective-permute-start(f32[32,512]{1,0:T(8,128)S(1)} %get-tuple-element.18), channel_id=1, source_target_pairs={{1,0},{2,1},{3,2},{5,4},{6,5},{7,6},{9,8},{10,9},{11,10},{13,12},{... | collective-permute-start | bytes 196616 | tf_op jit(solution)/shard_map/ppermute | solution.py:25
  35.8 3.9 %collective-permute-start.2 = (f32[32,512]{1,0:T(8,128)S(1)}, f32[32,512]{1,0:T(8,128)S(1)}, u32[]{:S(2)}, u32[]{:S(2)}) collective-permute-start(f32[32,512]{1,0:T(8,128)S(1)} %get-tuple-element.17), channel_id=1, source_target_pairs={{0,1},{1,2},{2,3},{4,5},{5,6},{6,7},{8,9},{9,10},{10,11},{12,13},{... | collective-permute-start | bytes 196616 | tf_op jit(solution)/shard_map/ppermute | solution.py:23
  42.5 7.4 %collective-permute-start.4 = (f32[2,128,2,512]{3,1,2,0:T(8,128)S(1)}, f32[2,128,2,512]{3,1,2,0:T(8,128)S(1)}, u32[]{:S(2)}, u32[]{:S(2)}) collective-permute-start(f32[2,128,2,512]{3,1,2,0:T(8,128)S(1)} %dynamic-slice_bitcast_fusion), channel_id=1, source_target_pairs={{0,1},{1,0},{2,3},{3,2},{4,5},{5,4},{6,7},{7,6},{8,9},{9,8},{10,11... | collective-permute-start | bytes 3145736 | tf_op jit(solution)/shard_map/ppermute | solution.py:60
  50.2 26.6 %collective-permute-start.5 = (f32[128,2,512]{2,0,1:T(8,128)S(1)}, f32[128,2,512]{2,0,1:T(8,128)S(1)}, u32[]{:S(2)}, u32[]{:S(2)}) collective-permute-start(f32[128,2,512]{2,0,1:T(8,128)S(1)} %dynamic-slice_bitcast_fusion.2), channel_id=1, source_target_pairs={{0,2},{2,0},{1,3},{3,1},{4,6},{6,4},{5,7},{7,5},{8,10},{10,8},{9,1... | collective-permute-start | bytes 1572872 | tf_op jit(solution)/shard_map/ppermute | solution.py:63
  57.3 42.3 %all-to-all-start = ((bf16[128,1,2,512]{3,2,1,0:T(2,128)(2,1)}), bf16[128,1,2,512]{3,2,1,0:T(2,128)(2,1)S(1)}, u32[]{:S(2)}, u32[]{:S(2)}) async-start(bf16[128,1,2,512]{3,2,1,0:T(2,128)(2,1)} %copy.29), calls=%async_computation | async-start | bytes 524288 | tf_op jit(solution)/shard_map/all_to_all | solution.py:94
  77.0 4.4 %collective-permute-start.7 = (f32[32,512]{1,0:T(8,128)S(1)}, f32[32,512]{1,0:T(8,128)S(1)}, u32[]{:S(2)}, u32[]{:S(2)}) collective-permute-start(f32[32,512]{1,0:T(8,128)S(1)} %get-tuple-element.16), channel_id=1, source_target_pairs={{1,0},{2,1},{3,2},{5,4},{6,5},{7,6},{9,8},{10,9},{11,10},{13,12},{... | collective-permute-start | bytes 196616 | tf_op jit(solution)/shard_map/ppermute | solution.py:25
  78.3 3.9 %collective-permute-start.6 = (f32[32,512]{1,0:T(8,128)S(1)}, f32[32,512]{1,0:T(8,128)S(1)}, u32[]{:S(2)}, u32[]{:S(2)}) collective-permute-start(f32[32,512]{1,0:T(8,128)S(1)} %get-tuple-element.15), channel_id=1, source_target_pairs={{0,1},{1,2},{2,3},{4,5},{5,6},{6,7},{8,9},{9,10},{10,11},{12,13},{... | collective-permute-start | bytes 196616 | tf_op jit(solution)/shard_map/ppermute | solution.py:23
  99.6 28.0 %all-to-all-start.1 = ((bf16[128,1,2,512]{3,2,1,0:T(2,128)(2,1)}), bf16[128,1,2,512]{3,2,1,0:T(2,128)(2,1)S(1)}, u32[]{:S(2)}, u32[]{:S(2)}) async-start(bf16[128,1,2,512]{3,2,1,0:T(2,128)(2,1)} %copy.31), calls=%async_computation.1 | async-start | bytes 524288 | tf_op jit(solution)/shard_map/all_to_all | solution.py:94
  135.4 12.3 %copy-start.6 = (s32[8]{0:T(128)S(1)}, s32[8]{0:T(128)}, u32[]{:S(2)}) copy-start(s32[8]{0:T(128)} %param.7) | copy-start | bytes 100
  135.4 12.3 %copy-start.7 = (s32[8]{0:T(128)S(1)}, s32[8]{0:T(128)}, u32[]{:S(2)}) copy-start(s32[8]{0:T(128)} %param.6) | copy-start | bytes 100
  141.5 41.8 %all-to-all-start.2 = ((bf16[128,2,1032]{2,1,0:T(2,128)(2,1)}), bf16[128,2,1032]{2,1,0:T(2,128)(2,1)S(1)}, u32[]{:S(2)}, u32[]{:S(2)}) async-start(bf16[128,2,1032]{2,1,0:T(2,128)(2,1)} %reshape.398), calls=%async_computation.2 | async-start | bytes 1179648 | tf_op jit(solution)/shard_map/all_to_all | solution.py:148

commit v6 on v4

--- a/solution.py
+++ b/solution.py
@@ -115,7 +115,7 @@
     skew = flat.reshape(blocks, 2, block, width + 1)[:, :, :, : REACH + 1]
     slabs = block // slab_width
     rows = skew.reshape(blocks, 2, slabs, slab_width * (REACH + 1)).transpose(0, 2, 1, 3)
-    return rows.reshape(blocks * slabs, 2 * slab_width * (REACH + 1))
+    return rows.reshape(blocks * slabs, 2, slab_width * (REACH + 1))
 
 
 def per_device(records, quality, band_low, band_high):

time: 175 us -> 169 us (0.966); the launches traced: 175 us -> 167 us
  other arithmetic: 13.6 us -> 9.49 us
  waiting for transfers between devices: 66.2 us -> 69.5 us
  local copies, waits for them, and re-layouts: 17.1 us -> 14.1 us
  blocking collectives: 52.3 us -> 49.3 us
    ppermute x1, waiting for transfers between devices: 0.01 us -> 5.26 us  [extended(): lax.ppermute(head, axis, [((i + 1) % count, i) for i in range(ends)])]
    all_to_all x1 -> x0, other arithmetic: 4.13 us -> none  [per_device(): back = lax.all_to_all(rows, 'ch', split_axis=0, concat_axis=0, tiled=True)]
    all_to_all x1, blocking collectives: 52.3 us -> 49.3 us  [per_device(): lax.all_to_all(whitened.reshape(band_rows, 1, 2, channels), 'ch', split_a...]
    unnamed x14 -> x12, local copies, waits for them, and re-layouts: 5.37 us -> 3.35 us
where the time goes in v6:
time: 169 us; the launch traced here: 167 us
  waiting for transfers between devices  69.5 us (41%)
  blocking collectives  49.3 us (29%)
  starting transfers between devices  18.5 us (11%)
  local copies, waits for them, and re-layouts  14.1 us (8%)
  other arithmetic  9.49 us (6%)
  matrix products  5.44 us (3%)
    all_to_all x1, blocking collectives, per_device(): lax.all_to_all(whitened.reshape(band_rows, 1, 2, channels), 'ch', split_a...  49.3 us
    all_to_all x1, waiting for transfers between devices, per_device(): back = lax.all_to_all(rows, 'ch', split_axis=0, concat_axis=0, tiled=True)  36.5 us
    ppermute x1, waiting for transfers between devices, reduce_scatter_af(): return keep + lax.ppermute(send, 'af', [(0, 2), (2, 0), (1, 3), (3, 1)])  23.6 us
    all_to_all x1, starting transfers between devices, per_device(): back = lax.all_to_all(rows, 'ch', split_axis=0, concat_axis=0, tiled=True)  8.92 us
    ppermute x1, waiting for transfers between devices, extended(): lax.ppermute(head, axis, [((i + 1) % count, i) for i in range(ends)])  5.26 us
    ppermute x1, starting transfers between devices, reduce_scatter_af(): return keep + lax.ppermute(send, 'af', [(0, 2), (2, 0), (1, 3), (3, 1)])  5.1 us
    dot_general x1, matrix products, whiten_local(): jnp.dot(basis_table, local_record, preferred_element_type=jnp.float32)  4.48 us
    ppermute x1, waiting for transfers between devices, reduce_scatter_af(): half = keep + lax.ppermute(send, 'af', [(0, 1), (1, 0), (2, 3), (3, 2)])  4.23 us
  transfers between devices with their start and end apart: 5, of which 4 were waited for; matrix products, arithmetic and copies ran while one was open for 0% of the time, Pallas kernels for 0%

profile of v6, /device:TPU:6, one launch (start us, length us, event | category | flops | bytes accessed | tf_op | source)
XLA Modules:
  0.0 166.8 jit_solution(3562356340735539757)
XLA Ops:
  0.0 0.1 multiply_subtract_fusion.1
  0.1 2.0 %fusion.34 = (f32[64,2048]{1,0:T(8,128)S(1)}, f32[64,2048]{1,0:T(8,128)S(1)}) fusion(s32[2048]{0:T(1024)S(1)} %iota_add_fusion), kind=kLoop, calls=%fused_computation.53 | loop fusion | flops 1835008 | bytes 1056768 | tf_op jit(solution)/shard_map/cos | solution.py:42
  2.1 0.3 fusion.42
  2.5 1.2 multiply_subtract_fusion
  3.7 0.0 copy-start.4
  3.7 1.2 multiply_convert_fusion
  4.9 1.0 copy-done.4
  5.9 4.5 %fusion = f32[2,2,128,2,1024]{4,2,3,1,0:T(8,128)S(1)} fusion(bf16[2,2,128,1,2048]{4,2,3,1,0:T(8,128)(2,1)S(1)} %get-tuple-element.18, bf16[2,2,128,1,2048]{4,2,3,1,0:T(8,128)(2,1)S(1)} %get-tuple-element.17, bf16[1,2048,1024]{2,1,0:T(8,128)(2,1)S(1)} %copy-done.4), kind=kOutput, calls=%fused_computation | convolution fusion | flops 4297064448 | bytes 12582912 | tf_op jit(solution)/shard_map/dot_general | solution.py:85
  10.3 0.0 copy-start
  10.4 0.1 dynamic-slice_bitcast_fusion
  10.5 1.8 %copy-done = f32[2,2,128,2,1024]{4,2,3,1,0:T(8,128)} copy-done((f32[2,2,128,2,1024]{4,2,3,1,0:T(8,128)}, f32[2,2,128,2,1024]{4,2,3,1,0:T(8,128)S(1)}, u32[]{:S(2)}) %copy-start) | copy-done | bytes 4194328
  12.3 1.9 %collective-permute-start = (f32[2,128,2,1024]{3,1,2,0:T(8,128)S(1)}, f32[2,128,2,1024]{3,1,2,0:T(8,128)}, u32[]{:S(2)}, u32[]{:S(2)}) collective-permute-start(f32[2,128,2,1024]{3,1,2,0:T(8,128)S(1)} %dynamic-slice_bitcast_fusion), channel_id=1, source_target_pairs={{0,1},{1,0},{2,3},{3,2},{4,5},{5,4},{6,7},{7,6},{8,9},{9,8},{10,11... | collective-permute-start | bytes 6291464 | tf_op jit(solution)/shard_map/ppermute | solution.py:60
  14.3 4.2 %collective-permute-done = f32[2,128,2,1024]{3,1,2,0:T(8,128)} collective-permute-done((f32[2,128,2,1024]{3,1,2,0:T(8,128)S(1)}, f32[2,128,2,1024]{3,1,2,0:T(8,128)}, u32[]{:S(2)}, u32[]{:S(2)}) %collective-permute-start) | collective-permute-done | bytes 2097184 | tf_op jit(solution)/shard_map/ppermute | solution.py:60
  18.5 2.6 %bitcast_add_fusion = f32[2,128,2,1024]{3,1,2,0:T(8,128)S(1)} fusion(f32[2,128,2,1024]{3,1,2,0:T(8,128)} %collective-permute-done, f32[2,2,128,2,1024]{4,2,3,1,0:T(8,128)} %copy-done, s32[]{:T(128)S(6)} %select_n.54), kind=kLoop, calls=%fused_computation.9 | loop fusion | flops 524288 | bytes 6291460 | tf_op jit(solution)/shard_map/add | solution.py:60
  21.1 0.0 copy-start.1
  21.1 0.1 dynamic-slice_bitcast_fusion.1
  21.2 5.1 %collective-permute-start.1 = (f32[128,2,1024]{2,0,1:T(8,128)S(1)}, f32[128,2,1024]{2,0,1:T(8,128)}, u32[]{:S(2)}, u32[]{:S(2)}) collective-permute-start(f32[128,2,1024]{2,0,1:T(8,128)S(1)} %dynamic-slice_bitcast_fusion.1), channel_id=1, source_target_pairs={{0,2},{2,0},{1,3},{3,1},{4,6},{6,4},{5,7},{7,5},{8,10},{10,8},{9,1... | collective-permute-start | bytes 3145736 | tf_op jit(solution)/shard_map/ppermute | solution.py:63
  26.3 0.0 copy-done.1
  26.4 23.6 %collective-permute-done.1 = f32[128,2,1024]{2,0,1:T(8,128)} collective-permute-done((f32[128,2,1024]{2,0,1:T(8,128)S(1)}, f32[128,2,1024]{2,0,1:T(8,128)}, u32[]{:S(2)}, u32[]{:S(2)}) %collective-permute-start.1) | collective-permute-done | bytes 1048608 | tf_op jit(solution)/shard_map/ppermute | solution.py:63
  49.9 1.4 bitcast_add_fusion.1
  51.3 0.1 fusion.29
  51.4 1.3 collective-permute-start.2
  52.7 1.3 collective-permute-start.3
  54.0 0.1 fusion.49
  54.1 0.0 collective-permute-done.2
  54.1 5.3 %collective-permute-done.3 = f32[32,1024]{1,0:T(8,128)S(1)} collective-permute-done((f32[32,1024]{1,0:T(8,128)S(1)}, f32[32,1024]{1,0:T(8,128)S(1)}, u32[]{:S(2)}, u32[]{:S(2)}) %collective-permute-start.3) | collective-permute-done | bytes 131104 | tf_op jit(solution)/shard_map/ppermute | solution.py:25
  59.4 0.5 fusion.7
  59.9 0.1 fusion.28
  60.0 0.5 copy.36
  60.6 49.3 %all_to_all.14 = bf16[128,1,2,1024]{3,2,1,0:T(2,128)(2,1)S(1)} all-to-all(bf16[128,1,2,1024]{3,2,1,0:T(2,128)(2,1)S(1)} %copy.36), channel_id=1, replica_groups=mesh['ch'=128,'af'=4] {'ch'}, dimensions={0} | all-to-all | bytes 1048576 | tf_op jit(solution)/shard_map/all_to_all | solution.py:126
  109.9 0.5 copy.37
  110.4 0.1 slice_bitcast_fusion.3
  110.6 0.1 fusion.24
  110.6 0.1 fusion.48
  110.7 0.3 copy.50
  111.0 0.3 copy.51
  111.3 0.1 neg.20
  111.4 0.4 convolution_convert_fusion
  111.8 0.3 reshape.371
  112.1 0.6 copy.40
  112.7 0.1 pad.9
  112.8 2.9 %reshape.372 = bf16[8,2,128,257]{3,2,0,1:T(8,128)(2,1)S(1)} reshape(bf16[8,2,32896]{2,0,1:T(8,128)(2,1)S(1)} %pad.9) | data formatting | bytes 2105344 | tf_op jit(solution)/shard_map/reshape | solution.py:115
  115.7 0.1 slice.54
  115.8 0.0 copy-start.2
  115.8 0.0 copy-start.3
  115.8 1.1 reshape.378
  116.8 1.4 copy.43
  118.3 8.9 %all-to-all-start.1 = ((bf16[128,2,1032]{2,1,0:T(2,128)(2,1)}), bf16[128,2,1032]{2,1,0:T(2,128)(2,1)S(1)}, u32[]{:S(2)}, u32[]{:S(2)}) async-start(bf16[128,2,1032]{2,1,0:T(2,128)(2,1)} %copy.43), calls=%async_computation.1 | async-start | bytes 1179648 | tf_op jit(solution)/shard_map/all_to_all | solution.py:135
  127.2 0.0 copy-done.2
  127.2 0.0 copy-done.3
  127.2 0.1 fusion.44
  127.3 36.5 %all-to-all-done.1 = bf16[128,2,1032]{2,1,0:T(2,128)(2,1)S(1)} async-done(((bf16[128,2,1032]{2,1,0:T(2,128)(2,1)}), bf16[128,2,1032]{2,1,0:T(2,128)(2,1)S(1)}, u32[]{:S(2)}, u32[]{:S(2)}) %all-to-all-start.1) | async-done | bytes 528416 | tf_op jit(solution)/shard_map/all_to_all | solution.py:135
  163.7 0.9 copy.44
  164.6 0.1 reshape.375
  164.8 0.2 multiply_bitcast_fusion
  165.0 1.8 %copy.45 = f32[8,129,2,128]{3,2,1,0:T(2,128)} copy(f32[8,129,2,128]{3,1,0,2:T(8,128)S(1)} %multiply_bitcast_fusion) | data formatting | bytes 2113536 | tf_op jit(solution)/shard_map/mul | solution.py:142
  (5 shorter events, 0.0 us)
Async XLA Ops:
  3.7 2.2 %copy-start.4 = (bf16[1,2048,1024]{2,1,0:T(8,128)(2,1)S(1)}, bf16[1,2048,1024]{2,1,0:T(8,128)(2,1)}, u32[]{:S(2)}) copy-start(bf16[1,2048,1024]{2,1,0:T(8,128)(2,1)} %param.4) | copy-start | bytes 12582916
  10.3 2.0 %copy-start = (f32[2,2,128,2,1024]{4,2,3,1,0:T(8,128)}, f32[2,2,128,2,1024]{4,2,3,1,0:T(8,128)S(1)}, u32[]{:S(2)}) copy-start(f32[2,2,128,2,1024]{4,2,3,1,0:T(8,128)S(1)} %fusion) | copy-start | bytes 12582916
  12.3 6.2 %collective-permute-start = (f32[2,128,2,1024]{3,1,2,0:T(8,128)S(1)}, f32[2,128,2,1024]{3,1,2,0:T(8,128)}, u32[]{:S(2)}, u32[]{:S(2)}) collective-permute-start(f32[2,128,2,1024]{3,1,2,0:T(8,128)S(1)} %dynamic-slice_bitcast_fusion), channel_id=1, source_target_pairs={{0,1},{1,0},{2,3},{3,2},{4,5},{5,4},{6,7},{7,6},{8,9},{9,8},{10,11... | collective-permute-start | bytes 6291464 | tf_op jit(solution)/shard_map/ppermute | solution.py:60
  21.1 5.2 %copy-start.1 = (s32[1024]{0:T(1024)S(1)}, s32[1024]{0:T(1024)}, u32[]{:S(2)}) copy-start(s32[1024]{0:T(1024)} %param.5) | copy-start | bytes 12292
  21.2 28.7 %collective-permute-start.1 = (f32[128,2,1024]{2,0,1:T(8,128)S(1)}, f32[128,2,1024]{2,0,1:T(8,128)}, u32[]{:S(2)}, u32[]{:S(2)}) collective-permute-start(f32[128,2,1024]{2,0,1:T(8,128)S(1)} %dynamic-slice_bitcast_fusion.1), channel_id=1, source_target_pairs={{0,2},{2,0},{1,3},{3,1},{4,6},{6,4},{5,7},{7,5},{8,10},{10,8},{9,1... | collective-permute-start | bytes 3145736 | tf_op jit(solution)/shard_map/ppermute | solution.py:63
  51.4 2.7 %collective-permute-start.2 = (f32[32,1024]{1,0:T(8,128)S(1)}, f32[32,1024]{1,0:T(8,128)S(1)}, u32[]{:S(2)}, u32[]{:S(2)}) collective-permute-start(f32[32,1024]{1,0:T(8,128)S(1)} %get-tuple-element.13), channel_id=1, source_target_pairs={{0,1},{1,2},{2,3},{4,5},{5,6},{6,7},{8,9},{9,10},{10,11},{12,13},{... | collective-permute-start | bytes 393224 | tf_op jit(solution)/shard_map/ppermute | solution.py:23
  52.7 6.7 %collective-permute-start.3 = (f32[32,1024]{1,0:T(8,128)S(1)}, f32[32,1024]{1,0:T(8,128)S(1)}, u32[]{:S(2)}, u32[]{:S(2)}) collective-permute-start(f32[32,1024]{1,0:T(8,128)S(1)} %get-tuple-element.14), channel_id=1, source_target_pairs={{1,0},{2,1},{3,2},{5,4},{6,5},{7,6},{9,8},{10,9},{11,10},{13,12},{... | collective-permute-start | bytes 393224 | tf_op jit(solution)/shard_map/ppermute | solution.py:25
  115.8 11.4 %copy-start.2 = (s32[8]{0:T(128)S(1)}, s32[8]{0:T(128)}, u32[]{:S(2)}) copy-start(s32[8]{0:T(128)} %param.7) | copy-start | bytes 100
  115.8 11.4 %copy-start.3 = (s32[8]{0:T(128)S(1)}, s32[8]{0:T(128)}, u32[]{:S(2)}) copy-start(s32[8]{0:T(128)} %param.6) | copy-start | bytes 100
  118.3 45.5 %all-to-all-start.1 = ((bf16[128,2,1032]{2,1,0:T(2,128)(2,1)}), bf16[128,2,1032]{2,1,0:T(2,128)(2,1)S(1)}, u32[]{:S(2)}, u32[]{:S(2)}) async-start(bf16[128,2,1032]{2,1,0:T(2,128)(2,1)} %copy.43), calls=%async_computation.1 | async-start | bytes 1179648 | tf_op jit(solution)/shard_map/all_to_all | solution.py:135

commit v7 on v6

--- a/solution.py
+++ b/solution.py
@@ -29,38 +29,55 @@
     return cells
 
 
-def taper_table(bin_start, sample_index, length):
-    fine = 64
-    groups = 8
+def fine_rotation(sample_index, length, fine):
     step = 2.0 * math.pi / length
-    coarse_bins = bin_start + fine * jnp.arange(groups, dtype=jnp.int32)
     fine_bins = jnp.arange(fine, dtype=jnp.int32)
+    fine_angle = (fine_bins[:, None] * sample_index[None, :] % length).astype(jnp.float32) * step
+    tapers = 0.5 - 0.5 * jnp.cos(sample_index.astype(jnp.float32) * step)
+    return jnp.cos(fine_angle)[None], jnp.sin(fine_angle)[None], tapers
+
+
+def taper_table(coarse_bins, sample_index, length, fine_table):
+    cos_f, sin_f, tapers = fine_table
+    step = 2.0 * math.pi / length
     coarse_angle = (coarse_bins[:, None] * sample_index[None, :] % length).astype(jnp.float32) * step
-    fine_angle = (fine_bins[:, None] * sample_index[None, :] % length).astype(jnp.float32) * step
     cos_c = jnp.cos(coarse_angle)[:, None, :]
     sin_c = jnp.sin(coarse_angle)[:, None, :]
-    cos_f = jnp.cos(fine_angle)[None, :, :]
-    sin_f = jnp.sin(fine_angle)[None, :, :]
-    rows = groups * fine
+    rows = coarse_bins.shape[0] * cos_f.shape[1]
     cos_a = (cos_c * cos_f - sin_c * sin_f).reshape(rows, -1)
     sin_a = (sin_c * cos_f + cos_c * sin_f).reshape(rows, -1)
-    tapers = 0.5 - 0.5 * jnp.cos(sample_index.astype(jnp.float32) * step)
     real_row = (tapers[None, :] * cos_a).astype(jnp.bfloat16)
     imag_row = (-(tapers[None, :] * sin_a)).astype(jnp.bfloat16)
     return jnp.stack([real_row, imag_row], axis=1)
 
 
-def reduce_scatter_af(partial):
+def quarter_spectra(local_record, sample_index, quarter_index, fine_table):
+    fine = fine_table[0].shape[1]
+    rows = BINS // 4
+    coarse_bins = LOWBIN + quarter_index * rows + fine * jnp.arange(rows // fine, dtype=jnp.int32)
+    basis = taper_table(coarse_bins, sample_index, SEGLEN, fine_table).reshape(2 * rows, -1)
+    out = jnp.dot(basis, local_record, preferred_element_type=jnp.float32)
+    return out.reshape(rows, 2, local_record.shape[1])
+
+
+def reduced_spectra(local_record):
+    quarter = local_record.shape[0]
     index = lax.axis_index("af")
     core = index % 2
     chip = index // 2
-    quarters = partial.reshape(2, 2, partial.shape[0] // 4, *partial.shape[1:])
-    keep = lax.dynamic_index_in_dim(quarters, core, axis=1, keepdims=False)
-    send = lax.dynamic_index_in_dim(quarters, 1 - core, axis=1, keepdims=False)
-    half = keep + lax.ppermute(send, "af", [(0, 1), (1, 0), (2, 3), (3, 2)])
-    keep = lax.dynamic_index_in_dim(half, chip, axis=0, keepdims=False)
-    send = lax.dynamic_index_in_dim(half, 1 - chip, axis=0, keepdims=False)
-    return keep + lax.ppermute(send, "af", [(0, 2), (2, 0), (1, 3), (3, 1)])
+    sample_index = index * quarter + jnp.arange(quarter, dtype=jnp.int32)
+    fine_table = fine_rotation(sample_index, SEGLEN, 64)
+    cores = [(0, 1), (1, 0), (2, 3), (3, 2)]
+    chips = [(0, 2), (2, 0), (1, 3), (3, 1)]
+
+    def spectra_of(q_chip, q_core):
+        return quarter_spectra(local_record, sample_index, 2 * q_chip + q_core, fine_table)
+
+    first = lax.ppermute(spectra_of(1 - chip, 1 - core), "af", cores)
+    second = lax.ppermute(spectra_of(chip, 1 - core), "af", cores)
+    outgoing = spectra_of(1 - chip, core) + first
+    incoming = lax.ppermute(outgoing, "af", chips)
+    return (spectra_of(chip, core) + second) + incoming
 
 
 def band_sum(padded, half_width):
@@ -74,18 +91,7 @@
 
 
 def whiten_local(records, quality):
-    local_record = records[0]
-    quarter = local_record.shape[0]
-    channels = local_record.shape[1]
-    parts = lax.axis_size("af")
-    band_rows = BINS // parts
-    sample_index = lax.axis_index("af") * quarter + jnp.arange(quarter, dtype=jnp.int32)
-    basis_table = taper_table(LOWBIN, sample_index, SEGLEN).reshape(2 * BINS, quarter)
-    spectra = reduce_scatter_af(
-        jnp.dot(basis_table, local_record, preferred_element_type=jnp.float32).reshape(
-            BINS, 2, channels
-        )
-    )
+    spectra = reduced_spectra(records[0])
     power_bins = spectra[:, 0] * spectra[:, 0] + spectra[:, 1] * spectra[:, 1]
     padded = extended(power_bins, (("af", 0),), SMOOTH)
     smoothed = band_sum(padded, SMOOTH)

time: 169 us -> 162 us (0.959)
  waiting for transfers between devices: 69.5 us -> 65.1 us
  other arithmetic: 9.49 us -> 6.32 us
  starting transfers between devices: 18.5 us -> 21 us
  local copies, waits for them, and re-layouts: 14.1 us -> 12 us
    ppermute x2 -> x3, waiting for transfers between devices: 27.8 us -> 23.3 us  [the longest x1 23.3 us: reduced_spectra(): incoming = lax.ppermute(outgoing, 'af', chips)]
    add x4 -> x3, other arithmetic: 3.98 us -> 0.02 us  [the longest x2 0.01 us: quarter_spectra(): LOWBIN + quarter_index * rows]
    ppermute x2 -> x3, starting transfers between devices: 7.01 us -> 9.43 us  [the longest x1 5.1 us: reduced_spectra(): incoming = lax.ppermute(outgoing, 'af', chips)]
    unnamed x12 -> x10, local copies, waits for them, and re-layouts: 3.35 us -> 1.48 us
    dot_general x1 -> x4, matrix products: 4.48 us -> 5.09 us  [quarter_spectra(): out = jnp.dot(basis, local_record, preferred_element_type=jnp.float32)]
  transfers between devices with their start and end apart: 5 -> 6, of which waited for: 4 -> 3; matrix products, arithmetic and copies ran while one was open for 0% -> 2% of each run, Pallas kernels for 0% -> 0%
where the time goes in v7:
time: 162 us; the launch traced here: 160 us
  waiting for transfers between devices  65.1 us (40%)
  blocking collectives  49.5 us (31%)
  starting transfers between devices  21 us (13%)
  local copies, waits for them, and re-layouts  12 us (7%)
  other arithmetic  6.32 us (4%)
  matrix products  6.05 us (4%)
    all_to_all x1, blocking collectives, per_device(): lax.all_to_all(whitened.reshape(band_rows, 1, 2, channels), 'ch', split_a...  49.5 us
    all_to_all x1, waiting for transfers between devices, per_device(): back = lax.all_to_all(rows, 'ch', split_axis=0, concat_axis=0, tiled=True)  36.5 us
    ppermute x1, waiting for transfers between devices, reduced_spectra(): incoming = lax.ppermute(outgoing, 'af', chips)  23.3 us
    all_to_all x1, starting transfers between devices, per_device(): back = lax.all_to_all(rows, 'ch', split_axis=0, concat_axis=0, tiled=True)  8.93 us
    ppermute x1, waiting for transfers between devices, extended(): lax.ppermute(head, axis, [((i + 1) % count, i) for i in range(ends)])  5.28 us
    ppermute x1, starting transfers between devices, reduced_spectra(): incoming = lax.ppermute(outgoing, 'af', chips)  5.1 us
    dot_general x4, matrix products, quarter_spectra(): out = jnp.dot(basis, local_record, preferred_element_type=jnp.float32)  5.09 us
  transfers between devices with their start and end apart: 6, of which 3 were waited for; matrix products, arithmetic and copies ran while one was open for 2% of the time, Pallas kernels for 0%

profile of v7, /device:TPU:6, one launch (start us, length us, event | category | flops | bytes accessed | tf_op | source)
XLA Modules:
  0.0 160.3 jit_solution(8407909485479143081)
XLA Ops:
  0.0 0.1 multiply_subtract_fusion.4
  0.1 2.0 %fusion.70 = (f32[64,2048]{1,0:T(8,128)S(1)}, f32[64,2048]{1,0:T(8,128)S(1)}) fusion(s32[2048]{0:T(1024)S(1)} %iota_add_fusion), kind=kLoop, calls=%fused_computation.91 | loop fusion | flops 1835008 | bytes 1056768 | tf_op jit(solution)/shard_map/cos | solution.py:37
  2.2 1.1 fusion.93
  3.3 1.2 multiply_subtract_fusion.3
  4.5 0.0 copy-start
  4.5 1.3 fusion.54
  5.7 0.9 copy-done
  6.6 1.3 fusion
  7.9 1.9 %collective-permute-start.1 = (f32[128,2,1024]{2,0,1:T(8,128)S(1)}, f32[128,2,1024]{2,0,1:T(8,128)S(1)}, u32[]{:S(2)}, u32[]{:S(2)}) collective-permute-start(f32[128,2,1024]{2,0,1:T(8,128)S(1)} %fusion), channel_id=1, source_target_pairs={{0,1},{1,0},{2,3},{3,2},{4,5},{5,4},{6,7},{7,6},{8,9},{9,8},{10,11... | collective-permute-start | bytes 3145736 | tf_op jit(solution)/shard_map/ppermute | solution.py:76
  9.8 1.3 fusion.4
  11.1 2.4 %collective-permute-start = (f32[128,2,1024]{2,0,1:T(8,128)S(1)}, f32[128,2,1024]{2,0,1:T(8,128)S(1)}, u32[]{:S(2)}, u32[]{:S(2)}) collective-permute-start(f32[128,2,1024]{2,0,1:T(8,128)S(1)} %fusion.4), channel_id=1, source_target_pairs={{0,1},{1,0},{2,3},{3,2},{4,5},{5,4},{6,7},{7,6},{8,9},{9,8},{10,11... | collective-permute-start | bytes 3145736 | tf_op jit(solution)/shard_map/ppermute | solution.py:77
  13.5 0.0 collective-permute-done.1
  13.6 0.0 copy-start.1
  13.6 1.3 fusion.11
  14.8 5.1 %collective-permute-start.2 = (f32[128,2,1024]{2,0,1:T(8,128)S(1)}, f32[128,2,1024]{2,0,1:T(8,128)S(1)}, u32[]{:S(2)}, u32[]{:S(2)}) collective-permute-start(f32[128,2,1024]{2,0,1:T(8,128)S(1)} %fusion.11), channel_id=1, source_target_pairs={{0,2},{2,0},{1,3},{3,1},{4,6},{6,4},{5,7},{7,5},{8,10},{10,8},{9,1... | collective-permute-start | bytes 3145736 | tf_op jit(solution)/shard_map/ppermute | solution.py:79
  20.0 0.0 copy-done.1
  20.0 0.0 collective-permute-done
  20.0 23.3 %collective-permute-done.2 = f32[128,2,1024]{2,0,1:T(8,128)S(1)} collective-permute-done((f32[128,2,1024]{2,0,1:T(8,128)S(1)}, f32[128,2,1024]{2,0,1:T(8,128)S(1)}, u32[]{:S(2)}, u32[]{:S(2)}) %collective-permute-start.2) | collective-permute-done | bytes 1048608 | tf_op jit(solution)/shard_map/ppermute | solution.py:79
  43.3 1.3 fusion.14
  44.6 0.1 fusion.65
  44.7 1.3 collective-permute-start.3
  46.0 1.3 collective-permute-start.4
  47.3 0.1 fusion.107
  47.4 0.0 collective-permute-done.3
  47.4 5.3 %collective-permute-done.4 = f32[32,1024]{1,0:T(8,128)S(1)} collective-permute-done((f32[32,1024]{1,0:T(8,128)S(1)}, f32[32,1024]{1,0:T(8,128)S(1)}, u32[]{:S(2)}, u32[]{:S(2)}) %collective-permute-start.4) | collective-permute-done | bytes 131104 | tf_op jit(solution)/shard_map/ppermute | solution.py:25
  52.7 0.5 fusion.19
  53.2 0.1 fusion.64
  53.3 0.5 copy.45
  53.9 49.5 %all_to_all.14 = bf16[128,1,2,1024]{3,2,1,0:T(2,128)(2,1)S(1)} all-to-all(bf16[128,1,2,1024]{3,2,1,0:T(2,128)(2,1)S(1)} %copy.45), channel_id=1, replica_groups=mesh['ch'=128,'af'=4] {'ch'}, dimensions={0} | all-to-all | bytes 1048576 | tf_op jit(solution)/shard_map/all_to_all | solution.py:132
  103.3 0.5 copy.46
  103.9 0.1 slice_bitcast_fusion.3
  104.0 0.1 fusion.60
  104.1 0.1 fusion.106
  104.2 0.3 copy.58
  104.5 0.3 copy.59
  104.8 0.1 neg.52
  104.8 0.4 convolution_convert_fusion
  105.3 0.3 reshape.1000
  105.5 0.6 copy.49
  106.1 0.1 pad.9
  106.2 2.9 %reshape.1001 = bf16[8,2,128,257]{3,2,0,1:T(8,128)(2,1)S(1)} reshape(bf16[8,2,32896]{2,0,1:T(8,128)(2,1)S(1)} %pad.9) | data formatting | bytes 2105344 | tf_op jit(solution)/shard_map/reshape | solution.py:121
  109.1 0.1 slice.54
  109.2 0.0 copy-start.2
  109.2 0.0 copy-start.3
  109.2 1.1 reshape.1007
  110.3 1.4 copy.52
  111.7 8.9 %all-to-all-start.1 = ((bf16[128,2,1032]{2,1,0:T(2,128)(2,1)}), bf16[128,2,1032]{2,1,0:T(2,128)(2,1)S(1)}, u32[]{:S(2)}, u32[]{:S(2)}) async-start(bf16[128,2,1032]{2,1,0:T(2,128)(2,1)} %copy.52), calls=%async_computation.1 | async-start | bytes 1179648 | tf_op jit(solution)/shard_map/all_to_all | solution.py:141
  120.7 0.0 copy-done.2
  120.7 0.0 copy-done.3
  120.7 0.1 fusion.95
  120.8 36.5 %all-to-all-done.1 = bf16[128,2,1032]{2,1,0:T(2,128)(2,1)S(1)} async-done(((bf16[128,2,1032]{2,1,0:T(2,128)(2,1)}), bf16[128,2,1032]{2,1,0:T(2,128)(2,1)S(1)}, u32[]{:S(2)}, u32[]{:S(2)}) %all-to-all-start.1) | async-done | bytes 528416 | tf_op jit(solution)/shard_map/all_to_all | solution.py:141
  157.2 0.9 copy.53
  158.1 0.1 reshape.1004
  158.3 0.2 multiply_bitcast_fusion
  158.5 1.8 %copy.54 = f32[8,129,2,128]{3,2,1,0:T(2,128)} copy(f32[8,129,2,128]{3,1,0,2:T(8,128)S(1)} %multiply_bitcast_fusion) | data formatting | bytes 2113536 | tf_op jit(solution)/shard_map/mul | solution.py:148
  (6 shorter events, 0.0 us)
Async XLA Ops:
  4.5 2.2 %copy-start = (bf16[1,2048,1024]{2,1,0:T(8,128)(2,1)S(1)}, bf16[1,2048,1024]{2,1,0:T(8,128)(2,1)}, u32[]{:S(2)}) copy-start(bf16[1,2048,1024]{2,1,0:T(8,128)(2,1)} %param.4) | copy-start | bytes 12582916
  7.9 5.6 %collective-permute-start.1 = (f32[128,2,1024]{2,0,1:T(8,128)S(1)}, f32[128,2,1024]{2,0,1:T(8,128)S(1)}, u32[]{:S(2)}, u32[]{:S(2)}) collective-permute-start(f32[128,2,1024]{2,0,1:T(8,128)S(1)} %fusion), channel_id=1, source_target_pairs={{0,1},{1,0},{2,3},{3,2},{4,5},{5,4},{6,7},{7,6},{8,9},{9,8},{10,11... | collective-permute-start | bytes 3145736 | tf_op jit(solution)/shard_map/ppermute | solution.py:76
  11.1 8.9 %collective-permute-start = (f32[128,2,1024]{2,0,1:T(8,128)S(1)}, f32[128,2,1024]{2,0,1:T(8,128)S(1)}, u32[]{:S(2)}, u32[]{:S(2)}) collective-permute-start(f32[128,2,1024]{2,0,1:T(8,128)S(1)} %fusion.4), channel_id=1, source_target_pairs={{0,1},{1,0},{2,3},{3,2},{4,5},{5,4},{6,7},{7,6},{8,9},{9,8},{10,11... | collective-permute-start | bytes 3145736 | tf_op jit(solution)/shard_map/ppermute | solution.py:77
  13.6 6.4 %copy-start.1 = (s32[1024]{0:T(1024)S(1)}, s32[1024]{0:T(1024)}, u32[]{:S(2)}) copy-start(s32[1024]{0:T(1024)} %param.5) | copy-start | bytes 12292
  14.8 28.5 %collective-permute-start.2 = (f32[128,2,1024]{2,0,1:T(8,128)S(1)}, f32[128,2,1024]{2,0,1:T(8,128)S(1)}, u32[]{:S(2)}, u32[]{:S(2)}) collective-permute-start(f32[128,2,1024]{2,0,1:T(8,128)S(1)} %fusion.11), channel_id=1, source_target_pairs={{0,2},{2,0},{1,3},{3,1},{4,6},{6,4},{5,7},{7,5},{8,10},{10,8},{9,1... | collective-permute-start | bytes 3145736 | tf_op jit(solution)/shard_map/ppermute | solution.py:79
  44.7 2.7 %collective-permute-start.3 = (f32[32,1024]{1,0:T(8,128)S(1)}, f32[32,1024]{1,0:T(8,128)S(1)}, u32[]{:S(2)}, u32[]{:S(2)}) collective-permute-start(f32[32,1024]{1,0:T(8,128)S(1)} %get-tuple-element.25), channel_id=1, source_target_pairs={{0,1},{1,2},{2,3},{4,5},{5,6},{6,7},{8,9},{9,10},{10,11},{12,13},{... | collective-permute-start | bytes 393224 | tf_op jit(solution)/shard_map/ppermute | solution.py:23
  46.0 6.7 %collective-permute-start.4 = (f32[32,1024]{1,0:T(8,128)S(1)}, f32[32,1024]{1,0:T(8,128)S(1)}, u32[]{:S(2)}, u32[]{:S(2)}) collective-permute-start(f32[32,1024]{1,0:T(8,128)S(1)} %get-tuple-element.26), channel_id=1, source_target_pairs={{1,0},{2,1},{3,2},{5,4},{6,5},{7,6},{9,8},{10,9},{11,10},{13,12},{... | collective-permute-start | bytes 393224 | tf_op jit(solution)/shard_map/ppermute | solution.py:25
  109.2 11.4 %copy-start.2 = (s32[8]{0:T(128)S(1)}, s32[8]{0:T(128)}, u32[]{:S(2)}) copy-start(s32[8]{0:T(128)} %param.7) | copy-start | bytes 100
  109.2 11.4 %copy-start.3 = (s32[8]{0:T(128)S(1)}, s32[8]{0:T(128)}, u32[]{:S(2)}) copy-start(s32[8]{0:T(128)} %param.6) | copy-start | bytes 100
  111.7 45.5 %all-to-all-start.1 = ((bf16[128,2,1032]{2,1,0:T(2,128)(2,1)}), bf16[128,2,1032]{2,1,0:T(2,128)(2,1)S(1)}, u32[]{:S(2)}, u32[]{:S(2)}) async-start(bf16[128,2,1032]{2,1,0:T(2,128)(2,1)} %copy.52), calls=%async_computation.1 | async-start | bytes 1179648 | tf_op jit(solution)/shard_map/all_to_all | solution.py:141

commit v8 on v7

--- a/solution.py
+++ b/solution.py
@@ -66,7 +66,7 @@
     core = index % 2
     chip = index // 2
     sample_index = index * quarter + jnp.arange(quarter, dtype=jnp.int32)
-    fine_table = fine_rotation(sample_index, SEGLEN, 64)
+    fine_table = fine_rotation(sample_index, SEGLEN, 32)
     cores = [(0, 1), (1, 0), (2, 3), (3, 2)]
     chips = [(0, 2), (2, 0), (1, 3), (3, 1)]
 
@@ -139,13 +139,14 @@
     segments = by_bin.shape[0]
     rows = bin_cross(by_bin, REACH, slab_width)
     back = lax.all_to_all(rows, "ch", split_axis=0, concat_axis=0, tiled=True)
-    back = back.reshape(slab_count, 2, slab_width, REACH + 1).astype(jnp.float32)
+    back = back.reshape(slab_count, 2, slab_width, REACH + 1)
+    back = jnp.transpose(back, (2, 3, 1, 0)).astype(jnp.float32)
     offsets = jnp.arange(REACH + 1, dtype=jnp.int32)
     inside_band = (
         (offsets[None, :] >= band_low[:, None]) & (offsets[None, :] <= band_high[:, None])
     ).astype(jnp.float32)
     result = (
-        jnp.transpose(back, (2, 3, 1, 0))
+        back
         * inside_band[:, :, None, None]
         * (1.0 / math.sqrt(segments))
     )

time: 162 us -> 161 us (level)
  no operation moved by 1% of the time
where the time goes in v8:
time: 161 us; the launch traced here: 159 us
  waiting for transfers between devices  65.1 us (40%)
  blocking collectives  49.3 us (31%)
  starting transfers between devices  20.9 us (13%)
  local copies, waits for them, and re-layouts  12 us (7%)
  matrix products  6.05 us (4%)
  other arithmetic  5.31 us (3%)
    all_to_all x1, blocking collectives, per_device(): lax.all_to_all(whitened.reshape(band_rows, 1, 2, channels), 'ch', split_a...  49.3 us
    all_to_all x1, waiting for transfers between devices, per_device(): back = lax.all_to_all(rows, 'ch', split_axis=0, concat_axis=0, tiled=True)  36.5 us
    ppermute x1, waiting for transfers between devices, reduced_spectra(): incoming = lax.ppermute(outgoing, 'af', chips)  23.3 us
    all_to_all x1, starting transfers between devices, per_device(): back = lax.all_to_all(rows, 'ch', split_axis=0, concat_axis=0, tiled=True)  8.92 us
    ppermute x1, waiting for transfers between devices, extended(): lax.ppermute(head, axis, [((i + 1) % count, i) for i in range(ends)])  5.28 us
    ppermute x1, starting transfers between devices, reduced_spectra(): incoming = lax.ppermute(outgoing, 'af', chips)  5.1 us
    dot_general x4, matrix products, quarter_spectra(): out = jnp.dot(basis, local_record, preferred_element_type=jnp.float32)  5.09 us
  transfers between devices with their start and end apart: 6, of which 3 were waited for; matrix products, arithmetic and copies ran while one was open for 2% of the time, Pallas kernels for 0%

profile of v8, /device:TPU:6, one launch (start us, length us, event | category | flops | bytes accessed | tf_op | source)
XLA Modules:
  0.0 159.2 jit_solution(10810332207745418885)
XLA Ops:
  0.0 0.1 multiply_subtract_fusion.4
  0.1 1.0 fusion.70
  1.1 1.1 fusion.93
  2.2 1.2 multiply_subtract_fusion.3
  3.4 0.0 copy-start
  3.5 1.3 fusion.54
  4.7 0.9 copy-done
  5.6 1.3 fusion
  6.9 1.9 %collective-permute-start.1 = (f32[128,2,1024]{2,0,1:T(8,128)S(1)}, f32[128,2,1024]{2,0,1:T(8,128)S(1)}, u32[]{:S(2)}, u32[]{:S(2)}) collective-permute-start(f32[128,2,1024]{2,0,1:T(8,128)S(1)} %fusion), channel_id=1, source_target_pairs={{0,1},{1,0},{2,3},{3,2},{4,5},{5,4},{6,7},{7,6},{8,9},{9,8},{10,11... | collective-permute-start | bytes 3145736 | tf_op jit(solution)/shard_map/ppermute | solution.py:76
  8.8 1.3 fusion.4
  10.1 2.4 %collective-permute-start = (f32[128,2,1024]{2,0,1:T(8,128)S(1)}, f32[128,2,1024]{2,0,1:T(8,128)S(1)}, u32[]{:S(2)}, u32[]{:S(2)}) collective-permute-start(f32[128,2,1024]{2,0,1:T(8,128)S(1)} %fusion.4), channel_id=1, source_target_pairs={{0,1},{1,0},{2,3},{3,2},{4,5},{5,4},{6,7},{7,6},{8,9},{9,8},{10,11... | collective-permute-start | bytes 3145736 | tf_op jit(solution)/shard_map/ppermute | solution.py:77
  12.5 0.0 collective-permute-done.1
  12.5 0.0 copy-start.1
  12.6 1.3 fusion.11
  13.8 5.1 %collective-permute-start.2 = (f32[128,2,1024]{2,0,1:T(8,128)S(1)}, f32[128,2,1024]{2,0,1:T(8,128)S(1)}, u32[]{:S(2)}, u32[]{:S(2)}) collective-permute-start(f32[128,2,1024]{2,0,1:T(8,128)S(1)} %fusion.11), channel_id=1, source_target_pairs={{0,2},{2,0},{1,3},{3,1},{4,6},{6,4},{5,7},{7,5},{8,10},{10,8},{9,1... | collective-permute-start | bytes 3145736 | tf_op jit(solution)/shard_map/ppermute | solution.py:79
  18.9 0.0 copy-done.1
  19.0 0.0 collective-permute-done
  19.0 23.3 %collective-permute-done.2 = f32[128,2,1024]{2,0,1:T(8,128)S(1)} collective-permute-done((f32[128,2,1024]{2,0,1:T(8,128)S(1)}, f32[128,2,1024]{2,0,1:T(8,128)S(1)}, u32[]{:S(2)}, u32[]{:S(2)}) %collective-permute-start.2) | collective-permute-done | bytes 1048608 | tf_op jit(solution)/shard_map/ppermute | solution.py:79
  42.3 1.3 fusion.14
  43.6 0.1 fusion.62
  43.7 1.3 collective-permute-start.3
  45.0 1.3 collective-permute-start.4
  46.3 0.1 fusion.107
  46.4 0.0 collective-permute-done.3
  46.4 5.3 %collective-permute-done.4 = f32[32,1024]{1,0:T(8,128)S(1)} collective-permute-done((f32[32,1024]{1,0:T(8,128)S(1)}, f32[32,1024]{1,0:T(8,128)S(1)}, u32[]{:S(2)}, u32[]{:S(2)}) %collective-permute-start.4) | collective-permute-done | bytes 131104 | tf_op jit(solution)/shard_map/ppermute | solution.py:25
  51.7 0.5 fusion.19
  52.2 0.1 fusion.61
  52.3 0.5 copy.45
  52.9 49.3 %all_to_all.14 = bf16[128,1,2,1024]{3,2,1,0:T(2,128)(2,1)S(1)} all-to-all(bf16[128,1,2,1024]{3,2,1,0:T(2,128)(2,1)S(1)} %copy.45), channel_id=1, replica_groups=mesh['ch'=128,'af'=4] {'ch'}, dimensions={0} | all-to-all | bytes 1048576 | tf_op jit(solution)/shard_map/all_to_all | solution.py:132
  102.2 0.5 copy.46
  102.7 0.1 slice_bitcast_fusion.3
  102.8 0.1 fusion.60
  102.9 0.1 fusion.106
  103.0 0.3 copy.58
  103.3 0.3 copy.59
  103.6 0.1 neg.52
  103.6 0.4 convolution_convert_fusion
  104.1 0.3 reshape.1000
  104.4 0.6 copy.49
  105.0 0.1 pad.9
  105.0 2.9 %reshape.1001 = bf16[8,2,128,257]{3,2,0,1:T(8,128)(2,1)S(1)} reshape(bf16[8,2,32896]{2,0,1:T(8,128)(2,1)S(1)} %pad.9) | data formatting | bytes 2105344 | tf_op jit(solution)/shard_map/reshape | solution.py:121
  108.0 0.1 slice.54
  108.0 0.0 copy-start.2
  108.1 0.0 copy-start.3
  108.1 1.1 reshape.1007
  109.1 1.4 copy.52
  110.5 8.9 %all-to-all-start.1 = ((bf16[128,2,1032]{2,1,0:T(2,128)(2,1)}), bf16[128,2,1032]{2,1,0:T(2,128)(2,1)S(1)}, u32[]{:S(2)}, u32[]{:S(2)}) async-start(bf16[128,2,1032]{2,1,0:T(2,128)(2,1)} %copy.52), calls=%async_computation.1 | async-start | bytes 1179648 | tf_op jit(solution)/shard_map/all_to_all | solution.py:141
  119.5 0.0 copy-done.2
  119.5 0.0 copy-done.3
  119.5 0.1 fusion.95
  119.6 36.5 %all-to-all-done.1 = bf16[128,2,1032]{2,1,0:T(2,128)(2,1)S(1)} async-done(((bf16[128,2,1032]{2,1,0:T(2,128)(2,1)}), bf16[128,2,1032]{2,1,0:T(2,128)(2,1)S(1)}, u32[]{:S(2)}, u32[]{:S(2)}) %all-to-all-start.1) | async-done | bytes 528416 | tf_op jit(solution)/shard_map/all_to_all | solution.py:141
  156.1 0.9 copy.53
  157.0 0.1 reshape.1004
  157.1 0.2 multiply_bitcast_fusion
  157.4 1.8 %copy.54 = f32[8,129,2,128]{3,2,1,0:T(2,128)} copy(f32[8,129,2,128]{3,1,0,2:T(8,128)S(1)} %multiply_bitcast_fusion) | data formatting | bytes 2113536 | tf_op jit(solution)/shard_map/mul | solution.py:149
  (6 shorter events, 0.0 us)
Async XLA Ops:
  3.4 2.2 %copy-start = (bf16[1,2048,1024]{2,1,0:T(8,128)(2,1)S(1)}, bf16[1,2048,1024]{2,1,0:T(8,128)(2,1)}, u32[]{:S(2)}) copy-start(bf16[1,2048,1024]{2,1,0:T(8,128)(2,1)} %param.4) | copy-start | bytes 12582916
  6.9 5.6 %collective-permute-start.1 = (f32[128,2,1024]{2,0,1:T(8,128)S(1)}, f32[128,2,1024]{2,0,1:T(8,128)S(1)}, u32[]{:S(2)}, u32[]{:S(2)}) collective-permute-start(f32[128,2,1024]{2,0,1:T(8,128)S(1)} %fusion), channel_id=1, source_target_pairs={{0,1},{1,0},{2,3},{3,2},{4,5},{5,4},{6,7},{7,6},{8,9},{9,8},{10,11... | collective-permute-start | bytes 3145736 | tf_op jit(solution)/shard_map/ppermute | solution.py:76
  10.1 8.9 %collective-permute-start = (f32[128,2,1024]{2,0,1:T(8,128)S(1)}, f32[128,2,1024]{2,0,1:T(8,128)S(1)}, u32[]{:S(2)}, u32[]{:S(2)}) collective-permute-start(f32[128,2,1024]{2,0,1:T(8,128)S(1)} %fusion.4), channel_id=1, source_target_pairs={{0,1},{1,0},{2,3},{3,2},{4,5},{5,4},{6,7},{7,6},{8,9},{9,8},{10,11... | collective-permute-start | bytes 3145736 | tf_op jit(solution)/shard_map/ppermute | solution.py:77
  12.5 6.4 %copy-start.1 = (s32[1024]{0:T(1024)S(1)}, s32[1024]{0:T(1024)}, u32[]{:S(2)}) copy-start(s32[1024]{0:T(1024)} %param.5) | copy-start | bytes 12292
  13.8 28.5 %collective-permute-start.2 = (f32[128,2,1024]{2,0,1:T(8,128)S(1)}, f32[128,2,1024]{2,0,1:T(8,128)S(1)}, u32[]{:S(2)}, u32[]{:S(2)}) collective-permute-start(f32[128,2,1024]{2,0,1:T(8,128)S(1)} %fusion.11), channel_id=1, source_target_pairs={{0,2},{2,0},{1,3},{3,1},{4,6},{6,4},{5,7},{7,5},{8,10},{10,8},{9,1... | collective-permute-start | bytes 3145736 | tf_op jit(solution)/shard_map/ppermute | solution.py:79
  43.7 2.7 %collective-permute-start.3 = (f32[32,1024]{1,0:T(8,128)S(1)}, f32[32,1024]{1,0:T(8,128)S(1)}, u32[]{:S(2)}, u32[]{:S(2)}) collective-permute-start(f32[32,1024]{1,0:T(8,128)S(1)} %get-tuple-element.19), channel_id=1, source_target_pairs={{0,1},{1,2},{2,3},{4,5},{5,6},{6,7},{8,9},{9,10},{10,11},{12,13},{... | collective-permute-start | bytes 393224 | tf_op jit(solution)/shard_map/ppermute | solution.py:23
  45.0 6.7 %collective-permute-start.4 = (f32[32,1024]{1,0:T(8,128)S(1)}, f32[32,1024]{1,0:T(8,128)S(1)}, u32[]{:S(2)}, u32[]{:S(2)}) collective-permute-start(f32[32,1024]{1,0:T(8,128)S(1)} %get-tuple-element.20), channel_id=1, source_target_pairs={{1,0},{2,1},{3,2},{5,4},{6,5},{7,6},{9,8},{10,9},{11,10},{13,12},{... | collective-permute-start | bytes 393224 | tf_op jit(solution)/shard_map/ppermute | solution.py:25
  108.0 11.4 %copy-start.2 = (s32[8]{0:T(128)S(1)}, s32[8]{0:T(128)}, u32[]{:S(2)}) copy-start(s32[8]{0:T(128)} %param.7) | copy-start | bytes 100
  108.1 11.4 %copy-start.3 = (s32[8]{0:T(128)S(1)}, s32[8]{0:T(128)}, u32[]{:S(2)}) copy-start(s32[8]{0:T(128)} %param.6) | copy-start | bytes 100
  110.5 45.5 %all-to-all-start.1 = ((bf16[128,2,1032]{2,1,0:T(2,128)(2,1)}), bf16[128,2,1032]{2,1,0:T(2,128)(2,1)S(1)}, u32[]{:S(2)}, u32[]{:S(2)}) async-start(bf16[128,2,1032]{2,1,0:T(2,128)(2,1)} %copy.52), calls=%async_computation.1 | async-start | bytes 1179648 | tf_op jit(solution)/shard_map/all_to_all | solution.py:141

commit v9 on v8

--- a/solution.py
+++ b/solution.py
@@ -76,8 +76,15 @@
     first = lax.ppermute(spectra_of(1 - chip, 1 - core), "af", cores)
     second = lax.ppermute(spectra_of(chip, 1 - core), "af", cores)
     outgoing = spectra_of(1 - chip, core) + first
-    incoming = lax.ppermute(outgoing, "af", chips)
-    return (spectra_of(chip, core) + second) + incoming
+    rows = outgoing.shape[0]
+    edge_rows = jnp.concatenate([outgoing[:SMOOTH], outgoing[rows - SMOOTH:]], axis=0)
+    incoming_edges = lax.ppermute(edge_rows, "af", chips)
+    incoming_middle = lax.ppermute(outgoing[SMOOTH : rows - SMOOTH], "af", chips)
+    own = spectra_of(chip, core) + second
+    own_edges = jnp.concatenate([own[:SMOOTH], own[rows - SMOOTH:]], axis=0)
+    edges = own_edges + incoming_edges
+    middle = own[SMOOTH : rows - SMOOTH] + incoming_middle
+    return edges, middle
 
 
 def band_sum(padded, half_width):
@@ -91,9 +98,16 @@
 
 
 def whiten_local(records, quality):
-    spectra = reduced_spectra(records[0])
-    power_bins = spectra[:, 0] * spectra[:, 0] + spectra[:, 1] * spectra[:, 1]
-    padded = extended(power_bins, (("af", 0),), SMOOTH)
+    edges, middle = reduced_spectra(records[0])
+    spectra = jnp.concatenate([edges[:SMOOTH], middle, edges[SMOOTH:]], axis=0)
+    edge_power = edges[:, 0] * edges[:, 0] + edges[:, 1] * edges[:, 1]
+    middle_power = middle[:, 0] * middle[:, 0] + middle[:, 1] * middle[:, 1]
+    count = lax.axis_size("af")
+    below = lax.ppermute(edge_power[SMOOTH:], "af", [(i, i + 1) for i in range(count - 1)])
+    above = lax.ppermute(edge_power[:SMOOTH], "af", [(i + 1, i) for i in range(count - 1)])
+    padded = jnp.concatenate(
+        [below, edge_power[:SMOOTH], middle_power, edge_power[SMOOTH:], above], axis=0
+    )
     smoothed = band_sum(padded, SMOOTH)
     factor = quality.astype(jnp.float32)[None, :] / jnp.sqrt(
         smoothed * (1.0 / (2 * SMOOTH + 1)) + 1e-06

time: 161 us -> 154 us (0.957)
  waiting for transfers between devices: 65.1 us -> 54.2 us
  blocking collectives: 49.3 us -> 54.4 us
    ppermute x3 -> x4, waiting for transfers between devices: 28.6 us -> 17.2 us  [the longest x1 9.5 us: reduced_spectra(): incoming_edges = lax.ppermute(edge_rows, 'af', chips)]
    all_to_all x1, blocking collectives: 49.3 us -> 54.4 us  [per_device(): lax.all_to_all(whitened.reshape(band_rows, 1, 2, channels), 'ch', split_a...]
    ppermute x3 -> x4, starting transfers between devices: 7.69 us -> 9.94 us  [the longest x1 5.1 us: reduced_spectra(): incoming_edges = lax.ppermute(edge_rows, 'af', chips)]
    all_to_all x1, starting transfers between devices: 8.92 us -> 6.75 us  [per_device(): back = lax.all_to_all(rows, 'ch', split_axis=0, concat_axis=0, tiled=True)]
  transfers between devices with their start and end apart: 6 -> 7, of which waited for: 3 -> 3; matrix products, arithmetic and copies ran while one was open for 2% -> 3% of each run, Pallas kernels for 0% -> 0%
where the time goes in v9:
time: 154 us
  blocking collectives  54.4 us (35%)
  waiting for transfers between devices  54.2 us (35%)
  starting transfers between devices  21 us (14%)
  local copies, waits for them, and re-layouts  12.2 us (8%)
  matrix products  6.05 us (4%)
  other arithmetic  5.4 us (4%)
    all_to_all x1, blocking collectives, per_device(): lax.all_to_all(whitened.reshape(band_rows, 1, 2, channels), 'ch', split_a...  54.4 us
    all_to_all x1, waiting for transfers between devices, per_device(): back = lax.all_to_all(rows, 'ch', split_axis=0, concat_axis=0, tiled=True)  37 us
    ppermute x1, waiting for transfers between devices, reduced_spectra(): incoming_edges = lax.ppermute(edge_rows, 'af', chips)  9.5 us
    ppermute x1, waiting for transfers between devices, reduced_spectra(): incoming_middle = lax.ppermute(outgoing[SMOOTH:rows - SMOOTH], 'af', chips)  7.7 us
    all_to_all x1, starting transfers between devices, per_device(): back = lax.all_to_all(rows, 'ch', split_axis=0, concat_axis=0, tiled=True)  6.75 us
    ppermute x1, starting transfers between devices, reduced_spectra(): incoming_edges = lax.ppermute(edge_rows, 'af', chips)  5.1 us
    dot_general x4, matrix products, quarter_spectra(): out = jnp.dot(basis, local_record, preferred_element_type=jnp.float32)  5.09 us
  transfers between devices with their start and end apart: 7, of which 3 were waited for; matrix products, arithmetic and copies ran while one was open for 3% of the time, Pallas kernels for 0%

profile of v9, /device:TPU:6, one launch (start us, length us, event | category | flops | bytes accessed | tf_op | source)
XLA Modules:
  0.0 153.7 jit_solution(10563963077817546535)
XLA Ops:
  0.0 0.1 multiply_subtract_fusion.4
  0.1 1.0 fusion.65
  1.1 1.1 fusion.88
  2.2 1.2 multiply_subtract_fusion.3
  3.4 0.0 copy-start.3
  3.5 1.3 fusion.52
  4.7 0.9 copy-done.3
  5.6 1.3 fusion
  6.9 1.9 %collective-permute-start.1 = (f32[128,2,1024]{2,0,1:T(8,128)S(1)}, f32[128,2,1024]{2,0,1:T(8,128)S(1)}, u32[]{:S(2)}, u32[]{:S(2)}) collective-permute-start(f32[128,2,1024]{2,0,1:T(8,128)S(1)} %fusion), channel_id=1, source_target_pairs={{0,1},{1,0},{2,3},{3,2},{4,5},{5,4},{6,7},{7,6},{8,9},{9,8},{10,11... | collective-permute-start | bytes 3145736 | tf_op jit(solution)/shard_map/ppermute | solution.py:76
  8.8 0.0 copy-start
  8.9 1.3 fusion.4
  10.1 2.4 %collective-permute-start = (f32[128,2,1024]{2,0,1:T(8,128)S(1)}, f32[128,2,1024]{2,0,1:T(8,128)S(1)}, u32[]{:S(2)}, u32[]{:S(2)}) collective-permute-start(f32[128,2,1024]{2,0,1:T(8,128)S(1)} %fusion.4), channel_id=1, source_target_pairs={{0,1},{1,0},{2,3},{3,2},{4,5},{5,4},{6,7},{7,6},{8,9},{9,8},{10,11... | collective-permute-start | bytes 3145736 | tf_op jit(solution)/shard_map/ppermute | solution.py:77
  12.5 0.0 copy-done
  12.6 0.0 collective-permute-done.1
  12.6 1.3 fusion.11
  14.0 5.1 %collective-permute-start.2 = (f32[64,2,1024]{2,0,1:T(8,128)S(1)}, f32[64,2,1024]{2,0,1:T(8,128)S(1)}, u32[]{:S(2)}, u32[]{:S(2)}) collective-permute-start(f32[64,2,1024]{2,0,1:T(8,128)S(1)} %pad_maximum_fusion), channel_id=1, source_target_pairs={{0,2},{2,0},{1,3},{3,1},{4,6},{6,4},{5,7},{7,5},{8,10},{10,8},{9,1... | collective-permute-start | bytes 1572872 | tf_op jit(solution)/shard_map/ppermute | solution.py:81
  19.1 2.2 %collective-permute-start.3 = (f32[64,2,1024]{2,0,1:T(8,128)S(1)}, f32[64,2,1024]{2,0,1:T(8,128)S(1)}, u32[]{:S(2)}, u32[]{:S(2)}) collective-permute-start(f32[64,2,1024]{2,0,1:T(8,128)S(1)} %slice.96), channel_id=1, source_target_pairs={{0,2},{2,0},{1,3},{3,1},{4,6},{6,4},{5,7},{7,5},{8,10},{10,8},{9,1... | collective-permute-start | bytes 1572872 | tf_op jit(solution)/shard_map/ppermute | solution.py:82
  21.4 0.0 collective-permute-done
  21.4 1.3 fusion.8
  22.7 9.5 %collective-permute-done.2 = f32[64,2,1024]{2,0,1:T(8,128)S(1)} collective-permute-done((f32[64,2,1024]{2,0,1:T(8,128)S(1)}, f32[64,2,1024]{2,0,1:T(8,128)S(1)}, u32[]{:S(2)}, u32[]{:S(2)}) %collective-permute-start.2) | collective-permute-done | bytes 524320 | tf_op jit(solution)/shard_map/ppermute | solution.py:81
  32.2 0.1 maximum_add_fusion
  32.3 1.3 collective-permute-start.4
  33.7 1.3 collective-permute-start.5
  35.0 7.7 %collective-permute-done.3 = f32[64,2,1024]{2,0,1:T(8,128)S(1)} collective-permute-done((f32[64,2,1024]{2,0,1:T(8,128)S(1)}, f32[64,2,1024]{2,0,1:T(8,128)S(1)}, u32[]{:S(2)}, u32[]{:S(2)}) %collective-permute-start.3) | collective-permute-done | bytes 524320 | tf_op jit(solution)/shard_map/ppermute | solution.py:82
  42.6 0.1 slice_add_fusion
  42.8 0.0 collective-permute-done.4
  42.9 0.0 collective-permute-done.5
  42.9 0.5 fusion.16
  43.4 0.1 fusion.31
  43.5 0.5 copy.45
  44.1 54.4 %all_to_all.14 = bf16[128,1,2,1024]{3,2,1,0:T(2,128)(2,1)S(1)} all-to-all(bf16[128,1,2,1024]{3,2,1,0:T(2,128)(2,1)S(1)} %copy.45), channel_id=1, replica_groups=mesh['ch'=128,'af'=4] {'ch'}, dimensions={0} | all-to-all | bytes 1048576 | tf_op jit(solution)/shard_map/all_to_all | solution.py:146
  98.5 0.5 copy.46
  99.0 0.1 slice_bitcast_fusion.5
  99.2 0.1 fusion.53
  99.2 0.1 fusion.102
  99.3 0.3 copy.58
  99.6 0.3 copy.59
  99.9 0.1 neg.52
  99.9 0.4 convolution_convert_fusion
  100.4 0.3 reshape.1045
  100.7 0.6 copy.49
  101.3 0.1 pad.9
  101.3 2.9 %reshape.1046 = bf16[8,2,128,257]{3,2,0,1:T(8,128)(2,1)S(1)} reshape(bf16[8,2,32896]{2,0,1:T(8,128)(2,1)S(1)} %pad.9) | data formatting | bytes 2105344 | tf_op jit(solution)/shard_map/reshape | solution.py:135
  104.3 0.1 slice.108
  104.4 0.0 copy-start.1
  104.4 0.0 copy-start.2
  104.4 1.1 reshape.1052
  105.4 1.4 copy.52
  106.9 6.8 %all-to-all-start.1 = ((bf16[128,2,1032]{2,1,0:T(2,128)(2,1)}), bf16[128,2,1032]{2,1,0:T(2,128)(2,1)S(1)}, u32[]{:S(2)}, u32[]{:S(2)}) async-start(bf16[128,2,1032]{2,1,0:T(2,128)(2,1)} %copy.52), calls=%async_computation.1 | async-start | bytes 1179648 | tf_op jit(solution)/shard_map/all_to_all | solution.py:155
  113.6 0.0 copy-done.1
  113.6 0.0 copy-done.2
  113.6 0.1 fusion.90
  113.7 37.0 %all-to-all-done.1 = bf16[128,2,1032]{2,1,0:T(2,128)(2,1)S(1)} async-done(((bf16[128,2,1032]{2,1,0:T(2,128)(2,1)}), bf16[128,2,1032]{2,1,0:T(2,128)(2,1)S(1)}, u32[]{:S(2)}, u32[]{:S(2)}) %all-to-all-start.1) | async-done | bytes 528416 | tf_op jit(solution)/shard_map/all_to_all | solution.py:155
  150.7 0.9 copy.53
  151.6 0.1 reshape.1049
  151.7 0.2 multiply_bitcast_fusion
  151.9 1.8 %copy.54 = f32[8,129,2,128]{3,2,1,0:T(2,128)} copy(f32[8,129,2,128]{3,1,0,2:T(8,128)S(1)} %multiply_bitcast_fusion) | data formatting | bytes 2113536 | tf_op jit(solution)/shard_map/mul | solution.py:163
  (17 shorter events, 0.3 us)
Async XLA Ops:
  3.4 2.2 %copy-start.3 = (bf16[1,2048,1024]{2,1,0:T(8,128)(2,1)S(1)}, bf16[1,2048,1024]{2,1,0:T(8,128)(2,1)}, u32[]{:S(2)}) copy-start(bf16[1,2048,1024]{2,1,0:T(8,128)(2,1)} %param.4) | copy-start | bytes 12582916
  6.9 5.7 %collective-permute-start.1 = (f32[128,2,1024]{2,0,1:T(8,128)S(1)}, f32[128,2,1024]{2,0,1:T(8,128)S(1)}, u32[]{:S(2)}, u32[]{:S(2)}) collective-permute-start(f32[128,2,1024]{2,0,1:T(8,128)S(1)} %fusion), channel_id=1, source_target_pairs={{0,1},{1,0},{2,3},{3,2},{4,5},{5,4},{6,7},{7,6},{8,9},{9,8},{10,11... | collective-permute-start | bytes 3145736 | tf_op jit(solution)/shard_map/ppermute | solution.py:76
  8.8 3.7 %copy-start = (s32[1024]{0:T(1024)S(1)}, s32[1024]{0:T(1024)}, u32[]{:S(2)}) copy-start(s32[1024]{0:T(1024)} %param.5) | copy-start | bytes 12292
  10.1 11.2 %collective-permute-start = (f32[128,2,1024]{2,0,1:T(8,128)S(1)}, f32[128,2,1024]{2,0,1:T(8,128)S(1)}, u32[]{:S(2)}, u32[]{:S(2)}) collective-permute-start(f32[128,2,1024]{2,0,1:T(8,128)S(1)} %fusion.4), channel_id=1, source_target_pairs={{0,1},{1,0},{2,3},{3,2},{4,5},{5,4},{6,7},{7,6},{8,9},{9,8},{10,11... | collective-permute-start | bytes 3145736 | tf_op jit(solution)/shard_map/ppermute | solution.py:77
  14.0 18.2 %collective-permute-start.2 = (f32[64,2,1024]{2,0,1:T(8,128)S(1)}, f32[64,2,1024]{2,0,1:T(8,128)S(1)}, u32[]{:S(2)}, u32[]{:S(2)}) collective-permute-start(f32[64,2,1024]{2,0,1:T(8,128)S(1)} %pad_maximum_fusion), channel_id=1, source_target_pairs={{0,2},{2,0},{1,3},{3,1},{4,6},{6,4},{5,7},{7,5},{8,10},{10,8},{9,1... | collective-permute-start | bytes 1572872 | tf_op jit(solution)/shard_map/ppermute | solution.py:81
  19.1 23.5 %collective-permute-start.3 = (f32[64,2,1024]{2,0,1:T(8,128)S(1)}, f32[64,2,1024]{2,0,1:T(8,128)S(1)}, u32[]{:S(2)}, u32[]{:S(2)}) collective-permute-start(f32[64,2,1024]{2,0,1:T(8,128)S(1)} %slice.96), channel_id=1, source_target_pairs={{0,2},{2,0},{1,3},{3,1},{4,6},{6,4},{5,7},{7,5},{8,10},{10,8},{9,1... | collective-permute-start | bytes 1572872 | tf_op jit(solution)/shard_map/ppermute | solution.py:82
  32.3 10.4 %collective-permute-start.4 = (f32[32,1024]{1,0:T(8,128)S(1)}, f32[32,1024]{1,0:T(8,128)S(1)}, u32[]{:S(2)}, u32[]{:S(2)}) collective-permute-start(f32[32,1024]{1,0:T(8,128)S(1)} %get-tuple-element.32), channel_id=1, source_target_pairs={{0,1},{1,2},{2,3},{4,5},{5,6},{6,7},{8,9},{9,10},{10,11},{12,13},{... | collective-permute-start | bytes 393224 | tf_op jit(solution)/shard_map/ppermute | solution.py:106
  33.7 9.2 %collective-permute-start.5 = (f32[32,1024]{1,0:T(8,128)S(1)}, f32[32,1024]{1,0:T(8,128)S(1)}, u32[]{:S(2)}, u32[]{:S(2)}) collective-permute-start(f32[32,1024]{1,0:T(8,128)S(1)} %get-tuple-element.31), channel_id=1, source_target_pairs={{1,0},{2,1},{3,2},{5,4},{6,5},{7,6},{9,8},{10,9},{11,10},{13,12},{... | collective-permute-start | bytes 393224 | tf_op jit(solution)/shard_map/ppermute | solution.py:107
  104.4 9.3 %copy-start.1 = (s32[8]{0:T(128)S(1)}, s32[8]{0:T(128)}, u32[]{:S(2)}) copy-start(s32[8]{0:T(128)} %param.7) | copy-start | bytes 100
  104.4 9.3 %copy-start.2 = (s32[8]{0:T(128)S(1)}, s32[8]{0:T(128)}, u32[]{:S(2)}) copy-start(s32[8]{0:T(128)} %param.6) | copy-start | bytes 100
  106.9 43.8 %all-to-all-start.1 = ((bf16[128,2,1032]{2,1,0:T(2,128)(2,1)}), bf16[128,2,1032]{2,1,0:T(2,128)(2,1)S(1)}, u32[]{:S(2)}, u32[]{:S(2)}) async-start(bf16[128,2,1032]{2,1,0:T(2,128)(2,1)} %copy.52), calls=%async_computation.1 | async-start | bytes 1179648 | tf_op jit(solution)/shard_map/all_to_all | solution.py:155

commit v10 on v9

--- a/solution.py
+++ b/solution.py
@@ -29,33 +29,30 @@
     return cells
 
 
-def fine_rotation(sample_index, length, fine):
+def rotation_tables(sample_index, length, fine, groups):
     step = 2.0 * math.pi / length
-    fine_bins = jnp.arange(fine, dtype=jnp.int32)
-    fine_angle = (fine_bins[:, None] * sample_index[None, :] % length).astype(jnp.float32) * step
+    bins = jnp.concatenate(
+        [jnp.arange(fine, dtype=jnp.int32), LOWBIN + fine * jnp.arange(groups, dtype=jnp.int32)]
+    )
+    angle = (bins[:, None] * sample_index[None, :] % length).astype(jnp.float32) * step
     tapers = 0.5 - 0.5 * jnp.cos(sample_index.astype(jnp.float32) * step)
-    return jnp.cos(fine_angle)[None], jnp.sin(fine_angle)[None], tapers
+    return jnp.cos(angle), jnp.sin(angle), tapers
 
 
-def taper_table(coarse_bins, sample_index, length, fine_table):
-    cos_f, sin_f, tapers = fine_table
-    step = 2.0 * math.pi / length
-    coarse_angle = (coarse_bins[:, None] * sample_index[None, :] % length).astype(jnp.float32) * step
-    cos_c = jnp.cos(coarse_angle)[:, None, :]
-    sin_c = jnp.sin(coarse_angle)[:, None, :]
-    rows = coarse_bins.shape[0] * cos_f.shape[1]
+def quarter_spectra(local_record, quarter_index, tables, fine):
+    cos_all, sin_all, tapers = tables
+    rows = BINS // 4
+    per_quarter = rows // fine
+    start = fine + quarter_index * per_quarter
+    cos_c = lax.dynamic_slice_in_dim(cos_all, start, per_quarter, axis=0)[:, None, :]
+    sin_c = lax.dynamic_slice_in_dim(sin_all, start, per_quarter, axis=0)[:, None, :]
+    cos_f = cos_all[None, :fine]
+    sin_f = sin_all[None, :fine]
     cos_a = (cos_c * cos_f - sin_c * sin_f).reshape(rows, -1)
     sin_a = (sin_c * cos_f + cos_c * sin_f).reshape(rows, -1)
     real_row = (tapers[None, :] * cos_a).astype(jnp.bfloat16)
     imag_row = (-(tapers[None, :] * sin_a)).astype(jnp.bfloat16)
-    return jnp.stack([real_row, imag_row], axis=1)
-
-
-def quarter_spectra(local_record, sample_index, quarter_index, fine_table):
-    fine = fine_table[0].shape[1]
-    rows = BINS // 4
-    coarse_bins = LOWBIN + quarter_index * rows + fine * jnp.arange(rows // fine, dtype=jnp.int32)
-    basis = taper_table(coarse_bins, sample_index, SEGLEN, fine_table).reshape(2 * rows, -1)
+    basis = jnp.stack([real_row, imag_row], axis=1).reshape(2 * rows, -1)
     out = jnp.dot(basis, local_record, preferred_element_type=jnp.float32)
     return out.reshape(rows, 2, local_record.shape[1])
 
@@ -66,12 +63,13 @@
     core = index % 2
     chip = index // 2
     sample_index = index * quarter + jnp.arange(quarter, dtype=jnp.int32)
-    fine_table = fine_rotation(sample_index, SEGLEN, 32)
+    fine = 32
+    tables = rotation_tables(sample_index, SEGLEN, fine, BINS // fine)
     cores = [(0, 1), (1, 0), (2, 3), (3, 2)]
     chips = [(0, 2), (2, 0), (1, 3), (3, 1)]
 
     def spectra_of(q_chip, q_core):
-        return quarter_spectra(local_record, sample_index, 2 * q_chip + q_core, fine_table)
+        return quarter_spectra(local_record, 2 * q_chip + q_core, tables, fine)
 
     first = lax.ppermute(spectra_of(1 - chip, 1 - core), "af", cores)
     second = lax.ppermute(spectra_of(chip, 1 - core), "af", cores)

time: 154 us -> 154 us (level)
  no operation moved by 1% of the time
where the time goes in v10:
time: 154 us; the launch traced here: 153 us
  blocking collectives  54.4 us (35%)
  waiting for transfers between devices  54.2 us (35%)
  starting transfers between devices  21 us (14%)
  local copies, waits for them, and re-layouts  12.3 us (8%)
  matrix products  6.05 us (4%)
  other arithmetic  4.94 us (3%)
    all_to_all x1, blocking collectives, per_device(): lax.all_to_all(whitened.reshape(band_rows, 1, 2, channels), 'ch', split_a...  54.4 us
    all_to_all x1, waiting for transfers between devices, per_device(): back = lax.all_to_all(rows, 'ch', split_axis=0, concat_axis=0, tiled=True)  37 us
    ppermute x1, waiting for transfers between devices, reduced_spectra(): incoming_edges = lax.ppermute(edge_rows, 'af', chips)  9.5 us
    ppermute x1, waiting for transfers between devices, reduced_spectra(): incoming_middle = lax.ppermute(outgoing[SMOOTH:rows - SMOOTH], 'af', chips)  7.7 us
    all_to_all x1, starting transfers between devices, per_device(): back = lax.all_to_all(rows, 'ch', split_axis=0, concat_axis=0, tiled=True)  6.74 us
    ppermute x1, starting transfers between devices, reduced_spectra(): incoming_edges = lax.ppermute(edge_rows, 'af', chips)  5.1 us
    dot_general x4, matrix products, quarter_spectra(): out = jnp.dot(basis, local_record, preferred_element_type=jnp.float32)  5.09 us
  transfers between devices with their start and end apart: 7, of which 3 were waited for; matrix products, arithmetic and copies ran while one was open for 3% of the time, Pallas kernels for 0%

profile of v10, /device:TPU:6, one launch (start us, length us, event | category | flops | bytes accessed | tf_op | source)
XLA Modules:
  0.0 153.4 jit_solution(4654600542431318769)
XLA Ops:
  0.0 0.1 multiply_subtract_fusion.4
  0.1 0.1 pad_add_fusion
  0.2 1.6 %fusion.62 = (f32[48,2048]{1,0:T(8,128)S(1)}, f32[48,2048]{1,0:T(8,128)S(1)}) fusion(s32[2048]{0:T(1024)S(1)} %iota_add_fusion, s32[48]{0:T(128)S(1)} %pad_add_fusion), kind=kLoop, calls=%fused_computation.96 | loop fusion | flops 1376256 | bytes 794816 | tf_op jit(solution)/shard_map/cos | solution.py:39
  1.9 0.1 constant_dynamic-slice_fusion.6
  1.9 1.2 multiply_subtract_fusion.3
  3.1 0.0 copy-start.3
  3.1 1.3 fusion.52
  4.4 0.9 copy-done.3
  5.3 1.3 fusion
  6.6 1.9 %collective-permute-start.1 = (f32[128,2,1024]{2,0,1:T(8,128)S(1)}, f32[128,2,1024]{2,0,1:T(8,128)S(1)}, u32[]{:S(2)}, u32[]{:S(2)}) collective-permute-start(f32[128,2,1024]{2,0,1:T(8,128)S(1)} %fusion), channel_id=1, source_target_pairs={{0,1},{1,0},{2,3},{3,2},{4,5},{5,4},{6,7},{7,6},{8,9},{9,8},{10,11... | collective-permute-start | bytes 3145736 | tf_op jit(solution)/shard_map/ppermute | solution.py:74
  8.5 0.0 copy-start
  8.5 1.3 fusion.4
  9.8 2.4 %collective-permute-start = (f32[128,2,1024]{2,0,1:T(8,128)S(1)}, f32[128,2,1024]{2,0,1:T(8,128)S(1)}, u32[]{:S(2)}, u32[]{:S(2)}) collective-permute-start(f32[128,2,1024]{2,0,1:T(8,128)S(1)} %fusion.4), channel_id=1, source_target_pairs={{0,1},{1,0},{2,3},{3,2},{4,5},{5,4},{6,7},{7,6},{8,9},{9,8},{10,11... | collective-permute-start | bytes 3145736 | tf_op jit(solution)/shard_map/ppermute | solution.py:75
  12.2 0.0 copy-done
  12.3 0.0 collective-permute-done.1
  12.3 1.3 fusion.11
  13.7 5.1 %collective-permute-start.2 = (f32[64,2,1024]{2,0,1:T(8,128)S(1)}, f32[64,2,1024]{2,0,1:T(8,128)S(1)}, u32[]{:S(2)}, u32[]{:S(2)}) collective-permute-start(f32[64,2,1024]{2,0,1:T(8,128)S(1)} %pad_maximum_fusion), channel_id=1, source_target_pairs={{0,2},{2,0},{1,3},{3,1},{4,6},{6,4},{5,7},{7,5},{8,10},{10,8},{9,1... | collective-permute-start | bytes 1572872 | tf_op jit(solution)/shard_map/ppermute | solution.py:79
  18.8 2.2 %collective-permute-start.3 = (f32[64,2,1024]{2,0,1:T(8,128)S(1)}, f32[64,2,1024]{2,0,1:T(8,128)S(1)}, u32[]{:S(2)}, u32[]{:S(2)}) collective-permute-start(f32[64,2,1024]{2,0,1:T(8,128)S(1)} %slice.112), channel_id=1, source_target_pairs={{0,2},{2,0},{1,3},{3,1},{4,6},{6,4},{5,7},{7,5},{8,10},{10,8},{9,1... | collective-permute-start | bytes 1572872 | tf_op jit(solution)/shard_map/ppermute | solution.py:80
  21.1 0.0 collective-permute-done
  21.1 1.3 fusion.8
  22.4 9.5 %collective-permute-done.2 = f32[64,2,1024]{2,0,1:T(8,128)S(1)} collective-permute-done((f32[64,2,1024]{2,0,1:T(8,128)S(1)}, f32[64,2,1024]{2,0,1:T(8,128)S(1)}, u32[]{:S(2)}, u32[]{:S(2)}) %collective-permute-start.2) | collective-permute-done | bytes 524320 | tf_op jit(solution)/shard_map/ppermute | solution.py:79
  31.9 0.1 maximum_add_fusion
  32.0 1.3 collective-permute-start.4
  33.3 1.3 collective-permute-start.5
  34.6 7.7 %collective-permute-done.3 = f32[64,2,1024]{2,0,1:T(8,128)S(1)} collective-permute-done((f32[64,2,1024]{2,0,1:T(8,128)S(1)}, f32[64,2,1024]{2,0,1:T(8,128)S(1)}, u32[]{:S(2)}, u32[]{:S(2)}) %collective-permute-start.3) | collective-permute-done | bytes 524320 | tf_op jit(solution)/shard_map/ppermute | solution.py:80
  42.3 0.1 slice_add_fusion
  42.4 0.0 collective-permute-done.4
  42.5 0.0 collective-permute-done.5
  42.6 0.5 fusion.16
  43.1 0.1 fusion.31
  43.2 0.5 copy.45
  43.8 54.4 %all_to_all.14 = bf16[128,1,2,1024]{3,2,1,0:T(2,128)(2,1)S(1)} all-to-all(bf16[128,1,2,1024]{3,2,1,0:T(2,128)(2,1)S(1)} %copy.45), channel_id=1, replica_groups=mesh['ch'=128,'af'=4] {'ch'}, dimensions={0} | all-to-all | bytes 1048576 | tf_op jit(solution)/shard_map/all_to_all | solution.py:144
  98.2 0.5 copy.46
  98.7 0.1 slice_bitcast_fusion.5
  98.8 0.1 fusion.53
  98.9 0.1 fusion.75
  99.0 0.3 copy.58
  99.3 0.3 copy.59
  99.6 0.1 neg.52
  99.6 0.4 convolution_convert_fusion
  100.1 0.3 reshape.749
  100.4 0.6 copy.49
  101.0 0.1 pad.9
  101.0 2.9 %reshape.750 = bf16[8,2,128,257]{3,2,0,1:T(8,128)(2,1)S(1)} reshape(bf16[8,2,32896]{2,0,1:T(8,128)(2,1)S(1)} %pad.9) | data formatting | bytes 2105344 | tf_op jit(solution)/shard_map/reshape | solution.py:133
  104.0 0.1 slice.124
  104.0 0.0 copy-start.1
  104.1 0.0 copy-start.2
  104.1 1.1 reshape.756
  105.1 1.4 copy.52
  106.5 6.7 %all-to-all-start.1 = ((bf16[128,2,1032]{2,1,0:T(2,128)(2,1)}), bf16[128,2,1032]{2,1,0:T(2,128)(2,1)S(1)}, u32[]{:S(2)}, u32[]{:S(2)}) async-start(bf16[128,2,1032]{2,1,0:T(2,128)(2,1)} %copy.52), calls=%async_computation.1 | async-start | bytes 1179648 | tf_op jit(solution)/shard_map/all_to_all | solution.py:153
  113.3 0.0 copy-done.1
  113.3 0.0 copy-done.2
  113.3 0.1 fusion.67
  113.4 37.0 %all-to-all-done.1 = bf16[128,2,1032]{2,1,0:T(2,128)(2,1)S(1)} async-done(((bf16[128,2,1032]{2,1,0:T(2,128)(2,1)}), bf16[128,2,1032]{2,1,0:T(2,128)(2,1)S(1)}, u32[]{:S(2)}, u32[]{:S(2)}) %all-to-all-start.1) | async-done | bytes 528416 | tf_op jit(solution)/shard_map/all_to_all | solution.py:153
  150.4 0.9 copy.53
  151.3 0.1 reshape.753
  151.4 0.2 multiply_bitcast_fusion
  151.6 1.8 %copy.54 = f32[8,129,2,128]{3,2,1,0:T(2,128)} copy(f32[8,129,2,128]{3,1,0,2:T(8,128)S(1)} %multiply_bitcast_fusion) | data formatting | bytes 2113536 | tf_op jit(solution)/shard_map/mul | solution.py:161
  (19 shorter events, 0.4 us)
Async XLA Ops:
  3.1 2.2 %copy-start.3 = (bf16[1,2048,1024]{2,1,0:T(8,128)(2,1)S(1)}, bf16[1,2048,1024]{2,1,0:T(8,128)(2,1)}, u32[]{:S(2)}) copy-start(bf16[1,2048,1024]{2,1,0:T(8,128)(2,1)} %param.4) | copy-start | bytes 12582916
  6.6 5.7 %collective-permute-start.1 = (f32[128,2,1024]{2,0,1:T(8,128)S(1)}, f32[128,2,1024]{2,0,1:T(8,128)S(1)}, u32[]{:S(2)}, u32[]{:S(2)}) collective-permute-start(f32[128,2,1024]{2,0,1:T(8,128)S(1)} %fusion), channel_id=1, source_target_pairs={{0,1},{1,0},{2,3},{3,2},{4,5},{5,4},{6,7},{7,6},{8,9},{9,8},{10,11... | collective-permute-start | bytes 3145736 | tf_op jit(solution)/shard_map/ppermute | solution.py:74
  8.5 3.7 %copy-start = (s32[1024]{0:T(1024)S(1)}, s32[1024]{0:T(1024)}, u32[]{:S(2)}) copy-start(s32[1024]{0:T(1024)} %param.5) | copy-start | bytes 12292
  9.8 11.2 %collective-permute-start = (f32[128,2,1024]{2,0,1:T(8,128)S(1)}, f32[128,2,1024]{2,0,1:T(8,128)S(1)}, u32[]{:S(2)}, u32[]{:S(2)}) collective-permute-start(f32[128,2,1024]{2,0,1:T(8,128)S(1)} %fusion.4), channel_id=1, source_target_pairs={{0,1},{1,0},{2,3},{3,2},{4,5},{5,4},{6,7},{7,6},{8,9},{9,8},{10,11... | collective-permute-start | bytes 3145736 | tf_op jit(solution)/shard_map/ppermute | solution.py:75
  13.7 18.2 %collective-permute-start.2 = (f32[64,2,1024]{2,0,1:T(8,128)S(1)}, f32[64,2,1024]{2,0,1:T(8,128)S(1)}, u32[]{:S(2)}, u32[]{:S(2)}) collective-permute-start(f32[64,2,1024]{2,0,1:T(8,128)S(1)} %pad_maximum_fusion), channel_id=1, source_target_pairs={{0,2},{2,0},{1,3},{3,1},{4,6},{6,4},{5,7},{7,5},{8,10},{10,8},{9,1... | collective-permute-start | bytes 1572872 | tf_op jit(solution)/shard_map/ppermute | solution.py:79
  18.8 23.5 %collective-permute-start.3 = (f32[64,2,1024]{2,0,1:T(8,128)S(1)}, f32[64,2,1024]{2,0,1:T(8,128)S(1)}, u32[]{:S(2)}, u32[]{:S(2)}) collective-permute-start(f32[64,2,1024]{2,0,1:T(8,128)S(1)} %slice.112), channel_id=1, source_target_pairs={{0,2},{2,0},{1,3},{3,1},{4,6},{6,4},{5,7},{7,5},{8,10},{10,8},{9,1... | collective-permute-start | bytes 1572872 | tf_op jit(solution)/shard_map/ppermute | solution.py:80
  32.0 10.4 %collective-permute-start.4 = (f32[32,1024]{1,0:T(8,128)S(1)}, f32[32,1024]{1,0:T(8,128)S(1)}, u32[]{:S(2)}, u32[]{:S(2)}) collective-permute-start(f32[32,1024]{1,0:T(8,128)S(1)} %get-tuple-element.40), channel_id=1, source_target_pairs={{0,1},{1,2},{2,3},{4,5},{5,6},{6,7},{8,9},{9,10},{10,11},{12,13},{... | collective-permute-start | bytes 393224 | tf_op jit(solution)/shard_map/ppermute | solution.py:104
  33.3 9.2 %collective-permute-start.5 = (f32[32,1024]{1,0:T(8,128)S(1)}, f32[32,1024]{1,0:T(8,128)S(1)}, u32[]{:S(2)}, u32[]{:S(2)}) collective-permute-start(f32[32,1024]{1,0:T(8,128)S(1)} %get-tuple-element.39), channel_id=1, source_target_pairs={{1,0},{2,1},{3,2},{5,4},{6,5},{7,6},{9,8},{10,9},{11,10},{13,12},{... | collective-permute-start | bytes 393224 | tf_op jit(solution)/shard_map/ppermute | solution.py:105
  104.0 9.3 %copy-start.1 = (s32[8]{0:T(128)S(1)}, s32[8]{0:T(128)}, u32[]{:S(2)}) copy-start(s32[8]{0:T(128)} %param.7) | copy-start | bytes 100
  104.1 9.3 %copy-start.2 = (s32[8]{0:T(128)S(1)}, s32[8]{0:T(128)}, u32[]{:S(2)}) copy-start(s32[8]{0:T(128)} %param.6) | copy-start | bytes 100
  106.5 43.8 %all-to-all-start.1 = ((bf16[128,2,1032]{2,1,0:T(2,128)(2,1)}), bf16[128,2,1032]{2,1,0:T(2,128)(2,1)S(1)}, u32[]{:S(2)}, u32[]{:S(2)}) async-start(bf16[128,2,1032]{2,1,0:T(2,128)(2,1)} %copy.52), calls=%async_computation.1 | async-start | bytes 1179648 | tf_op jit(solution)/shard_map/all_to_all | solution.py:153
